TPU v7x, 512 devices: a whole 4x4x16 slice. The times are simulated.
512 devices in a mesh: wide: 32 (over y, x, core), grp: 16 (over z).
Axes of the slice: x: 4, y: 4, z: 16, core: 2. Of those that a mesh axis runs over, the one named last changes fastest.
Arguments:
- embeds: bfloat16 [147456, 1024], P(('wide', 'grp')), may hold values from -700 to 700
- bucket: int32 [147456], P(('wide', 'grp')), may hold values from 0 to 31, as said below
- pairs: int32 [8192], P(('wide', 'grp')), may hold values from -1 to 15, as said below
Outputs:
- density: float32 [512, 384], P(('wide', 'grp'))
Inputs may be any that keep to these rules, and one draw needn't show every extreme that they name: At most 12 rows of one file shard name the same bucket; for every g some bucket is named by exactly 12 rows of every shard (s, g). `pairs`: the 16 entries of block (o, g) name distinct blocks (o, b) by b, live entries first and -1 after; for every o some block has all 16 entries live.
All inputs are finite; a program needn't handle non-finite values.
Results may differ from a plain program's by a relative error of at most 0.0034.
Values may be sent and summed in bfloat16 or wider, within the bound.
No kernel may reach another device: no remote copies, remote signals or barrier semaphores. Data moves between devices by JAX's collectives and lax.ppermute only.
A program may use at most 64 MiB of HBM per device.

v0:
```python
import jax
import jax.numpy as jnp
from jax import lax
from jax.sharding import PartitionSpec as P

BLK = 384


SHARPNESS = 10.0
EPSILON = 1e-06


def pair_sums(left_rows, right_rows, right_weight):
    cosines = lax.dot_general(
        left_rows, right_rows, (((1,), (1,)), ((), ())), preferred_element_type=jnp.float32
    )
    return jnp.sum(jnp.exp(SHARPNESS * (cosines - 1.0)) * right_weight[None, :], axis=1)


def per_device(embeds, bucket, pairs):
    wide_count = lax.axis_size("wide")
    feature_width = embeds.shape[1]
    capacity = BLK // wide_count
    floats = embeds.astype(jnp.float32)
    unit_rows = (
        floats * lax.rsqrt(jnp.sum(floats * floats, axis=1, keepdims=True) + EPSILON)
    ).astype(jnp.bfloat16)
    onehot = (bucket[:, None] == jnp.arange(wide_count, dtype=jnp.int32)[None, :]).astype(jnp.int32)
    row_ranks = jnp.sum(jnp.cumsum(onehot, axis=0) * onehot, axis=1) - 1
    counts = jnp.sum(onehot, axis=0)
    send_slots = bucket * capacity + row_ranks
    outgoing = (
        jnp.zeros((wide_count * capacity, feature_width), jnp.bfloat16)
        .at[send_slots]
        .set(unit_rows)
    )
    received, arrived = (
        lax.all_to_all(
            outgoing.reshape(wide_count, capacity, feature_width),
            "wide",
            split_axis=0,
            concat_axis=0,
            tiled=True,
        ),
        lax.all_to_all(
            counts.reshape(wide_count, 1), "wide", split_axis=0, concat_axis=0, tiled=True
        ),
    )
    arrived = arrived.reshape(wide_count)
    offsets = jnp.cumsum(arrived) - arrived
    within = jnp.arange(capacity, dtype=jnp.int32)
    places = jnp.where(within[None, :] < arrived[:, None], offsets[:, None] + within[None, :], BLK)
    own_block = (
        jnp.zeros((BLK, feature_width), jnp.bfloat16)
        .at[places.reshape(-1)]
        .set(received.reshape(wide_count * capacity, feature_width), mode="drop")
    )
    total_rows = jnp.sum(arrived)
    valid_rows = (jnp.arange(BLK, dtype=jnp.int32) < total_rows).astype(jnp.float32)
    flags_wire = valid_rows.astype(jnp.bfloat16)
    live_count = jnp.sum((pairs >= 0).astype(jnp.int32))
    first_row = jnp.int32(0)
    panel_rows = lax.all_gather(own_block, "grp", axis=0, tiled=True)
    panel_flags = lax.all_gather(flags_wire, "grp", axis=0, tiled=True)
    length = panel_rows.shape[0]
    span_rows = min(BLK, length)

    def add_pair(pair_index, running_sum):
        target = pairs[pair_index] * BLK
        shift_rows = jnp.clip(target, 0, length - span_rows)

        def add_tile(before):
            right_rows = lax.dynamic_slice_in_dim(panel_rows, shift_rows, span_rows, 0)
            right_flags = lax.dynamic_slice_in_dim(panel_flags, shift_rows, span_rows, 0).astype(
                jnp.float32
            )
            global_rows = shift_rows + jnp.arange(span_rows, dtype=jnp.int32)
            inside = (global_rows >= target) & (global_rows < target + BLK)
            return before + pair_sums(own_block, right_rows, jnp.where(inside, right_flags, 0.0))

        touches = (target < first_row + length) & (target + BLK > first_row)
        return lax.cond(touches, add_tile, lambda before: before, running_sum)

    density = lax.fori_loop(0, live_count, add_pair, jnp.zeros((BLK,), jnp.float32))
    return (density * valid_rows).reshape(1, BLK)


def solution(mesh):
    placed = (P(("wide", "grp"), None), P(("wide", "grp")), P(("wide", "grp")))
    return jax.shard_map(
        per_device, mesh=mesh, in_specs=placed, out_specs=P(("wide", "grp"), None), check_vma=False
    )
```

profile of v0, /device:TPU:6, one launch (start us, length us, event | category | flops | bytes accessed | tf_op | source)
XLA Modules:
  0.0 272.1 jit_solution(11040874624499148679)
XLA Ops:
  10.0 9.4 %all-to-all-start = ((s32[32,1,1]{2,1,0:T(1,128)}), s32[32,1,1]{2,1,0:T(1,128)S(1)}, u32[]{:S(2)}, u32[]{:S(2)}) async-start(s32[32,1,1]{2,1,0:T(1,128)} %copy.12), calls=%async_computation | async-start | bytes 32768 | tf_op jit(solution)/shard_map/all_to_all | solution.py:45
  21.4 2.1 scatter_custom_fusion
  25.0 7.1 %all-to-all-start.1 = ((bf16[32,12,1024]{2,1,0:T(8,128)(2,1)}), bf16[32,12,1024]{2,1,0:T(8,128)(2,1)S(1)}, u32[]{:S(2)}, u32[]{:S(2)}) async-start(bf16[32,12,1024]{2,1,0:T(8,128)(2,1)} %reshape.123), calls=%async_computation.1 | async-start | bytes 2097152 | tf_op jit(solution)/shard_map/all_to_all | solution.py:38
  33.8 12.9 %all-to-all-done.1 = bf16[32,12,1024]{2,1,0:T(8,128)(2,1)S(1)} async-done(((bf16[32,12,1024]{2,1,0:T(8,128)(2,1)}), bf16[32,12,1024]{2,1,0:T(8,128)(2,1)S(1)}, u32[]{:S(2)}, u32[]{:S(2)}) %all-to-all-start.1) | async-done | bytes 786464 | tf_op jit(solution)/shard_map/all_to_all | solution.py:38
  46.9 3.1 %scatter_custom_fusion.1 = bf16[384,1024]{1,0:T(8,128)(2,1)} fusion(s32[384]{0:T(512)S(1)} %fusion.19, bf16[384,1024]{1,0:T(8,128)(2,1)S(1)} %reshape.139, bf16[]{:T(256)} %constant.61.clone.1), kind=kCustom, calls=%fused_computation.20 | custom fusion | bytes 786434 | tf_op jit(solution)/shard_map/scatter | solution.py:56
  51.4 34.3 %all-gather = bf16[16,1,384]{2,1,0:T(2,128)(2,1)S(1)} all-gather(bf16[1,1,384]{2,1,0:T(2,128)(2,1)S(1)} %reshape.144), channel_id=1, replica_groups=mesh['wide'=32,'grp'=16] {'grp'}, dimensions={0}, use_global_device_ids=true | all-gather | bytes 13056 | tf_op jit(solution)/shard_map/all_gather | solution.py:64
  85.8 113.9 %all-gather.3.cloned.1.call-done = bf16[6144,1024]{1,0:T(8,128)(2,1)} async-done(((bf16[384,1024]{1,0:T(8,128)(2,1)}), bf16[6144,1024]{1,0:T(8,128)(2,1)}) %all-gather.3.cloned.1.call-update) | async-done | bytes 12582928 | tf_op jit(solution)/shard_map/all_gather | solution.py:63
  199.7 64.4 %while.13 = (s32[]{:T(128)}, f32[384]{0:T(512)S(1)}, s32[]{:T(128)}, s32[16]{0:T(128)S(1)}, bf16[6144,1024]{1,0:T(8,128)(2,1)}, /*index=5*/bf16[384,1024]{1,0:T(...) while((s32[]{:T(128)}, f32[384]{0:T(512)S(1)}, ...), condition=%wide.region_14.15_spmd, body=%wide.region_10.14_spmd.sunk | while | flops 302582016 | bytes 1584705 | solution.py:84
  201.5 2.1 conditional.2
  205.5 2.1 conditional.2
  209.5 2.1 conditional.2
  213.5 2.1 conditional.2
  217.5 2.1 conditional.2
  221.5 2.1 conditional.2
  225.5 2.1 conditional.2
  229.4 2.1 conditional.2
  233.4 2.1 conditional.2
  237.4 2.1 conditional.2
  241.4 2.1 conditional.2
  245.4 2.1 conditional.2
  249.4 2.1 conditional.2
  253.4 2.1 conditional.2
  257.4 2.1 conditional.2
  261.3 2.1 conditional.2
  (99 shorter events, 55.3 us)
Async XLA Ops:
  6.5 14.9 %copy-start = (bf16[288,1024]{1,0:T(8,128)(2,1)S(1)}, bf16[288,1024]{1,0:T(8,128)(2,1)}, u32[]{:S(2)}) copy-start(bf16[288,1024]{1,0:T(8,128)(2,1)} %param.7) | copy-start | bytes 1769476
  10.0 15.0 %all-to-all-start = ((s32[32,1,1]{2,1,0:T(1,128)}), s32[32,1,1]{2,1,0:T(1,128)S(1)}, u32[]{:S(2)}, u32[]{:S(2)}) async-start(s32[32,1,1]{2,1,0:T(1,128)} %copy.12), calls=%async_computation | async-start | bytes 32768 | tf_op jit(solution)/shard_map/all_to_all | solution.py:45
  25.0 21.7 %all-to-all-start.1 = ((bf16[32,12,1024]{2,1,0:T(8,128)(2,1)}), bf16[32,12,1024]{2,1,0:T(8,128)(2,1)S(1)}, u32[]{:S(2)}, u32[]{:S(2)}) async-start(bf16[32,12,1024]{2,1,0:T(8,128)(2,1)} %reshape.123), calls=%async_computation.1 | async-start | bytes 2097152 | tf_op jit(solution)/shard_map/all_to_all | solution.py:38
  32.1 167.5 %all-gather.3.cloned.1.call-start = ((), (), s32[]{:S(2)}) async-start(), calls=%async_computation.2 | async-start | bytes 13369344 | tf_op jit(solution)/shard_map/all_gather | solution.py:63
  46.9 3.2 %copy-start.1 = (s32[16]{0:T(128)S(1)}, s32[16]{0:T(128)}, u32[]{:S(2)}) copy-start(s32[16]{0:T(128)} %param.9) | copy-start | bytes 196
Sparse Core Ops, SparseCore 0:
  50.2 149.3 all-gather.2
where the time goes:
time: 273 us; the launch traced here: 272 us
  waiting for transfers between devices  127 us (47%)
  blocking collectives  34.3 us (13%)
  matrix products  32 us (12%)
  loops' own time  20.5 us (8%)
  starting transfers between devices  16.5 us (6%)
  local copies, waits for them, and re-layouts  16.3 us (6%)
  between operations  13.5 us (5%)
  other arithmetic  11.8 us (4%)
    all_gather x1, waiting for transfers between devices, per_device(): panel_rows = lax.all_gather(own_block, 'grp', axis=0, tiled=True)  114 us
    all_gather x1, blocking collectives, per_device(): panel_flags = lax.all_gather(flags_wire, 'grp', axis=0, tiled=True)  34.3 us
    dot_general x16, matrix products, pair_sums(): lax.dot_general(left_rows, right_rows, (((1,), (1,)), ((), ())), preferre...  32 us
    another operation x1, loops' own time, per_device(): lax.fori_loop(0, live_count, add_pair, jnp.zeros((BLK,), jnp.float32))  20.2 us
    all_to_all x1, waiting for transfers between devices, per_device(): lax.all_to_all(outgoing.reshape(wide_count, capacity, feature_width), 'wi...  12.9 us
    dynamic_slice x16, local copies, waits for them, and re-layouts, add_pair(): target = pairs[pair_index] * BLK  10.2 us
    all_to_all x1, starting transfers between devices, per_device(): lax.all_to_all(counts.reshape(wide_count, 1), 'wide', split_axis=0, conca...  9.36 us
    all_to_all x1, starting transfers between devices, per_device(): lax.all_to_all(outgoing.reshape(wide_count, capacity, feature_width), 'wi...  7.1 us
  transfers between devices with their start and end apart: 3, of which 3 were waited for; matrix products, arithmetic and copies ran while one was open for 3% of the time, Pallas kernels for 0%

commit v1 on v0

v1 whole, which is shorter than its diff:
```python
import jax
import jax.numpy as jnp
from jax import lax
from jax.sharding import PartitionSpec as P

BLK = 384


SHARPNESS = 10.0
EPSILON = 1e-06
SENTINEL = 2.0


def pair_products(left_rows, right_rows):
    cosines = lax.dot_general(
        left_rows, right_rows, (((1,), (1,)), ((), ())), preferred_element_type=jnp.float32
    )
    return jnp.exp(SHARPNESS * (cosines - 1.0))


def per_device(embeds, bucket, pairs):
    wide_count = lax.axis_size("wide")
    grp_count = lax.axis_size("grp")
    feature_width = embeds.shape[1]
    capacity = BLK // wide_count
    me = lax.axis_index("grp")

    all_pairs = lax.all_gather(pairs, "grp", axis=0, tiled=False)
    blocks_iota = jnp.arange(grp_count, dtype=jnp.int32)
    member = jnp.any(all_pairs[:, :, None] == blocks_iota[None, None, :], axis=1).astype(jnp.float32)

    floats = embeds.astype(jnp.float32)
    unit_rows = (
        floats * lax.rsqrt(jnp.sum(floats * floats, axis=1, keepdims=True) + EPSILON)
    ).astype(jnp.bfloat16)
    onehot = (bucket[:, None] == jnp.arange(wide_count, dtype=jnp.int32)[None, :]).astype(jnp.int32)
    row_ranks = jnp.sum(jnp.cumsum(onehot, axis=0) * onehot, axis=1) - 1
    send_slots = bucket * capacity + row_ranks
    empty = jnp.zeros((wide_count * capacity, feature_width), jnp.bfloat16).at[:, 0].set(SENTINEL)
    outgoing = empty.at[send_slots].set(unit_rows)
    own = lax.all_to_all(
        outgoing.reshape(wide_count, capacity, feature_width),
        "wide",
        split_axis=0,
        concat_axis=0,
        tiled=True,
    ).reshape(BLK, feature_width)

    def valid_of(rows):
        return (rows[:, 0].astype(jnp.float32) < 1.5).astype(jnp.float32)

    from_left = [(i, (i + 1) % grp_count) for i in range(grp_count)]
    from_right = [(i, (i - 1) % grp_count) for i in range(grp_count)]
    left = {0: own}
    right = {0: own}
    for step in range(1, 5):
        left[step] = lax.ppermute(left[step - 1], "grp", from_left)
        right[step] = lax.ppermute(right[step - 1], "grp", from_right)
    rows_at = {0: own}
    for step in range(1, 5):
        rows_at[-step] = left[step]
        rows_at[step] = right[step]
    valid_at = {k: valid_of(v) for k, v in rows_at.items()}

    def block_at(k):
        return (me + k) % grp_count

    targets = []
    vectors = []
    e = pair_products(own, own)
    targets.append(block_at(0))
    vectors.append(jnp.sum(e * valid_at[0][None, :], axis=1) * member[me, me])
    half = grp_count // 2
    plan = [(0, 1), (0, 2), (0, 3), (0, 4), (-2, 3), (-3, 3), (-3, 4), (-4, 4)]
    for p, q in plan:
        a = block_at(p)
        b = block_at(q)
        e = pair_products(rows_at[p], rows_at[q])
        scale = jnp.float32(1.0)
        if q - p == half:
            scale = (me < half).astype(jnp.float32)
        to_a = jnp.sum(e * valid_at[q][None, :], axis=1) * (member[a, b] * scale)
        to_b = jnp.sum(e * valid_at[p][:, None], axis=0) * (member[b, a] * scale)
        targets += [a, b]
        vectors += [to_a, to_b]
    contrib = (
        jnp.zeros((grp_count, BLK), jnp.float32)
        .at[jnp.stack(targets)]
        .add(jnp.stack(vectors))
    )
    slot_sums = lax.psum_scatter(contrib, "grp", scatter_dimension=0, tiled=True).reshape(BLK)

    own_valid = valid_at[0].reshape(wide_count, capacity)
    arrived = jnp.sum(own_valid, axis=1).astype(jnp.int32)
    offsets = jnp.cumsum(arrived) - arrived
    within = jnp.arange(capacity, dtype=jnp.int32)
    places = jnp.where(own_valid > 0, offsets[:, None] + within[None, :], BLK).reshape(-1)
    density = jnp.zeros((BLK,), jnp.float32).at[places].set(slot_sums, mode="drop")
    return density.reshape(1, BLK)


def solution(mesh):
    placed = (P(("wide", "grp"), None), P(("wide", "grp")), P(("wide", "grp")))
    return jax.shard_map(
        per_device, mesh=mesh, in_specs=placed, out_specs=P(("wide", "grp"), None), check_vma=False
    )
```

time: 273 us -> 196 us (0.72)
  the two profiles are of different devices: /device:TPU:6 before, /device:TPU:32 now
where the time goes in v1:
time: 196 us; the launch traced here: 195 us
  blocking collectives  83 us (42%)
  waiting for transfers between devices  45 us (23%)
  starting transfers between devices  31 us (16%)
  other arithmetic  19 us (10%)
  local copies, waits for them, and re-layouts  8.12 us (4%)
  matrix products  6.12 us (3%)
  between operations  3.19 us (2%)
    unnamed x2, blocking collectives  83 us
    ppermute x4, waiting for transfers between devices, per_device(): right[step] = lax.ppermute(right[step - 1], 'grp', from_right)  39.7 us
    ppermute x4, starting transfers between devices, per_device(): right[step] = lax.ppermute(right[step - 1], 'grp', from_right)  12.5 us
    ppermute x4, starting transfers between devices, per_device(): left[step] = lax.ppermute(left[step - 1], 'grp', from_left)  11 us
    mul x11, other arithmetic, per_device(): to_b = jnp.sum(e * valid_at[p][:, None], axis=0) * (member[b, a] * scale)  9.11 us
    all_to_all x1, starting transfers between devices, per_device(): lax.all_to_all(outgoing.reshape(wide_count, capacity, feature_width), 'wi...  7.45 us
    dot_general x9, matrix products, pair_products(): lax.dot_general(left_rows, right_rows, (((1,), (1,)), ((), ())), preferre...  6.12 us
    ppermute x4, waiting for transfers between devices, per_device(): left[step] = lax.ppermute(left[step - 1], 'grp', from_left)  5.36 us
  transfers between devices with their start and end apart: 9, of which 6 were waited for; matrix products, arithmetic and copies ran while one was open for 5% of the time, Pallas kernels for 0%

profile of v1, /device:TPU:32, one launch (start us, length us, event | category | flops | bytes accessed | tf_op | source)
XLA Modules:
  0.0 195.4 jit_solution(14997682475637029147)
XLA Ops:
  1.3 1.3 fusion.20
  6.0 2.3 %scatter_custom_fusion = bf16[384,1024]{1,0:T(8,128)(2,1)S(1)} fusion(bf16[384,1024]{1,0:T(8,128)(2,1)S(1)} %scatter.22, s32[288]{0:T(512)S(1)} %compare_select_fusion.1, bf16[288,1024]{1,0:T(8,128)(2,1)S(1)} %copy-done, f32[288]{0:T(512)S(1)} %add_rsqrt_fusion), kind=kCustom, calls=%fused_computation.36 | custom fusion | flops 884736 | bytes 1378304 | tf_op jit(solution)/shard_map/scatter | solution.py:40
  9.5 7.5 %all-to-all-start = ((bf16[32,12,1024]{2,1,0:T(8,128)(2,1)}), bf16[32,12,1024]{2,1,0:T(8,128)(2,1)S(1)}, u32[]{:S(2)}, u32[]{:S(2)}) async-start(bf16[32,12,1024]{2,1,0:T(8,128)(2,1)} %reshape.985), calls=%async_computation | async-start | bytes 2097152 | tf_op jit(solution)/shard_map/all_to_all | solution.py:41
  18.7 25.8 %all-reduce.2 = s32[256]{0:T(256)S(1)} all-reduce(s32[256]{0:T(256)S(1)} %dynamic-update-slice.3), channel_id=2, replica_groups=mesh['wide'=32,'grp'=16] {'grp'}, use_global_device_ids=true, to_apply=%add.2 | all-reduce | flops 256 | bytes 2048
  45.7 2.9 %collective-permute-start = (bf16[384,1024]{1,0:T(8,128)(2,1)S(1)}, bf16[384,1024]{1,0:T(8,128)(2,1)S(1)}, u32[]{:S(2)}, u32[]{:S(2)}) collective-permute-start(bf16[384,1024]{1,0:T(8,128)(2,1)S(1)} %reshape.986), channel_id=1, source_target_pairs={{0,15},{1,0},{2,1},{3,2},{4,3},{5,4},{6,5},{7,6},{8,7},{9,8},{10,9... | collective-permute-start | bytes 2359304 | tf_op jit(solution)/shard_map/ppermute | solution.py:58
  48.7 2.9 %collective-permute-start.4 = (bf16[384,1024]{1,0:T(8,128)(2,1)S(1)}, bf16[384,1024]{1,0:T(8,128)(2,1)}, u32[]{:S(2)}, u32[]{:S(2)}) collective-permute-start(bf16[384,1024]{1,0:T(8,128)(2,1)S(1)} %reshape.986), channel_id=1, source_target_pairs={{0,1},{1,2},{2,3},{3,4},{4,5},{5,6},{6,7},{7,8},{8,9},{9,10},{10,1... | collective-permute-start | bytes 2359304 | tf_op jit(solution)/shard_map/ppermute | solution.py:57
  54.5 9.9 %collective-permute-done = bf16[384,1024]{1,0:T(8,128)(2,1)S(1)} collective-permute-done((bf16[384,1024]{1,0:T(8,128)(2,1)S(1)}, bf16[384,1024]{1,0:T(8,128)(2,1)S(1)}, u32[]{:S(2)}, u32[]{:S(2)}) %collective-permute-start) | collective-permute-done | bytes 786464 | tf_op jit(solution)/shard_map/ppermute | solution.py:58
  64.4 2.9 %collective-permute-start.1 = (bf16[384,1024]{1,0:T(8,128)(2,1)S(1)}, bf16[384,1024]{1,0:T(8,128)(2,1)S(1)}, u32[]{:S(2)}, u32[]{:S(2)}) collective-permute-start(bf16[384,1024]{1,0:T(8,128)(2,1)S(1)} %collective-permute-done), channel_id=1, source_target_pairs={{0,15},{1,0},{2,1},{3,2},{4,3},{5,4},{6,5},{7,6},{8,7},{9,8},{10,9... | collective-permute-start | bytes 2359304 | tf_op jit(solution)/shard_map/ppermute | solution.py:58
  67.6 2.9 %collective-permute-start.5 = (bf16[384,1024]{1,0:T(8,128)(2,1)}, bf16[384,1024]{1,0:T(8,128)(2,1)S(1)}, u32[]{:S(2)}, u32[]{:S(2)}) collective-permute-start(bf16[384,1024]{1,0:T(8,128)(2,1)} %collective-permute-done.4), channel_id=1, source_target_pairs={{0,1},{1,2},{2,3},{3,4},{4,5},{5,6},{6,7},{7,8},{8,9},{9,10},{10,1... | collective-permute-start | bytes 2359304 | tf_op jit(solution)/shard_map/ppermute | solution.py:57
  71.0 11.4 %collective-permute-done.1 = bf16[384,1024]{1,0:T(8,128)(2,1)S(1)} collective-permute-done((bf16[384,1024]{1,0:T(8,128)(2,1)S(1)}, bf16[384,1024]{1,0:T(8,128)(2,1)S(1)}, u32[]{:S(2)}, u32[]{:S(2)}) %collective-permute-start.1) | collective-permute-done | bytes 786464 | tf_op jit(solution)/shard_map/ppermute | solution.py:58
  82.4 2.9 %collective-permute-start.2 = (bf16[384,1024]{1,0:T(8,128)(2,1)S(1)}, bf16[384,1024]{1,0:T(8,128)(2,1)S(1)}, u32[]{:S(2)}, u32[]{:S(2)}) collective-permute-start(bf16[384,1024]{1,0:T(8,128)(2,1)S(1)} %collective-permute-done.1), channel_id=1, source_target_pairs={{0,15},{1,0},{2,1},{3,2},{4,3},{5,4},{6,5},{7,6},{8,7},{9,8},{10,9... | collective-permute-start | bytes 2359304 | tf_op jit(solution)/shard_map/ppermute | solution.py:58
  85.9 2.9 %collective-permute-start.6 = (bf16[384,1024]{1,0:T(8,128)(2,1)S(1)}, bf16[384,1024]{1,0:T(8,128)(2,1)S(1)}, u32[]{:S(2)}, u32[]{:S(2)}) collective-permute-start(bf16[384,1024]{1,0:T(8,128)(2,1)S(1)} %collective-permute-done.5), channel_id=1, source_target_pairs={{0,1},{1,2},{2,3},{3,4},{4,5},{5,6},{6,7},{7,8},{8,9},{9,10},{10,1... | collective-permute-start | bytes 2359304 | tf_op jit(solution)/shard_map/ppermute | solution.py:57
  89.7 9.8 %collective-permute-done.2 = bf16[384,1024]{1,0:T(8,128)(2,1)S(1)} collective-permute-done((bf16[384,1024]{1,0:T(8,128)(2,1)S(1)}, bf16[384,1024]{1,0:T(8,128)(2,1)S(1)}, u32[]{:S(2)}, u32[]{:S(2)}) %collective-permute-start.2) | collective-permute-done | bytes 786464 | tf_op jit(solution)/shard_map/ppermute | solution.py:58
  99.5 3.8 %collective-permute-start.3 = (bf16[384,1024]{1,0:T(8,128)(2,1)S(1)}, bf16[384,1024]{1,0:T(8,128)(2,1)S(1)}, u32[]{:S(2)}, u32[]{:S(2)}) collective-permute-start(bf16[384,1024]{1,0:T(8,128)(2,1)S(1)} %collective-permute-done.2), channel_id=1, source_target_pairs={{0,15},{1,0},{2,1},{3,2},{4,3},{5,4},{6,5},{7,6},{8,7},{9,8},{10,9... | collective-permute-start | bytes 2359304 | tf_op jit(solution)/shard_map/ppermute | solution.py:58
  104.5 2.2 %collective-permute-start.7 = (bf16[384,1024]{1,0:T(8,128)(2,1)S(1)}, bf16[384,1024]{1,0:T(8,128)(2,1)S(1)}, u32[]{:S(2)}, u32[]{:S(2)}) collective-permute-start(bf16[384,1024]{1,0:T(8,128)(2,1)S(1)} %collective-permute-done.6), channel_id=1, source_target_pairs={{0,1},{1,2},{2,3},{3,4},{4,5},{5,6},{6,7},{7,8},{8,9},{9,10},{10,1... | collective-permute-start | bytes 2359304 | tf_op jit(solution)/shard_map/ppermute | solution.py:57
  108.1 8.6 %collective-permute-done.3 = bf16[384,1024]{1,0:T(8,128)(2,1)S(1)} collective-permute-done((bf16[384,1024]{1,0:T(8,128)(2,1)S(1)}, bf16[384,1024]{1,0:T(8,128)(2,1)S(1)}, u32[]{:S(2)}, u32[]{:S(2)}) %collective-permute-start.3) | collective-permute-done | bytes 786464 | tf_op jit(solution)/shard_map/ppermute | solution.py:58
  118.0 4.9 %collective-permute-done.7 = bf16[384,1024]{1,0:T(8,128)(2,1)S(1)} collective-permute-done((bf16[384,1024]{1,0:T(8,128)(2,1)S(1)}, bf16[384,1024]{1,0:T(8,128)(2,1)S(1)}, u32[]{:S(2)}, u32[]{:S(2)}) %collective-permute-start.7) | collective-permute-done | bytes 786464 | tf_op jit(solution)/shard_map/ppermute | solution.py:57
  124.3 1.3 broadcast_multiply_fusion.8
  125.6 1.3 broadcast_multiply_fusion.12
  126.8 1.3 broadcast_multiply_fusion.10
  128.1 1.3 broadcast_multiply_fusion.14
  132.0 1.3 broadcast_multiply_fusion.6
  134.0 57.1 %all-reduce.3 = f32[16,384]{1,0:T(8,128)S(1)} all-reduce(f32[16,384]{1,0:T(8,128)S(1)} %scatter_custom_fusion.1), channel_id=3, replica_groups=mesh['wide'=32,'grp'=16] {'grp'}, use_global_device_ids=true, to_apply=%region_27.28.clone | all-reduce | flops 6144 | bytes 49152
  191.9 2.9 %scatter_custom_fusion.2 = f32[384]{0:T(512)S(1)} fusion(s32[384]{0:T(512)S(1)} %fusion.25, f32[384]{0:T(512)S(1)} %dynamic-slice_reduce_fusion, f32[]{:T(128)} %constant.134.clone.1), kind=kCustom, calls=%fused_computation.109 | custom fusion | bytes 1540 | tf_op jit(solution)/shard_map/scatter | solution.py:98
  (85 shorter events, 20.9 us)
Async XLA Ops:
  0.0 6.0 %copy-start = (bf16[288,1024]{1,0:T(8,128)(2,1)S(1)}, bf16[288,1024]{1,0:T(8,128)(2,1)}, u32[]{:S(2)}) copy-start(bf16[288,1024]{1,0:T(8,128)(2,1)} %param.5) | copy-start | bytes 1769476
  9.5 7.6 %copy-start.1 = (u32[512]{0:T(512)S(1)}, u32[512]{0:T(512)}, u32[]{:S(2)}) copy-start(u32[512]{0:T(512)} %constant.168) | copy-start | bytes 6148
  9.5 8.9 %copy-start.2 = (s32[16]{0:T(128)S(1)}, s32[16]{0:T(128)}, u32[]{:S(2)}) copy-start(s32[16]{0:T(128)} %param.7) | copy-start | bytes 196
  9.5 36.0 %all-to-all-start = ((bf16[32,12,1024]{2,1,0:T(8,128)(2,1)}), bf16[32,12,1024]{2,1,0:T(8,128)(2,1)S(1)}, u32[]{:S(2)}, u32[]{:S(2)}) async-start(bf16[32,12,1024]{2,1,0:T(8,128)(2,1)} %reshape.985), calls=%async_computation | async-start | bytes 2097152 | tf_op jit(solution)/shard_map/all_to_all | solution.py:41
  45.7 18.7 %collective-permute-start = (bf16[384,1024]{1,0:T(8,128)(2,1)S(1)}, bf16[384,1024]{1,0:T(8,128)(2,1)S(1)}, u32[]{:S(2)}, u32[]{:S(2)}) collective-permute-start(bf16[384,1024]{1,0:T(8,128)(2,1)S(1)} %reshape.986), channel_id=1, source_target_pairs={{0,15},{1,0},{2,1},{3,2},{4,3},{5,4},{6,5},{7,6},{8,7},{9,8},{10,9... | collective-permute-start | bytes 2359304 | tf_op jit(solution)/shard_map/ppermute | solution.py:58
  48.7 18.9 %collective-permute-start.4 = (bf16[384,1024]{1,0:T(8,128)(2,1)S(1)}, bf16[384,1024]{1,0:T(8,128)(2,1)}, u32[]{:S(2)}, u32[]{:S(2)}) collective-permute-start(bf16[384,1024]{1,0:T(8,128)(2,1)S(1)} %reshape.986), channel_id=1, source_target_pairs={{0,1},{1,2},{2,3},{3,4},{4,5},{5,6},{6,7},{7,8},{8,9},{9,10},{10,1... | collective-permute-start | bytes 2359304 | tf_op jit(solution)/shard_map/ppermute | solution.py:57
  64.4 18.0 %collective-permute-start.1 = (bf16[384,1024]{1,0:T(8,128)(2,1)S(1)}, bf16[384,1024]{1,0:T(8,128)(2,1)S(1)}, u32[]{:S(2)}, u32[]{:S(2)}) collective-permute-start(bf16[384,1024]{1,0:T(8,128)(2,1)S(1)} %collective-permute-done), channel_id=1, source_target_pairs={{0,15},{1,0},{2,1},{3,2},{4,3},{5,4},{6,5},{7,6},{8,7},{9,8},{10,9... | collective-permute-start | bytes 2359304 | tf_op jit(solution)/shard_map/ppermute | solution.py:58
  67.6 18.3 %collective-permute-start.5 = (bf16[384,1024]{1,0:T(8,128)(2,1)}, bf16[384,1024]{1,0:T(8,128)(2,1)S(1)}, u32[]{:S(2)}, u32[]{:S(2)}) collective-permute-start(bf16[384,1024]{1,0:T(8,128)(2,1)} %collective-permute-done.4), channel_id=1, source_target_pairs={{0,1},{1,2},{2,3},{3,4},{4,5},{5,6},{6,7},{7,8},{8,9},{9,10},{10,1... | collective-permute-start | bytes 2359304 | tf_op jit(solution)/shard_map/ppermute | solution.py:57
  82.4 17.1 %collective-permute-start.2 = (bf16[384,1024]{1,0:T(8,128)(2,1)S(1)}, bf16[384,1024]{1,0:T(8,128)(2,1)S(1)}, u32[]{:S(2)}, u32[]{:S(2)}) collective-permute-start(bf16[384,1024]{1,0:T(8,128)(2,1)S(1)} %collective-permute-done.1), channel_id=1, source_target_pairs={{0,15},{1,0},{2,1},{3,2},{4,3},{5,4},{6,5},{7,6},{8,7},{9,8},{10,9... | collective-permute-start | bytes 2359304 | tf_op jit(solution)/shard_map/ppermute | solution.py:58
  85.9 18.5 %collective-permute-start.6 = (bf16[384,1024]{1,0:T(8,128)(2,1)S(1)}, bf16[384,1024]{1,0:T(8,128)(2,1)S(1)}, u32[]{:S(2)}, u32[]{:S(2)}) collective-permute-start(bf16[384,1024]{1,0:T(8,128)(2,1)S(1)} %collective-permute-done.5), channel_id=1, source_target_pairs={{0,1},{1,2},{2,3},{3,4},{4,5},{5,6},{6,7},{7,8},{8,9},{9,10},{10,1... | collective-permute-start | bytes 2359304 | tf_op jit(solution)/shard_map/ppermute | solution.py:57
  99.5 17.2 %collective-permute-start.3 = (bf16[384,1024]{1,0:T(8,128)(2,1)S(1)}, bf16[384,1024]{1,0:T(8,128)(2,1)S(1)}, u32[]{:S(2)}, u32[]{:S(2)}) collective-permute-start(bf16[384,1024]{1,0:T(8,128)(2,1)S(1)} %collective-permute-done.2), channel_id=1, source_target_pairs={{0,15},{1,0},{2,1},{3,2},{4,3},{5,4},{6,5},{7,6},{8,7},{9,8},{10,9... | collective-permute-start | bytes 2359304 | tf_op jit(solution)/shard_map/ppermute | solution.py:58
  104.5 18.5 %collective-permute-start.7 = (bf16[384,1024]{1,0:T(8,128)(2,1)S(1)}, bf16[384,1024]{1,0:T(8,128)(2,1)S(1)}, u32[]{:S(2)}, u32[]{:S(2)}) collective-permute-start(bf16[384,1024]{1,0:T(8,128)(2,1)S(1)} %collective-permute-done.6), channel_id=1, source_target_pairs={{0,1},{1,2},{2,3},{3,4},{4,5},{5,6},{6,7},{7,8},{8,9},{9,10},{10,1... | collective-permute-start | bytes 2359304 | tf_op jit(solution)/shard_map/ppermute | solution.py:57

commit v2 on v1

--- a/solution.py
+++ b/solution.py
@@ -25,9 +25,8 @@
     capacity = BLK // wide_count
     me = lax.axis_index("grp")
 
-    all_pairs = lax.all_gather(pairs, "grp", axis=0, tiled=False)
     blocks_iota = jnp.arange(grp_count, dtype=jnp.int32)
-    member = jnp.any(all_pairs[:, :, None] == blocks_iota[None, None, :], axis=1).astype(jnp.float32)
+    member = jnp.any(pairs[:, None] == blocks_iota[None, :], axis=0).astype(jnp.float32)
 
     floats = embeds.astype(jnp.float32)
     unit_rows = (
@@ -49,46 +48,50 @@
     def valid_of(rows):
         return (rows[:, 0].astype(jnp.float32) < 1.5).astype(jnp.float32)
 
-    from_left = [(i, (i + 1) % grp_count) for i in range(grp_count)]
-    from_right = [(i, (i - 1) % grp_count) for i in range(grp_count)]
+    def shift(value, offset):
+        return lax.ppermute(
+            value, "grp", [(i, (i + offset) % grp_count) for i in range(grp_count)]
+        )
+
+    reach = 4
     left = {0: own}
     right = {0: own}
-    for step in range(1, 5):
-        left[step] = lax.ppermute(left[step - 1], "grp", from_left)
-        right[step] = lax.ppermute(right[step - 1], "grp", from_right)
+    for step in range(1, reach + 1):
+        left[step] = shift(left[step - 1], 1)
+        right[step] = shift(right[step - 1], -1)
     rows_at = {0: own}
-    for step in range(1, 5):
+    for step in range(1, reach + 1):
         rows_at[-step] = left[step]
         rows_at[step] = right[step]
     valid_at = {k: valid_of(v) for k, v in rows_at.items()}
 
-    def block_at(k):
-        return (me + k) % grp_count
+    outgoing_sums = {}
 
-    targets = []
-    vectors = []
+    def add(target, source, sums):
+        outgoing_sums.setdefault(target, []).append((source, sums))
+
     e = pair_products(own, own)
-    targets.append(block_at(0))
-    vectors.append(jnp.sum(e * valid_at[0][None, :], axis=1) * member[me, me])
+    add(0, 0, jnp.sum(e * valid_at[0][None, :], axis=1))
     half = grp_count // 2
     plan = [(0, 1), (0, 2), (0, 3), (0, 4), (-2, 3), (-3, 3), (-3, 4), (-4, 4)]
     for p, q in plan:
-        a = block_at(p)
-        b = block_at(q)
         e = pair_products(rows_at[p], rows_at[q])
-        scale = jnp.float32(1.0)
+        to_p = jnp.sum(e * valid_at[q][None, :], axis=1)
+        to_q = jnp.sum(e * valid_at[p][:, None], axis=0)
         if q - p == half:
-            scale = (me < half).astype(jnp.float32)
-        to_a = jnp.sum(e * valid_at[q][None, :], axis=1) * (member[a, b] * scale)
-        to_b = jnp.sum(e * valid_at[p][:, None], axis=0) * (member[b, a] * scale)
-        targets += [a, b]
-        vectors += [to_a, to_b]
-    contrib = (
-        jnp.zeros((grp_count, BLK), jnp.float32)
-        .at[jnp.stack(targets)]
-        .add(jnp.stack(vectors))
-    )
-    slot_sums = lax.psum_scatter(contrib, "grp", scatter_dimension=0, tiled=True).reshape(BLK)
+            keep = (me < half).astype(jnp.float32)
+            to_p = to_p * keep
+            to_q = to_q * keep
+        add(p, q, to_p)
+        add(q, p, to_q)
+
+    slot_sums = jnp.zeros((BLK,), jnp.float32)
+    for target, items in sorted(outgoing_sums.items()):
+        stacked = jnp.stack([sums for _, sums in items])
+        if target != 0:
+            stacked = shift(stacked, target)
+        sources = (me + jnp.array([s - target for s, _ in items], jnp.int32)) % grp_count
+        slot_sums = slot_sums + jnp.sum(stacked * member[sources][:, None], axis=0)
 
     own_valid = valid_at[0].reshape(wide_count, capacity)
     arrived = jnp.sum(own_valid, axis=1).astype(jnp.int32)

time: 196 us -> 172 us (0.88)
  the two profiles are of different devices: /device:TPU:32 before, /device:TPU:6 now
where the time goes in v2:
time: 172 us; the launch traced here: 171 us
  waiting for transfers between devices  73.2 us (43%)
  starting transfers between devices  69.5 us (40%)
  other arithmetic  11.8 us (7%)
  local copies, waits for them, and re-layouts  8.76 us (5%)
  matrix products  6.25 us (4%)
    ppermute x15, waiting for transfers between devices, shift(): lax.ppermute(value, 'grp', [(i, (i + offset) % grp_count) for i in range(...  60 us
    ppermute x15, starting transfers between devices, shift(): lax.ppermute(value, 'grp', [(i, (i + offset) % grp_count) for i in range(...  59.9 us
    all_to_all x1, waiting for transfers between devices, per_device(): lax.all_to_all(outgoing.reshape(wide_count, capacity, feature_width), 'wi...  13.1 us
    all_to_all x1, starting transfers between devices, per_device(): lax.all_to_all(outgoing.reshape(wide_count, capacity, feature_width), 'wi...  9.57 us
    dot_general x9, matrix products, pair_products(): lax.dot_general(left_rows, right_rows, (((1,), (1,)), ((), ())), preferre...  6.25 us
  transfers between devices with their start and end apart: 16, of which 8 were waited for; matrix products, arithmetic and copies ran while one was open for 7% of the time, Pallas kernels for 0%

profile of v2, /device:TPU:6, one launch (start us, length us, event | category | flops | bytes accessed | tf_op | source)
XLA Modules:
  0.0 170.8 jit_solution(7080359943222596794)
XLA Ops:
  6.0 2.3 %scatter_custom_fusion = bf16[384,1024]{1,0:T(8,128)(2,1)S(1)} fusion(bf16[384,1024]{1,0:T(8,128)(2,1)S(1)} %scatter.22, s32[288]{0:T(512)S(1)} %compare_select_fusion.1, bf16[288,1024]{1,0:T(8,128)(2,1)S(1)} %copy-done, f32[288]{0:T(512)S(1)} %add_rsqrt_fusion), kind=kCustom, calls=%fused_computation.39 | custom fusion | flops 884736 | bytes 1378304 | tf_op jit(solution)/shard_map/scatter | solution.py:39
  9.5 9.6 %all-to-all-start = ((bf16[32,12,1024]{2,1,0:T(8,128)(2,1)}), bf16[32,12,1024]{2,1,0:T(8,128)(2,1)S(1)}, u32[]{:S(2)}, u32[]{:S(2)}) async-start(bf16[32,12,1024]{2,1,0:T(8,128)(2,1)} %reshape.220), calls=%async_computation | async-start | bytes 2097152 | tf_op jit(solution)/shard_map/all_to_all | solution.py:40
  20.6 13.1 %all-to-all-done = bf16[32,12,1024]{2,1,0:T(8,128)(2,1)S(1)} async-done(((bf16[32,12,1024]{2,1,0:T(8,128)(2,1)}), bf16[32,12,1024]{2,1,0:T(8,128)(2,1)S(1)}, u32[]{:S(2)}, u32[]{:S(2)}) %all-to-all-start) | async-done | bytes 786464 | tf_op jit(solution)/shard_map/all_to_all | solution.py:40
  33.9 9.4 %collective-permute-start.4 = (bf16[384,1024]{1,0:T(8,128)(2,1)S(1)}, bf16[384,1024]{1,0:T(8,128)(2,1)S(1)}, u32[]{:S(2)}, u32[]{:S(2)}) collective-permute-start(bf16[384,1024]{1,0:T(8,128)(2,1)S(1)} %reshape.221), channel_id=1, source_target_pairs={{0,15},{1,0},{2,1},{3,2},{4,3},{5,4},{6,5},{7,6},{8,7},{9,8},{10,9... | collective-permute-start | bytes 2359304 | tf_op jit(solution)/shard_map/ppermute | solution.py:52
  43.4 1.9 %collective-permute-start = (bf16[384,1024]{1,0:T(8,128)(2,1)S(1)}, bf16[384,1024]{1,0:T(8,128)(2,1)}, u32[]{:S(2)}, u32[]{:S(2)}) collective-permute-start(bf16[384,1024]{1,0:T(8,128)(2,1)S(1)} %reshape.221), channel_id=1, source_target_pairs={{0,1},{1,2},{2,3},{3,4},{4,5},{5,6},{6,7},{7,8},{8,9},{9,10},{10,1... | collective-permute-start | bytes 2359304 | tf_op jit(solution)/shard_map/ppermute | solution.py:52
  47.9 13.0 %collective-permute-done.4 = bf16[384,1024]{1,0:T(8,128)(2,1)S(1)} collective-permute-done((bf16[384,1024]{1,0:T(8,128)(2,1)S(1)}, bf16[384,1024]{1,0:T(8,128)(2,1)S(1)}, u32[]{:S(2)}, u32[]{:S(2)}) %collective-permute-start.4) | collective-permute-done | bytes 786464 | tf_op jit(solution)/shard_map/ppermute | solution.py:52
  60.9 5.6 %collective-permute-start.5 = (bf16[384,1024]{1,0:T(8,128)(2,1)S(1)}, bf16[384,1024]{1,0:T(8,128)(2,1)S(1)}, u32[]{:S(2)}, u32[]{:S(2)}) collective-permute-start(bf16[384,1024]{1,0:T(8,128)(2,1)S(1)} %collective-permute-done.4), channel_id=1, source_target_pairs={{0,15},{1,0},{2,1},{3,2},{4,3},{5,4},{6,5},{7,6},{8,7},{9,8},{10,9... | collective-permute-start | bytes 2359304 | tf_op jit(solution)/shard_map/ppermute | solution.py:52
  70.0 13.7 %collective-permute-done.5 = bf16[384,1024]{1,0:T(8,128)(2,1)S(1)} collective-permute-done((bf16[384,1024]{1,0:T(8,128)(2,1)S(1)}, bf16[384,1024]{1,0:T(8,128)(2,1)S(1)}, u32[]{:S(2)}, u32[]{:S(2)}) %collective-permute-start.5) | collective-permute-done | bytes 786464 | tf_op jit(solution)/shard_map/ppermute | solution.py:52
  83.7 5.6 %collective-permute-start.6 = (bf16[384,1024]{1,0:T(8,128)(2,1)S(1)}, bf16[384,1024]{1,0:T(8,128)(2,1)S(1)}, u32[]{:S(2)}, u32[]{:S(2)}) collective-permute-start(bf16[384,1024]{1,0:T(8,128)(2,1)S(1)} %collective-permute-done.5), channel_id=1, source_target_pairs={{0,15},{1,0},{2,1},{3,2},{4,3},{5,4},{6,5},{7,6},{8,7},{9,8},{10,9... | collective-permute-start | bytes 2359304 | tf_op jit(solution)/shard_map/ppermute | solution.py:52
  89.9 1.9 %collective-permute-start.2 = (bf16[384,1024]{1,0:T(8,128)(2,1)S(1)}, bf16[384,1024]{1,0:T(8,128)(2,1)S(1)}, u32[]{:S(2)}, u32[]{:S(2)}) collective-permute-start(bf16[384,1024]{1,0:T(8,128)(2,1)S(1)} %collective-permute-done.1), channel_id=1, source_target_pairs={{0,1},{1,2},{2,3},{3,4},{4,5},{5,6},{6,7},{7,8},{8,9},{9,10},{10,1... | collective-permute-start | bytes 2359304 | tf_op jit(solution)/shard_map/ppermute | solution.py:52
  92.7 12.9 %collective-permute-done.6 = bf16[384,1024]{1,0:T(8,128)(2,1)S(1)} collective-permute-done((bf16[384,1024]{1,0:T(8,128)(2,1)S(1)}, bf16[384,1024]{1,0:T(8,128)(2,1)S(1)}, u32[]{:S(2)}, u32[]{:S(2)}) %collective-permute-start.6) | collective-permute-done | bytes 786464 | tf_op jit(solution)/shard_map/ppermute | solution.py:52
  105.6 5.6 %collective-permute-start.7 = (bf16[384,1024]{1,0:T(8,128)(2,1)S(1)}, bf16[384,1024]{1,0:T(8,128)(2,1)S(1)}, u32[]{:S(2)}, u32[]{:S(2)}) collective-permute-start(bf16[384,1024]{1,0:T(8,128)(2,1)S(1)} %collective-permute-done.6), channel_id=1, source_target_pairs={{0,15},{1,0},{2,1},{3,2},{4,3},{5,4},{6,5},{7,6},{8,7},{9,8},{10,9... | collective-permute-start | bytes 2359304 | tf_op jit(solution)/shard_map/ppermute | solution.py:52
  111.8 1.9 %collective-permute-start.3 = (bf16[384,1024]{1,0:T(8,128)(2,1)S(1)}, bf16[384,1024]{1,0:T(8,128)(2,1)S(1)}, u32[]{:S(2)}, u32[]{:S(2)}) collective-permute-start(bf16[384,1024]{1,0:T(8,128)(2,1)S(1)} %collective-permute-done.2), channel_id=1, source_target_pairs={{0,1},{1,2},{2,3},{3,4},{4,5},{5,6},{6,7},{7,8},{8,9},{9,10},{10,1... | collective-permute-start | bytes 2359304 | tf_op jit(solution)/shard_map/ppermute | solution.py:52
  115.2 11.4 %collective-permute-done.7 = bf16[384,1024]{1,0:T(8,128)(2,1)S(1)} collective-permute-done((bf16[384,1024]{1,0:T(8,128)(2,1)S(1)}, bf16[384,1024]{1,0:T(8,128)(2,1)S(1)}, u32[]{:S(2)}, u32[]{:S(2)}) %collective-permute-start.7) | collective-permute-done | bytes 786464 | tf_op jit(solution)/shard_map/ppermute | solution.py:52
  127.4 5.2 %collective-permute-done.3 = bf16[384,1024]{1,0:T(8,128)(2,1)S(1)} collective-permute-done((bf16[384,1024]{1,0:T(8,128)(2,1)S(1)}, bf16[384,1024]{1,0:T(8,128)(2,1)S(1)}, u32[]{:S(2)}, u32[]{:S(2)}) %collective-permute-start.3) | collective-permute-done | bytes 786464 | tf_op jit(solution)/shard_map/ppermute | solution.py:52
  134.8 5.5 %collective-permute-start.8 = (f32[1,384]{1,0:T(1,128)S(1)}, f32[1,384]{1,0:T(1,128)S(1)}, u32[]{:S(2)}, u32[]{:S(2)}) collective-permute-start(f32[1,384]{1,0:T(1,128)S(1)} %mul.297), channel_id=1, source_target_pairs={{0,12},{1,13},{2,14},{3,15},{4,0},{5,1},{6,2},{7,3},{8,4},{9,5},{1... | collective-permute-start | bytes 4616 | tf_op jit(solution)/shard_map/ppermute | solution.py:52
  140.3 1.9 %collective-permute-start.10 = (f32[1,384]{1,0:T(1,128)S(1)}, f32[1,384]{1,0:T(1,128)S(1)}, u32[]{:S(2)}, u32[]{:S(2)}) collective-permute-start(f32[1,384]{1,0:T(1,128)S(1)} %stack.62), channel_id=1, source_target_pairs={{0,14},{1,15},{2,0},{3,1},{4,2},{5,3},{6,4},{7,5},{8,6},{9,7},{10,... | collective-permute-start | bytes 4616 | tf_op jit(solution)/shard_map/ppermute | solution.py:52
  142.2 4.8 %collective-permute-start.12 = (f32[1,384]{1,0:T(1,128)S(1)}, f32[1,384]{1,0:T(1,128)S(1)}, u32[]{:S(2)}, u32[]{:S(2)}) collective-permute-start(f32[1,384]{1,0:T(1,128)S(1)} %stack.70), channel_id=1, source_target_pairs={{0,2},{1,3},{2,4},{3,5},{4,6},{5,7},{6,8},{7,9},{8,10},{9,11},{10,... | collective-permute-start | bytes 4616 | tf_op jit(solution)/shard_map/ppermute | solution.py:52
  147.0 1.9 %collective-permute-start.11 = (f32[1,384]{1,0:T(1,128)S(1)}, f32[1,384]{1,0:T(1,128)S(1)}, u32[]{:S(2)}, u32[]{:S(2)}) collective-permute-start(f32[1,384]{1,0:T(1,128)S(1)} %stack.69), channel_id=1, source_target_pairs={{0,1},{1,2},{2,3},{3,4},{4,5},{5,6},{6,7},{7,8},{8,9},{9,10},{10,1... | collective-permute-start | bytes 4616 | tf_op jit(solution)/shard_map/ppermute | solution.py:52
  149.0 4.6 %collective-permute-start.9 = (f32[2,384]{1,0:T(2,128)S(1)}, f32[2,384]{1,0:T(2,128)S(1)}, u32[]{:S(2)}, u32[]{:S(2)}) collective-permute-start(f32[2,384]{1,0:T(2,128)S(1)} %pad_maximum_fusion.2), channel_id=1, source_target_pairs={{0,13},{1,14},{2,15},{3,0},{4,1},{5,2},{6,3},{7,4},{8,5},{9,6},{10... | collective-permute-start | bytes 9224 | tf_op jit(solution)/shard_map/ppermute | solution.py:52
  153.7 4.3 %collective-permute-start.14 = (f32[3,384]{1,0:T(4,128)S(1)}, f32[3,384]{1,0:T(4,128)S(1)}, u32[]{:S(2)}, u32[]{:S(2)}) collective-permute-start(f32[3,384]{1,0:T(4,128)S(1)} %pad_maximum_fusion.1), channel_id=1, source_target_pairs={{0,4},{1,5},{2,6},{3,7},{4,8},{5,9},{6,10},{7,11},{8,12},{9,13},{1... | collective-permute-start | bytes 13832 | tf_op jit(solution)/shard_map/ppermute | solution.py:52
  158.7 3.1 %collective-permute-start.13 = (f32[3,384]{1,0:T(4,128)S(1)}, f32[3,384]{1,0:T(4,128)S(1)}, u32[]{:S(2)}, u32[]{:S(2)}) collective-permute-start(f32[3,384]{1,0:T(4,128)S(1)} %pad_maximum_fusion), channel_id=1, source_target_pairs={{0,3},{1,4},{2,5},{3,6},{4,7},{5,8},{6,9},{7,10},{8,11},{9,12},{10... | collective-permute-start | bytes 13832 | tf_op jit(solution)/shard_map/ppermute | solution.py:52
  163.8 3.4 %collective-permute-done.13 = f32[3,384]{1,0:T(4,128)S(1)} collective-permute-done((f32[3,384]{1,0:T(4,128)S(1)}, f32[3,384]{1,0:T(4,128)S(1)}, u32[]{:S(2)}, u32[]{:S(2)}) %collective-permute-start.13) | collective-permute-done | bytes 4640 | tf_op jit(solution)/shard_map/ppermute | solution.py:52
  167.3 2.9 %scatter_custom_fusion.1 = f32[384]{0:T(512)S(1)} fusion(s32[384]{0:T(512)S(1)} %fusion.25, f32[384]{0:T(512)S(1)} %add_add_fusion, f32[]{:T(128)} %constant.155.clone.1), kind=kCustom, calls=%fused_computation.125 | custom fusion | bytes 1540 | tf_op jit(solution)/shard_map/scatter | solution.py:101
  (109 shorter events, 23.9 us)
Async XLA Ops:
  0.0 6.0 %copy-start = (bf16[288,1024]{1,0:T(8,128)(2,1)S(1)}, bf16[288,1024]{1,0:T(8,128)(2,1)}, u32[]{:S(2)}) copy-start(bf16[288,1024]{1,0:T(8,128)(2,1)} %param.13) | copy-start | bytes 1769476
  9.5 9.7 %copy-start.3 = (s32[16]{0:T(128)S(1)}, s32[16]{0:T(128)}, u32[]{:S(2)}) copy-start(s32[16]{0:T(128)} %param.15) | copy-start | bytes 196
  9.5 9.8 %copy-start.1 = (s32[3]{0:T(128)S(1)}, s32[3]{0:T(128)}, u32[]{:S(2)}) copy-start(s32[3]{0:T(128)} %constant.182.clone) | copy-start | bytes 40
  9.5 9.8 %copy-start.2 = (s32[3]{0:T(128)S(1)}, s32[3]{0:T(128)}, u32[]{:S(2)}) copy-start(s32[3]{0:T(128)} %constant.181.clone) | copy-start | bytes 40
  9.5 24.3 %all-to-all-start = ((bf16[32,12,1024]{2,1,0:T(8,128)(2,1)}), bf16[32,12,1024]{2,1,0:T(8,128)(2,1)S(1)}, u32[]{:S(2)}, u32[]{:S(2)}) async-start(bf16[32,12,1024]{2,1,0:T(8,128)(2,1)} %reshape.220), calls=%async_computation | async-start | bytes 2097152 | tf_op jit(solution)/shard_map/all_to_all | solution.py:40
  20.6 22.8 %copy-start.4 = (s32[2]{0:T(128)S(1)}, s32[2]{0:T(128)}, u32[]{:S(2)}) copy-start(s32[2]{0:T(128)} %constant.177.clone) | copy-start | bytes 28
  33.9 27.0 %collective-permute-start.4 = (bf16[384,1024]{1,0:T(8,128)(2,1)S(1)}, bf16[384,1024]{1,0:T(8,128)(2,1)S(1)}, u32[]{:S(2)}, u32[]{:S(2)}) collective-permute-start(bf16[384,1024]{1,0:T(8,128)(2,1)S(1)} %reshape.221), channel_id=1, source_target_pairs={{0,15},{1,0},{2,1},{3,2},{4,3},{5,4},{6,5},{7,6},{8,7},{9,8},{10,9... | collective-permute-start | bytes 2359304 | tf_op jit(solution)/shard_map/ppermute | solution.py:52
  43.4 23.5 %collective-permute-start = (bf16[384,1024]{1,0:T(8,128)(2,1)S(1)}, bf16[384,1024]{1,0:T(8,128)(2,1)}, u32[]{:S(2)}, u32[]{:S(2)}) collective-permute-start(bf16[384,1024]{1,0:T(8,128)(2,1)S(1)} %reshape.221), channel_id=1, source_target_pairs={{0,1},{1,2},{2,3},{3,4},{4,5},{5,6},{6,7},{7,8},{8,9},{9,10},{10,1... | collective-permute-start | bytes 2359304 | tf_op jit(solution)/shard_map/ppermute | solution.py:52
  60.9 22.8 %collective-permute-start.5 = (bf16[384,1024]{1,0:T(8,128)(2,1)S(1)}, bf16[384,1024]{1,0:T(8,128)(2,1)S(1)}, u32[]{:S(2)}, u32[]{:S(2)}) collective-permute-start(bf16[384,1024]{1,0:T(8,128)(2,1)S(1)} %collective-permute-done.4), channel_id=1, source_target_pairs={{0,15},{1,0},{2,1},{3,2},{4,3},{5,4},{6,5},{7,6},{8,7},{9,8},{10,9... | collective-permute-start | bytes 2359304 | tf_op jit(solution)/shard_map/ppermute | solution.py:52
  66.9 23.0 %collective-permute-start.1 = (bf16[384,1024]{1,0:T(8,128)(2,1)}, bf16[384,1024]{1,0:T(8,128)(2,1)S(1)}, u32[]{:S(2)}, u32[]{:S(2)}) collective-permute-start(bf16[384,1024]{1,0:T(8,128)(2,1)} %collective-permute-done), channel_id=1, source_target_pairs={{0,1},{1,2},{2,3},{3,4},{4,5},{5,6},{6,7},{7,8},{8,9},{9,10},{10,1... | collective-permute-start | bytes 2359304 | tf_op jit(solution)/shard_map/ppermute | solution.py:52
  83.7 21.9 %collective-permute-start.6 = (bf16[384,1024]{1,0:T(8,128)(2,1)S(1)}, bf16[384,1024]{1,0:T(8,128)(2,1)S(1)}, u32[]{:S(2)}, u32[]{:S(2)}) collective-permute-start(bf16[384,1024]{1,0:T(8,128)(2,1)S(1)} %collective-permute-done.5), channel_id=1, source_target_pairs={{0,15},{1,0},{2,1},{3,2},{4,3},{5,4},{6,5},{7,6},{8,7},{9,8},{10,9... | collective-permute-start | bytes 2359304 | tf_op jit(solution)/shard_map/ppermute | solution.py:52
  89.9 21.9 %collective-permute-start.2 = (bf16[384,1024]{1,0:T(8,128)(2,1)S(1)}, bf16[384,1024]{1,0:T(8,128)(2,1)S(1)}, u32[]{:S(2)}, u32[]{:S(2)}) collective-permute-start(bf16[384,1024]{1,0:T(8,128)(2,1)S(1)} %collective-permute-done.1), channel_id=1, source_target_pairs={{0,1},{1,2},{2,3},{3,4},{4,5},{5,6},{6,7},{7,8},{8,9},{9,10},{10,1... | collective-permute-start | bytes 2359304 | tf_op jit(solution)/shard_map/ppermute | solution.py:52
  105.6 21.1 %collective-permute-start.7 = (bf16[384,1024]{1,0:T(8,128)(2,1)S(1)}, bf16[384,1024]{1,0:T(8,128)(2,1)S(1)}, u32[]{:S(2)}, u32[]{:S(2)}) collective-permute-start(bf16[384,1024]{1,0:T(8,128)(2,1)S(1)} %collective-permute-done.6), channel_id=1, source_target_pairs={{0,15},{1,0},{2,1},{3,2},{4,3},{5,4},{6,5},{7,6},{8,7},{9,8},{10,9... | collective-permute-start | bytes 2359304 | tf_op jit(solution)/shard_map/ppermute | solution.py:52
  111.8 20.8 %collective-permute-start.3 = (bf16[384,1024]{1,0:T(8,128)(2,1)S(1)}, bf16[384,1024]{1,0:T(8,128)(2,1)S(1)}, u32[]{:S(2)}, u32[]{:S(2)}) collective-permute-start(bf16[384,1024]{1,0:T(8,128)(2,1)S(1)} %collective-permute-done.2), channel_id=1, source_target_pairs={{0,1},{1,2},{2,3},{3,4},{4,5},{5,6},{6,7},{7,8},{8,9},{9,10},{10,1... | collective-permute-start | bytes 2359304 | tf_op jit(solution)/shard_map/ppermute | solution.py:52
  134.8 18.9 %collective-permute-start.8 = (f32[1,384]{1,0:T(1,128)S(1)}, f32[1,384]{1,0:T(1,128)S(1)}, u32[]{:S(2)}, u32[]{:S(2)}) collective-permute-start(f32[1,384]{1,0:T(1,128)S(1)} %mul.297), channel_id=1, source_target_pairs={{0,12},{1,13},{2,14},{3,15},{4,0},{5,1},{6,2},{7,3},{8,4},{9,5},{1... | collective-permute-start | bytes 4616 | tf_op jit(solution)/shard_map/ppermute | solution.py:52
  140.3 18.4 %collective-permute-start.10 = (f32[1,384]{1,0:T(1,128)S(1)}, f32[1,384]{1,0:T(1,128)S(1)}, u32[]{:S(2)}, u32[]{:S(2)}) collective-permute-start(f32[1,384]{1,0:T(1,128)S(1)} %stack.62), channel_id=1, source_target_pairs={{0,14},{1,15},{2,0},{3,1},{4,2},{5,3},{6,4},{7,5},{8,6},{9,7},{10,... | collective-permute-start | bytes 4616 | tf_op jit(solution)/shard_map/ppermute | solution.py:52
  142.2 20.2 %collective-permute-start.12 = (f32[1,384]{1,0:T(1,128)S(1)}, f32[1,384]{1,0:T(1,128)S(1)}, u32[]{:S(2)}, u32[]{:S(2)}) collective-permute-start(f32[1,384]{1,0:T(1,128)S(1)} %stack.70), channel_id=1, source_target_pairs={{0,2},{1,3},{2,4},{3,5},{4,6},{5,7},{6,8},{7,9},{8,10},{9,11},{10,... | collective-permute-start | bytes 4616 | tf_op jit(solution)/shard_map/ppermute | solution.py:52
  147.0 15.9 %collective-permute-start.11 = (f32[1,384]{1,0:T(1,128)S(1)}, f32[1,384]{1,0:T(1,128)S(1)}, u32[]{:S(2)}, u32[]{:S(2)}) collective-permute-start(f32[1,384]{1,0:T(1,128)S(1)} %stack.69), channel_id=1, source_target_pairs={{0,1},{1,2},{2,3},{3,4},{4,5},{5,6},{6,7},{7,8},{8,9},{9,10},{10,1... | collective-permute-start | bytes 4616 | tf_op jit(solution)/shard_map/ppermute | solution.py:52
  149.0 14.7 %collective-permute-start.9 = (f32[2,384]{1,0:T(2,128)S(1)}, f32[2,384]{1,0:T(2,128)S(1)}, u32[]{:S(2)}, u32[]{:S(2)}) collective-permute-start(f32[2,384]{1,0:T(2,128)S(1)} %pad_maximum_fusion.2), channel_id=1, source_target_pairs={{0,13},{1,14},{2,15},{3,0},{4,1},{5,2},{6,3},{7,4},{8,5},{9,6},{10... | collective-permute-start | bytes 9224 | tf_op jit(solution)/shard_map/ppermute | solution.py:52
  153.7 10.0 %collective-permute-start.14 = (f32[3,384]{1,0:T(4,128)S(1)}, f32[3,384]{1,0:T(4,128)S(1)}, u32[]{:S(2)}, u32[]{:S(2)}) collective-permute-start(f32[3,384]{1,0:T(4,128)S(1)} %pad_maximum_fusion.1), channel_id=1, source_target_pairs={{0,4},{1,5},{2,6},{3,7},{4,8},{5,9},{6,10},{7,11},{8,12},{9,13},{1... | collective-permute-start | bytes 13832 | tf_op jit(solution)/shard_map/ppermute | solution.py:52
  158.7 8.5 %collective-permute-start.13 = (f32[3,384]{1,0:T(4,128)S(1)}, f32[3,384]{1,0:T(4,128)S(1)}, u32[]{:S(2)}, u32[]{:S(2)}) collective-permute-start(f32[3,384]{1,0:T(4,128)S(1)} %pad_maximum_fusion), channel_id=1, source_target_pairs={{0,3},{1,4},{2,5},{3,6},{4,7},{5,8},{6,9},{7,10},{8,11},{9,12},{10... | collective-permute-start | bytes 13832 | tf_op jit(solution)/shard_map/ppermute | solution.py:52

commit v3 on v2

--- a/solution.py
+++ b/solution.py
@@ -85,13 +85,27 @@
         add(p, q, to_p)
         add(q, p, to_q)
 
-    slot_sums = jnp.zeros((BLK,), jnp.float32)
-    for target, items in sorted(outgoing_sums.items()):
-        stacked = jnp.stack([sums for _, sums in items])
-        if target != 0:
-            stacked = shift(stacked, target)
-        sources = (me + jnp.array([s - target for s, _ in items], jnp.int32)) % grp_count
-        slot_sums = slot_sums + jnp.sum(stacked * member[sources][:, None], axis=0)
+    depth = max(len(items) for t, items in outgoing_sums.items() if t != 0)
+    zero = jnp.zeros((BLK,), jnp.float32)
+    table = [[zero] * depth for _ in range(grp_count)]
+    source_table = [[0] * depth for _ in range(grp_count)]
+    present_table = [[0.0] * depth for _ in range(grp_count)]
+    for target, items in outgoing_sums.items():
+        if target == 0:
+            continue
+        for k, (source, sums) in enumerate(items):
+            table[target % grp_count][k] = sums
+            source_table[target % grp_count][k] = source - target
+            present_table[target % grp_count][k] = 1.0
+    by_offset = jnp.stack([jnp.stack(row) for row in table])
+    by_device = by_offset[(blocks_iota - me) % grp_count]
+    arrived_sums = lax.all_to_all(by_device, "grp", split_axis=0, concat_axis=0, tiled=True)
+    offset_of_sender = (me - blocks_iota) % grp_count
+    sources = (me + jnp.array(source_table, jnp.int32)[offset_of_sender]) % grp_count
+    weights = member[sources] * jnp.array(present_table, jnp.float32)[offset_of_sender]
+    slot_sums = jnp.sum(arrived_sums * weights[:, :, None], axis=(0, 1))
+    for source, sums in outgoing_sums[0]:
+        slot_sums = slot_sums + sums * member[(me + source) % grp_count]
 
     own_valid = valid_at[0].reshape(wide_count, capacity)
     arrived = jnp.sum(own_valid, axis=1).astype(jnp.int32)

time: 172 us -> 165 us (0.959)
  starting transfers between devices: 69.5 us -> 49.6 us
  waiting for transfers between devices: 73.2 us -> 82.9 us
    ppermute x15 -> x8, starting transfers between devices: 59.9 us -> 33.9 us  [shift(): lax.ppermute(value, 'grp', [(i, (i + offset) % grp_count) for i in range(...]
    all_to_all x0 -> x1, waiting for transfers between devices: none -> 12.2 us  [per_device(): lax.all_to_all(by_device, 'grp', split_axis=0, concat_axis=0, tiled=True)]
    all_to_all x0 -> x1, starting transfers between devices: none -> 6.19 us  [per_device(): lax.all_to_all(by_device, 'grp', split_axis=0, concat_axis=0, tiled=True)]
    ppermute x15 -> x8, waiting for transfers between devices: 60 us -> 56.8 us  [shift(): lax.ppermute(value, 'grp', [(i, (i + offset) % grp_count) for i in range(...]
    add x1 -> x2, other arithmetic: 0.01 us -> 3.17 us  [the longest x1 3.16 us: per_device(): slot_sums = slot_sums + sums * member[(me + source) % grp_count]]
    mul x5 -> x1, other arithmetic: 2.51 us -> 0.01 us  [per_device(): member[sources] * jnp.array(present_table, jnp.float32)[offset_of_sender]]
  transfers between devices with their start and end apart: 16 -> 10, of which waited for: 8 -> 7; matrix products, arithmetic and copies ran while one was open for 7% -> 6% of each run, Pallas kernels for 0% -> 0%
where the time goes in v3:
time: 165 us; the launch traced here: 164 us
  waiting for transfers between devices  82.9 us (50%)
  starting transfers between devices  49.6 us (30%)
  other arithmetic  13.2 us (8%)
  local copies, waits for them, and re-layouts  9.78 us (6%)
  matrix products  7.3 us (4%)
    ppermute x8, waiting for transfers between devices, shift(): lax.ppermute(value, 'grp', [(i, (i + offset) % grp_count) for i in range(...  56.8 us
    ppermute x8, starting transfers between devices, shift(): lax.ppermute(value, 'grp', [(i, (i + offset) % grp_count) for i in range(...  33.9 us
    all_to_all x1, waiting for transfers between devices, per_device(): lax.all_to_all(outgoing.reshape(wide_count, capacity, feature_width), 'wi...  13.9 us
    all_to_all x1, waiting for transfers between devices, per_device(): lax.all_to_all(by_device, 'grp', split_axis=0, concat_axis=0, tiled=True)  12.2 us
    all_to_all x1, starting transfers between devices, per_device(): lax.all_to_all(outgoing.reshape(wide_count, capacity, feature_width), 'wi...  9.57 us
    dot_general x9, matrix products, pair_products(): lax.dot_general(left_rows, right_rows, (((1,), (1,)), ((), ())), preferre...  7.3 us
    all_to_all x1, starting transfers between devices, per_device(): lax.all_to_all(by_device, 'grp', split_axis=0, concat_axis=0, tiled=True)  6.19 us
  transfers between devices with their start and end apart: 10, of which 7 were waited for; matrix products, arithmetic and copies ran while one was open for 6% of the time, Pallas kernels for 0%

profile of v3, /device:TPU:6, one launch (start us, length us, event | category | flops | bytes accessed | tf_op | source)
XLA Modules:
  0.0 164.0 jit_solution(4481105108497179653)
XLA Ops:
  1.3 1.3 fusion.20
  6.0 2.3 %scatter_custom_fusion = bf16[384,1024]{1,0:T(8,128)(2,1)S(1)} fusion(bf16[384,1024]{1,0:T(8,128)(2,1)S(1)} %scatter.22, s32[288]{0:T(512)S(1)} %compare_select_fusion.2, bf16[288,1024]{1,0:T(8,128)(2,1)S(1)} %copy-done, f32[288]{0:T(512)S(1)} %add_rsqrt_fusion), kind=kCustom, calls=%fused_computation.39 | custom fusion | flops 884736 | bytes 1378304 | tf_op jit(solution)/shard_map/scatter | solution.py:39
  8.3 1.2 reshape.346
  9.5 9.6 %all-to-all-start = ((bf16[32,12,1024]{2,1,0:T(8,128)(2,1)}), bf16[32,12,1024]{2,1,0:T(8,128)(2,1)S(1)}, u32[]{:S(2)}, u32[]{:S(2)}) async-start(bf16[32,12,1024]{2,1,0:T(8,128)(2,1)} %reshape.346), calls=%async_computation | async-start | bytes 2097152 | tf_op jit(solution)/shard_map/all_to_all | solution.py:40
  19.9 13.9 %all-to-all-done = bf16[32,12,1024]{2,1,0:T(8,128)(2,1)S(1)} async-done(((bf16[32,12,1024]{2,1,0:T(8,128)(2,1)}), bf16[32,12,1024]{2,1,0:T(8,128)(2,1)S(1)}, u32[]{:S(2)}, u32[]{:S(2)}) %all-to-all-start) | async-done | bytes 786464 | tf_op jit(solution)/shard_map/all_to_all | solution.py:40
  33.9 9.4 %collective-permute-start = (bf16[384,1024]{1,0:T(8,128)(2,1)S(1)}, bf16[384,1024]{1,0:T(8,128)(2,1)S(1)}, u32[]{:S(2)}, u32[]{:S(2)}) collective-permute-start(bf16[384,1024]{1,0:T(8,128)(2,1)S(1)} %reshape.347), channel_id=1, source_target_pairs={{0,15},{1,0},{2,1},{3,2},{4,3},{5,4},{6,5},{7,6},{8,7},{9,8},{10,9... | collective-permute-start | bytes 2359304 | tf_op jit(solution)/shard_map/ppermute | solution.py:52
  43.4 1.9 %collective-permute-start.3 = (bf16[384,1024]{1,0:T(8,128)(2,1)S(1)}, bf16[384,1024]{1,0:T(8,128)(2,1)}, u32[]{:S(2)}, u32[]{:S(2)}) collective-permute-start(bf16[384,1024]{1,0:T(8,128)(2,1)S(1)} %reshape.347), channel_id=1, source_target_pairs={{0,1},{1,2},{2,3},{3,4},{4,5},{5,6},{6,7},{7,8},{8,9},{9,10},{10,1... | collective-permute-start | bytes 2359304 | tf_op jit(solution)/shard_map/ppermute | solution.py:52
  48.2 12.7 %collective-permute-done = bf16[384,1024]{1,0:T(8,128)(2,1)S(1)} collective-permute-done((bf16[384,1024]{1,0:T(8,128)(2,1)S(1)}, bf16[384,1024]{1,0:T(8,128)(2,1)S(1)}, u32[]{:S(2)}, u32[]{:S(2)}) %collective-permute-start) | collective-permute-done | bytes 786464 | tf_op jit(solution)/shard_map/ppermute | solution.py:52
  60.9 5.6 %collective-permute-start.1 = (bf16[384,1024]{1,0:T(8,128)(2,1)S(1)}, bf16[384,1024]{1,0:T(8,128)(2,1)S(1)}, u32[]{:S(2)}, u32[]{:S(2)}) collective-permute-start(bf16[384,1024]{1,0:T(8,128)(2,1)S(1)} %collective-permute-done), channel_id=1, source_target_pairs={{0,15},{1,0},{2,1},{3,2},{4,3},{5,4},{6,5},{7,6},{8,7},{9,8},{10,9... | collective-permute-start | bytes 2359304 | tf_op jit(solution)/shard_map/ppermute | solution.py:52
  66.9 1.9 %collective-permute-start.4 = (bf16[384,1024]{1,0:T(8,128)(2,1)}, bf16[384,1024]{1,0:T(8,128)(2,1)}, u32[]{:S(2)}, u32[]{:S(2)}) collective-permute-start(bf16[384,1024]{1,0:T(8,128)(2,1)} %collective-permute-done.3), channel_id=1, source_target_pairs={{0,1},{1,2},{2,3},{3,4},{4,5},{5,6},{6,7},{7,8},{8,9},{9,10},{10,1... | collective-permute-start | bytes 2359304 | tf_op jit(solution)/shard_map/ppermute | solution.py:52
  69.1 14.5 %collective-permute-done.1 = bf16[384,1024]{1,0:T(8,128)(2,1)S(1)} collective-permute-done((bf16[384,1024]{1,0:T(8,128)(2,1)S(1)}, bf16[384,1024]{1,0:T(8,128)(2,1)S(1)}, u32[]{:S(2)}, u32[]{:S(2)}) %collective-permute-start.1) | collective-permute-done | bytes 786464 | tf_op jit(solution)/shard_map/ppermute | solution.py:52
  83.7 5.6 %collective-permute-start.2 = (bf16[384,1024]{1,0:T(8,128)(2,1)S(1)}, bf16[384,1024]{1,0:T(8,128)(2,1)S(1)}, u32[]{:S(2)}, u32[]{:S(2)}) collective-permute-start(bf16[384,1024]{1,0:T(8,128)(2,1)S(1)} %collective-permute-done.1), channel_id=1, source_target_pairs={{0,15},{1,0},{2,1},{3,2},{4,3},{5,4},{6,5},{7,6},{8,7},{9,8},{10,9... | collective-permute-start | bytes 2359304 | tf_op jit(solution)/shard_map/ppermute | solution.py:52
  89.9 1.9 %collective-permute-start.5 = (bf16[384,1024]{1,0:T(8,128)(2,1)}, bf16[384,1024]{1,0:T(8,128)(2,1)S(1)}, u32[]{:S(2)}, u32[]{:S(2)}) collective-permute-start(bf16[384,1024]{1,0:T(8,128)(2,1)} %collective-permute-done.4), channel_id=1, source_target_pairs={{0,1},{1,2},{2,3},{3,4},{4,5},{5,6},{6,7},{7,8},{8,9},{9,10},{10,1... | collective-permute-start | bytes 2359304 | tf_op jit(solution)/shard_map/ppermute | solution.py:52
  93.6 12.0 %collective-permute-done.2 = bf16[384,1024]{1,0:T(8,128)(2,1)S(1)} collective-permute-done((bf16[384,1024]{1,0:T(8,128)(2,1)S(1)}, bf16[384,1024]{1,0:T(8,128)(2,1)S(1)}, u32[]{:S(2)}, u32[]{:S(2)}) %collective-permute-start.2) | collective-permute-done | bytes 786464 | tf_op jit(solution)/shard_map/ppermute | solution.py:52
  105.6 5.6 %collective-permute-start.6 = (bf16[384,1024]{1,0:T(8,128)(2,1)S(1)}, bf16[384,1024]{1,0:T(8,128)(2,1)S(1)}, u32[]{:S(2)}, u32[]{:S(2)}) collective-permute-start(bf16[384,1024]{1,0:T(8,128)(2,1)S(1)} %collective-permute-done.2), channel_id=1, source_target_pairs={{0,15},{1,0},{2,1},{3,2},{4,3},{5,4},{6,5},{7,6},{8,7},{9,8},{10,9... | collective-permute-start | bytes 2359304 | tf_op jit(solution)/shard_map/ppermute | solution.py:52
  111.2 1.7 %fusion.7 = f32[384,384]{1,0:T(8,128)S(1)} fusion(bf16[384,1024]{1,0:T(8,128)(2,1)} %collective-permute-done.4, bf16[384,1024]{1,0:T(8,128)(2,1)S(1)} %collective-permute-done.2), kind=kOutput, calls=%fused_computation.24 | convolution fusion | flops 302284800 | bytes 2162688 | tf_op jit(solution)/shard_map/dot_general | solution.py:15
  112.9 1.9 %collective-permute-start.7 = (bf16[384,1024]{1,0:T(8,128)(2,1)S(1)}, bf16[384,1024]{1,0:T(8,128)(2,1)S(1)}, u32[]{:S(2)}, u32[]{:S(2)}) collective-permute-start(bf16[384,1024]{1,0:T(8,128)(2,1)S(1)} %collective-permute-done.5), channel_id=1, source_target_pairs={{0,1},{1,2},{2,3},{3,4},{4,5},{5,6},{6,7},{7,8},{8,9},{9,10},{10,1... | collective-permute-start | bytes 2359304 | tf_op jit(solution)/shard_map/ppermute | solution.py:52
  116.3 17.4 %collective-permute-done.7 = bf16[384,1024]{1,0:T(8,128)(2,1)S(1)} collective-permute-done((bf16[384,1024]{1,0:T(8,128)(2,1)S(1)}, bf16[384,1024]{1,0:T(8,128)(2,1)S(1)}, u32[]{:S(2)}, u32[]{:S(2)}) %collective-permute-start.7) | collective-permute-done | bytes 786464 | tf_op jit(solution)/shard_map/ppermute | solution.py:52
  135.2 1.2 multiply_reduce_fusion.10
  136.8 1.2 gather_fusion
  138.0 6.2 %all-to-all-start.1 = ((f32[16,3,384]{2,1,0:T(4,128)}), f32[16,3,384]{2,1,0:T(4,128)S(1)}, u32[]{:S(2)}, u32[]{:S(2)}) async-start(f32[16,3,384]{2,1,0:T(4,128)} %gather_fusion), calls=%async_computation.1 | async-start | bytes 196608 | tf_op jit(solution)/shard_map/all_to_all | solution.py:102
  145.0 12.2 %all-to-all-done.1 = f32[16,3,384]{2,1,0:T(4,128)S(1)} async-done(((f32[16,3,384]{2,1,0:T(4,128)}), f32[16,3,384]{2,1,0:T(4,128)S(1)}, u32[]{:S(2)}, u32[]{:S(2)}) %all-to-all-start.1) | async-done | bytes 73760 | tf_op jit(solution)/shard_map/all_to_all | solution.py:102
  157.3 3.2 %multiply_add_fusion = f32[384]{0:T(512)S(1)} fusion(f32[384]{0:T(512)S(1)} %get-tuple-element.26, f32[384]{0:T(512)S(1)} %get-tuple-element.43, f32[384]{0:T(512)S(1)} %get-tuple-element.47, f32[384]{0:T(512)S(1)} %get-tuple-element.49, f32[384]{0:T(512)S(1)} %multiply_reduce_fusion.16, f32[384]{0:T(512)S(1)} %fusion.19, f32[]{:T(128)} %bitcast.17, ...), kind=kLoop, calls=%fused_computation.120 | loop fusion | flops 3840 | bytes 10772 | tf_op jit(solution)/shard_map/add | solution.py:108
  160.5 2.9 %scatter_custom_fusion.1 = f32[384]{0:T(512)S(1)} fusion(s32[384]{0:T(512)S(1)} %fusion.25, f32[384]{0:T(512)S(1)} %multiply_add_fusion, f32[]{:T(128)} %constant.130.clone.1), kind=kCustom, calls=%fused_computation.127 | custom fusion | bytes 1540 | tf_op jit(solution)/shard_map/scatter | solution.py:115
  (95 shorter events, 15.4 us)
Async XLA Ops:
  0.0 6.0 %copy-start = (bf16[288,1024]{1,0:T(8,128)(2,1)S(1)}, bf16[288,1024]{1,0:T(8,128)(2,1)}, u32[]{:S(2)}) copy-start(bf16[288,1024]{1,0:T(8,128)(2,1)} %param.7) | copy-start | bytes 1769476
  9.5 9.7 %copy-start.2 = (s32[16,3]{1,0:T(8,128)S(1)}, s32[16,3]{1,0:T(8,128)}, u32[]{:S(2)}) copy-start(s32[16,3]{1,0:T(8,128)} %constant.152.clone) | copy-start | bytes 580
  9.5 24.3 %all-to-all-start = ((bf16[32,12,1024]{2,1,0:T(8,128)(2,1)}), bf16[32,12,1024]{2,1,0:T(8,128)(2,1)S(1)}, u32[]{:S(2)}, u32[]{:S(2)}) async-start(bf16[32,12,1024]{2,1,0:T(8,128)(2,1)} %reshape.346), calls=%async_computation | async-start | bytes 2097152 | tf_op jit(solution)/shard_map/all_to_all | solution.py:40
  19.1 26.3 %copy-start.3 = (s32[16]{0:T(128)S(1)}, s32[16]{0:T(128)}, u32[]{:S(2)}) copy-start(s32[16]{0:T(128)} %param.9) | copy-start | bytes 196
  19.1 26.4 %copy-start.1 = (f32[16,3]{1,0:T(8,128)S(1)}, f32[16,3]{1,0:T(8,128)}, u32[]{:S(2)}) copy-start(f32[16,3]{1,0:T(8,128)} %constant.153.clone) | copy-start | bytes 580
  33.9 27.0 %collective-permute-start = (bf16[384,1024]{1,0:T(8,128)(2,1)S(1)}, bf16[384,1024]{1,0:T(8,128)(2,1)S(1)}, u32[]{:S(2)}, u32[]{:S(2)}) collective-permute-start(bf16[384,1024]{1,0:T(8,128)(2,1)S(1)} %reshape.347), channel_id=1, source_target_pairs={{0,15},{1,0},{2,1},{3,2},{4,3},{5,4},{6,5},{7,6},{8,7},{9,8},{10,9... | collective-permute-start | bytes 2359304 | tf_op jit(solution)/shard_map/ppermute | solution.py:52
  43.4 23.5 %collective-permute-start.3 = (bf16[384,1024]{1,0:T(8,128)(2,1)S(1)}, bf16[384,1024]{1,0:T(8,128)(2,1)}, u32[]{:S(2)}, u32[]{:S(2)}) collective-permute-start(bf16[384,1024]{1,0:T(8,128)(2,1)S(1)} %reshape.347), channel_id=1, source_target_pairs={{0,1},{1,2},{2,3},{3,4},{4,5},{5,6},{6,7},{7,8},{8,9},{9,10},{10,1... | collective-permute-start | bytes 2359304 | tf_op jit(solution)/shard_map/ppermute | solution.py:52
  60.9 22.8 %collective-permute-start.1 = (bf16[384,1024]{1,0:T(8,128)(2,1)S(1)}, bf16[384,1024]{1,0:T(8,128)(2,1)S(1)}, u32[]{:S(2)}, u32[]{:S(2)}) collective-permute-start(bf16[384,1024]{1,0:T(8,128)(2,1)S(1)} %collective-permute-done), channel_id=1, source_target_pairs={{0,15},{1,0},{2,1},{3,2},{4,3},{5,4},{6,5},{7,6},{8,7},{9,8},{10,9... | collective-permute-start | bytes 2359304 | tf_op jit(solution)/shard_map/ppermute | solution.py:52
  66.9 23.0 %collective-permute-start.4 = (bf16[384,1024]{1,0:T(8,128)(2,1)}, bf16[384,1024]{1,0:T(8,128)(2,1)}, u32[]{:S(2)}, u32[]{:S(2)}) collective-permute-start(bf16[384,1024]{1,0:T(8,128)(2,1)} %collective-permute-done.3), channel_id=1, source_target_pairs={{0,1},{1,2},{2,3},{3,4},{4,5},{5,6},{6,7},{7,8},{8,9},{9,10},{10,1... | collective-permute-start | bytes 2359304 | tf_op jit(solution)/shard_map/ppermute | solution.py:52
  83.7 21.9 %collective-permute-start.2 = (bf16[384,1024]{1,0:T(8,128)(2,1)S(1)}, bf16[384,1024]{1,0:T(8,128)(2,1)S(1)}, u32[]{:S(2)}, u32[]{:S(2)}) collective-permute-start(bf16[384,1024]{1,0:T(8,128)(2,1)S(1)} %collective-permute-done.1), channel_id=1, source_target_pairs={{0,15},{1,0},{2,1},{3,2},{4,3},{5,4},{6,5},{7,6},{8,7},{9,8},{10,9... | collective-permute-start | bytes 2359304 | tf_op jit(solution)/shard_map/ppermute | solution.py:52
  89.9 23.0 %collective-permute-start.5 = (bf16[384,1024]{1,0:T(8,128)(2,1)}, bf16[384,1024]{1,0:T(8,128)(2,1)S(1)}, u32[]{:S(2)}, u32[]{:S(2)}) collective-permute-start(bf16[384,1024]{1,0:T(8,128)(2,1)} %collective-permute-done.4), channel_id=1, source_target_pairs={{0,1},{1,2},{2,3},{3,4},{4,5},{5,6},{6,7},{7,8},{8,9},{9,10},{10,1... | collective-permute-start | bytes 2359304 | tf_op jit(solution)/shard_map/ppermute | solution.py:52
  105.6 28.3 %collective-permute-start.6 = (bf16[384,1024]{1,0:T(8,128)(2,1)S(1)}, bf16[384,1024]{1,0:T(8,128)(2,1)S(1)}, u32[]{:S(2)}, u32[]{:S(2)}) collective-permute-start(bf16[384,1024]{1,0:T(8,128)(2,1)S(1)} %collective-permute-done.2), channel_id=1, source_target_pairs={{0,15},{1,0},{2,1},{3,2},{4,3},{5,4},{6,5},{7,6},{8,7},{9,8},{10,9... | collective-permute-start | bytes 2359304 | tf_op jit(solution)/shard_map/ppermute | solution.py:52
  112.9 20.8 %collective-permute-start.7 = (bf16[384,1024]{1,0:T(8,128)(2,1)S(1)}, bf16[384,1024]{1,0:T(8,128)(2,1)S(1)}, u32[]{:S(2)}, u32[]{:S(2)}) collective-permute-start(bf16[384,1024]{1,0:T(8,128)(2,1)S(1)} %collective-permute-done.5), channel_id=1, source_target_pairs={{0,1},{1,2},{2,3},{3,4},{4,5},{5,6},{6,7},{7,8},{8,9},{9,10},{10,1... | collective-permute-start | bytes 2359304 | tf_op jit(solution)/shard_map/ppermute | solution.py:52
  138.0 19.2 %all-to-all-start.1 = ((f32[16,3,384]{2,1,0:T(4,128)}), f32[16,3,384]{2,1,0:T(4,128)S(1)}, u32[]{:S(2)}, u32[]{:S(2)}) async-start(f32[16,3,384]{2,1,0:T(4,128)} %gather_fusion), calls=%async_computation.1 | async-start | bytes 196608 | tf_op jit(solution)/shard_map/all_to_all | solution.py:102

commit v4 on v3

--- a/solution.py
+++ b/solution.py
@@ -36,14 +36,13 @@
     row_ranks = jnp.sum(jnp.cumsum(onehot, axis=0) * onehot, axis=1) - 1
     send_slots = bucket * capacity + row_ranks
     empty = jnp.zeros((wide_count * capacity, feature_width), jnp.bfloat16).at[:, 0].set(SENTINEL)
-    outgoing = empty.at[send_slots].set(unit_rows)
-    own = lax.all_to_all(
-        outgoing.reshape(wide_count, capacity, feature_width),
-        "wide",
-        split_axis=0,
-        concat_axis=0,
-        tiled=True,
-    ).reshape(BLK, feature_width)
+    outgoing = empty.at[send_slots].set(unit_rows).reshape(wide_count, capacity, feature_width)
+    split = capacity // 2
+    halves = [outgoing[:, :split], outgoing[:, split:]]
+    own_halves = [
+        lax.all_to_all(h, "wide", split_axis=0, concat_axis=0, tiled=True).reshape(-1, feature_width)
+        for h in halves
+    ]
 
     def valid_of(rows):
         return (rows[:, 0].astype(jnp.float32) < 1.5).astype(jnp.float32)
@@ -54,15 +53,18 @@
         )
 
     reach = 4
-    left = {0: own}
-    right = {0: own}
-    for step in range(1, reach + 1):
-        left[step] = shift(left[step - 1], 1)
-        right[step] = shift(right[step - 1], -1)
-    rows_at = {0: own}
-    for step in range(1, reach + 1):
-        rows_at[-step] = left[step]
-        rows_at[step] = right[step]
+    rows_at = {}
+    for part in own_halves:
+        left = part
+        right = part
+        rows_at.setdefault(0, []).append(part)
+        for step in range(1, reach + 1):
+            left = shift(left, 1)
+            right = shift(right, -1)
+            rows_at.setdefault(-step, []).append(left)
+            rows_at.setdefault(step, []).append(right)
+    rows_at = {k: jnp.concatenate(v, axis=0) for k, v in rows_at.items()}
+    own = rows_at[0]
     valid_at = {k: valid_of(v) for k, v in rows_at.items()}
 
     outgoing_sums = {}
@@ -107,11 +109,12 @@
     for source, sums in outgoing_sums[0]:
         slot_sums = slot_sums + sums * member[(me + source) % grp_count]
 
-    own_valid = valid_at[0].reshape(wide_count, capacity)
+    own_valid = valid_at[0].reshape(2, wide_count, split).transpose(1, 0, 2).reshape(wide_count, capacity)
     arrived = jnp.sum(own_valid, axis=1).astype(jnp.int32)
     offsets = jnp.cumsum(arrived) - arrived
     within = jnp.arange(capacity, dtype=jnp.int32)
-    places = jnp.where(own_valid > 0, offsets[:, None] + within[None, :], BLK).reshape(-1)
+    places = jnp.where(own_valid > 0, offsets[:, None] + within[None, :], BLK)
+    places = places.reshape(wide_count, 2, split).transpose(1, 0, 2).reshape(-1)
     density = jnp.zeros((BLK,), jnp.float32).at[places].set(slot_sums, mode="drop")
     return density.reshape(1, BLK)
 

time: 165 us -> 163 us (0.988)
  waiting for transfers between devices: 82.9 us -> 44.2 us
  starting transfers between devices: 49.6 us -> 86.6 us
    ppermute x8 -> x16, waiting for transfers between devices: 56.8 us -> 23.6 us  [shift(): lax.ppermute(value, 'grp', [(i, (i + offset) % grp_count) for i in range(...]
    ppermute x8 -> x16, starting transfers between devices: 33.9 us -> 61.1 us  [shift(): lax.ppermute(value, 'grp', [(i, (i + offset) % grp_count) for i in range(...]
    all_to_all x1 -> x2, starting transfers between devices: 9.57 us -> 15.6 us  [per_device(): lax.all_to_all(h, 'wide', split_axis=0, concat_axis=0, tiled=True)]
    all_to_all x1 -> x2, waiting for transfers between devices: 13.9 us -> 8.42 us  [per_device(): lax.all_to_all(h, 'wide', split_axis=0, concat_axis=0, tiled=True)]
    all_to_all x1, starting transfers between devices: 6.19 us -> 9.92 us  [per_device(): lax.all_to_all(by_device, 'grp', split_axis=0, concat_axis=0, tiled=True)]
  transfers between devices with their start and end apart: 10 -> 19, of which waited for: 7 -> 9; matrix products, arithmetic and copies ran while one was open for 6% -> 6% of each run, Pallas kernels for 0% -> 0%
where the time goes in v4:
time: 163 us; the launch traced here: 161 us
  starting transfers between devices  86.6 us (53%)
  waiting for transfers between devices  44.2 us (27%)
  other arithmetic  12.3 us (8%)
  local copies, waits for them, and re-layouts  10.6 us (7%)
  matrix products  6.26 us (4%)
    ppermute x16, starting transfers between devices, shift(): lax.ppermute(value, 'grp', [(i, (i + offset) % grp_count) for i in range(...  61.1 us
    ppermute x16, waiting for transfers between devices, shift(): lax.ppermute(value, 'grp', [(i, (i + offset) % grp_count) for i in range(...  23.6 us
    all_to_all x2, starting transfers between devices, per_device(): lax.all_to_all(h, 'wide', split_axis=0, concat_axis=0, tiled=True)  15.6 us
    all_to_all x1, waiting for transfers between devices, per_device(): lax.all_to_all(by_device, 'grp', split_axis=0, concat_axis=0, tiled=True)  12.2 us
    all_to_all x1, starting transfers between devices, per_device(): lax.all_to_all(by_device, 'grp', split_axis=0, concat_axis=0, tiled=True)  9.92 us
    all_to_all x2, waiting for transfers between devices, per_device(): lax.all_to_all(h, 'wide', split_axis=0, concat_axis=0, tiled=True)  8.42 us
    dot_general x9, matrix products, pair_products(): lax.dot_general(left_rows, right_rows, (((1,), (1,)), ((), ())), preferre...  6.26 us
  transfers between devices with their start and end apart: 19, of which 9 were waited for; matrix products, arithmetic and copies ran while one was open for 6% of the time, Pallas kernels for 0%

profile of v4, /device:TPU:6, one launch (start us, length us, event | category | flops | bytes accessed | tf_op | source)
XLA Modules:
  0.0 161.5 jit_solution(3552143591611528739)
XLA Ops:
  6.0 2.3 %scatter_custom_fusion = bf16[384,1024]{1,0:T(8,128)(2,1)S(1)} fusion(bf16[384,1024]{1,0:T(8,128)(2,1)S(1)} %scatter.22, s32[288]{0:T(512)S(1)} %compare_select_fusion.2, bf16[288,1024]{1,0:T(8,128)(2,1)S(1)} %copy-done, f32[288]{0:T(512)S(1)} %add_rsqrt_fusion), kind=kCustom, calls=%fused_computation.39 | custom fusion | flops 884736 | bytes 1378304 | tf_op jit(solution)/shard_map/scatter | solution.py:39
  9.7 9.5 %all-to-all-start = ((bf16[32,6,1024]{2,1,0:T(8,128)(2,1)}), bf16[32,6,1024]{2,1,0:T(8,128)(2,1)S(1)}, u32[]{:S(2)}, u32[]{:S(2)}) async-start(bf16[32,6,1024]{2,1,0:T(8,128)(2,1)} %get-tuple-element.52), calls=%async_computation | async-start | bytes 1048576 | tf_op jit(solution)/shard_map/all_to_all | solution.py:43
  20.3 8.4 %all-to-all-done = bf16[32,6,1024]{2,1,0:T(8,128)(2,1)S(1)} async-done(((bf16[32,6,1024]{2,1,0:T(8,128)(2,1)}), bf16[32,6,1024]{2,1,0:T(8,128)(2,1)S(1)}, u32[]{:S(2)}, u32[]{:S(2)}) %all-to-all-start) | async-done | bytes 393248 | tf_op jit(solution)/shard_map/all_to_all | solution.py:43
  28.7 6.1 %all-to-all-start.1 = ((bf16[32,6,1024]{2,1,0:T(8,128)(2,1)}), bf16[32,6,1024]{2,1,0:T(8,128)(2,1)S(1)}, u32[]{:S(2)}, u32[]{:S(2)}) async-start(bf16[32,6,1024]{2,1,0:T(8,128)(2,1)} %get-tuple-element.51), calls=%async_computation.1 | async-start | bytes 1048576 | tf_op jit(solution)/shard_map/all_to_all | solution.py:43
  37.2 1.9 %collective-permute-start.6 = (bf16[192,1024]{1,0:T(8,128)(2,1)S(1)}, bf16[192,1024]{1,0:T(8,128)(2,1)}, u32[]{:S(2)}, u32[]{:S(2)}) collective-permute-start(bf16[192,1024]{1,0:T(8,128)(2,1)S(1)} %reshape.382), channel_id=1, source_target_pairs={{0,1},{1,2},{2,3},{3,4},{4,5},{5,6},{6,7},{7,8},{8,9},{9,10},{10,1... | collective-permute-start | bytes 1179656 | tf_op jit(solution)/shard_map/ppermute | solution.py:51
  39.1 9.5 %collective-permute-start = (bf16[192,1024]{1,0:T(8,128)(2,1)S(1)}, bf16[192,1024]{1,0:T(8,128)(2,1)S(1)}, u32[]{:S(2)}, u32[]{:S(2)}) collective-permute-start(bf16[192,1024]{1,0:T(8,128)(2,1)S(1)} %reshape.382), channel_id=1, source_target_pairs={{0,15},{1,0},{2,1},{3,2},{4,3},{5,4},{6,5},{7,6},{8,7},{9,8},{10,9... | collective-permute-start | bytes 1179656 | tf_op jit(solution)/shard_map/ppermute | solution.py:51
  48.8 1.9 %collective-permute-start.8 = (bf16[192,1024]{1,0:T(8,128)(2,1)S(1)}, bf16[192,1024]{1,0:T(8,128)(2,1)S(1)}, u32[]{:S(2)}, u32[]{:S(2)}) collective-permute-start(bf16[192,1024]{1,0:T(8,128)(2,1)S(1)} %reshape.383), channel_id=1, source_target_pairs={{0,1},{1,2},{2,3},{3,4},{4,5},{5,6},{6,7},{7,8},{8,9},{9,10},{10,1... | collective-permute-start | bytes 1179656 | tf_op jit(solution)/shard_map/ppermute | solution.py:51
  50.7 5.1 %collective-permute-start.1 = (bf16[192,1024]{1,0:T(8,128)(2,1)S(1)}, bf16[192,1024]{1,0:T(8,128)(2,1)S(1)}, u32[]{:S(2)}, u32[]{:S(2)}) collective-permute-start(bf16[192,1024]{1,0:T(8,128)(2,1)S(1)} %reshape.383), channel_id=1, source_target_pairs={{0,15},{1,0},{2,1},{3,2},{4,3},{5,4},{6,5},{7,6},{8,7},{9,8},{10,9... | collective-permute-start | bytes 1179656 | tf_op jit(solution)/shard_map/ppermute | solution.py:51
  58.7 5.1 %collective-permute-start.2 = (bf16[192,1024]{1,0:T(8,128)(2,1)S(1)}, bf16[192,1024]{1,0:T(8,128)(2,1)S(1)}, u32[]{:S(2)}, u32[]{:S(2)}) collective-permute-start(bf16[192,1024]{1,0:T(8,128)(2,1)S(1)} %collective-permute-done), channel_id=1, source_target_pairs={{0,15},{1,0},{2,1},{3,2},{4,3},{5,4},{6,5},{7,6},{8,7},{9,8},{10,9... | collective-permute-start | bytes 1179656 | tf_op jit(solution)/shard_map/ppermute | solution.py:51
  66.9 5.1 %collective-permute-start.3 = (bf16[192,1024]{1,0:T(8,128)(2,1)S(1)}, bf16[192,1024]{1,0:T(8,128)(2,1)S(1)}, u32[]{:S(2)}, u32[]{:S(2)}) collective-permute-start(bf16[192,1024]{1,0:T(8,128)(2,1)S(1)} %collective-permute-done.1), channel_id=1, source_target_pairs={{0,15},{1,0},{2,1},{3,2},{4,3},{5,4},{6,5},{7,6},{8,7},{9,8},{10,9... | collective-permute-start | bytes 1179656 | tf_op jit(solution)/shard_map/ppermute | solution.py:51
  74.5 5.6 %collective-permute-start.4 = (bf16[192,1024]{1,0:T(8,128)(2,1)S(1)}, bf16[192,1024]{1,0:T(8,128)(2,1)S(1)}, u32[]{:S(2)}, u32[]{:S(2)}) collective-permute-start(bf16[192,1024]{1,0:T(8,128)(2,1)S(1)} %collective-permute-done.2), channel_id=1, source_target_pairs={{0,15},{1,0},{2,1},{3,2},{4,3},{5,4},{6,5},{7,6},{8,7},{9,8},{10,9... | collective-permute-start | bytes 1179656 | tf_op jit(solution)/shard_map/ppermute | solution.py:51
  80.2 1.9 %collective-permute-start.10 = (bf16[192,1024]{1,0:T(8,128)(2,1)S(1)}, bf16[192,1024]{1,0:T(8,128)(2,1)S(1)}, u32[]{:S(2)}, u32[]{:S(2)}) collective-permute-start(bf16[192,1024]{1,0:T(8,128)(2,1)S(1)} %collective-permute-done.7), channel_id=1, source_target_pairs={{0,1},{1,2},{2,3},{3,4},{4,5},{5,6},{6,7},{7,8},{8,9},{9,10},{10,1... | collective-permute-start | bytes 1179656 | tf_op jit(solution)/shard_map/ppermute | solution.py:51
  83.0 5.6 %collective-permute-start.5 = (bf16[192,1024]{1,0:T(8,128)(2,1)S(1)}, bf16[192,1024]{1,0:T(8,128)(2,1)S(1)}, u32[]{:S(2)}, u32[]{:S(2)}) collective-permute-start(bf16[192,1024]{1,0:T(8,128)(2,1)S(1)} %collective-permute-done.3), channel_id=1, source_target_pairs={{0,15},{1,0},{2,1},{3,2},{4,3},{5,4},{6,5},{7,6},{8,7},{9,8},{10,9... | collective-permute-start | bytes 1179656 | tf_op jit(solution)/shard_map/ppermute | solution.py:51
  88.8 1.9 %collective-permute-start.11 = (bf16[192,1024]{1,0:T(8,128)(2,1)S(1)}, bf16[192,1024]{1,0:T(8,128)(2,1)S(1)}, u32[]{:S(2)}, u32[]{:S(2)}) collective-permute-start(bf16[192,1024]{1,0:T(8,128)(2,1)S(1)} %collective-permute-done.9), channel_id=1, source_target_pairs={{0,1},{1,2},{2,3},{3,4},{4,5},{5,6},{6,7},{7,8},{8,9},{9,10},{10,1... | collective-permute-start | bytes 1179656 | tf_op jit(solution)/shard_map/ppermute | solution.py:51
  91.5 7.9 %collective-permute-done.5 = bf16[192,1024]{1,0:T(8,128)(2,1)S(1)} collective-permute-done((bf16[192,1024]{1,0:T(8,128)(2,1)S(1)}, bf16[192,1024]{1,0:T(8,128)(2,1)S(1)}, u32[]{:S(2)}, u32[]{:S(2)}) %collective-permute-start.5) | collective-permute-done | bytes 393248 | tf_op jit(solution)/shard_map/ppermute | solution.py:51
  100.1 1.9 %collective-permute-start.14 = (bf16[192,1024]{1,0:T(8,128)(2,1)S(1)}, bf16[192,1024]{1,0:T(8,128)(2,1)S(1)}, u32[]{:S(2)}, u32[]{:S(2)}) collective-permute-start(bf16[192,1024]{1,0:T(8,128)(2,1)S(1)} %collective-permute-done.10), channel_id=1, source_target_pairs={{0,1},{1,2},{2,3},{3,4},{4,5},{5,6},{6,7},{7,8},{8,9},{9,10},{10,1... | collective-permute-start | bytes 1179656 | tf_op jit(solution)/shard_map/ppermute | solution.py:51
  105.2 5.6 %collective-permute-start.12 = (bf16[192,1024]{1,0:T(8,128)(2,1)S(1)}, bf16[192,1024]{1,0:T(8,128)(2,1)S(1)}, u32[]{:S(2)}, u32[]{:S(2)}) collective-permute-start(bf16[192,1024]{1,0:T(8,128)(2,1)S(1)} %collective-permute-done.4), channel_id=1, source_target_pairs={{0,15},{1,0},{2,1},{3,2},{4,3},{5,4},{6,5},{7,6},{8,7},{9,8},{10,9... | collective-permute-start | bytes 1179656 | tf_op jit(solution)/shard_map/ppermute | solution.py:51
  111.1 4.1 %collective-permute-start.13 = (bf16[192,1024]{1,0:T(8,128)(2,1)S(1)}, bf16[192,1024]{1,0:T(8,128)(2,1)S(1)}, u32[]{:S(2)}, u32[]{:S(2)}) collective-permute-start(bf16[192,1024]{1,0:T(8,128)(2,1)S(1)} %collective-permute-done.5), channel_id=1, source_target_pairs={{0,15},{1,0},{2,1},{3,2},{4,3},{5,4},{6,5},{7,6},{8,7},{9,8},{10,9... | collective-permute-start | bytes 1179656 | tf_op jit(solution)/shard_map/ppermute | solution.py:51
  115.7 7.4 %collective-permute-done.15 = bf16[192,1024]{1,0:T(8,128)(2,1)S(1)} collective-permute-done((bf16[192,1024]{1,0:T(8,128)(2,1)S(1)}, bf16[192,1024]{1,0:T(8,128)(2,1)S(1)}, u32[]{:S(2)}, u32[]{:S(2)}) %collective-permute-start.15) | collective-permute-done | bytes 393248 | tf_op jit(solution)/shard_map/ppermute | solution.py:51
  123.3 4.2 %collective-permute-done.13 = bf16[192,1024]{1,0:T(8,128)(2,1)S(1)} collective-permute-done((bf16[192,1024]{1,0:T(8,128)(2,1)S(1)}, bf16[192,1024]{1,0:T(8,128)(2,1)S(1)}, u32[]{:S(2)}, u32[]{:S(2)}) %collective-permute-start.13) | collective-permute-done | bytes 393248 | tf_op jit(solution)/shard_map/ppermute | solution.py:51
  131.7 9.9 %all-to-all-start.2 = ((f32[16,3,384]{2,1,0:T(4,128)}), f32[16,3,384]{2,1,0:T(4,128)S(1)}, u32[]{:S(2)}, u32[]{:S(2)}) async-start(f32[16,3,384]{2,1,0:T(4,128)} %gather_fusion), calls=%async_computation.2 | async-start | bytes 196608 | tf_op jit(solution)/shard_map/all_to_all | solution.py:104
  142.5 12.2 %all-to-all-done.2 = f32[16,3,384]{2,1,0:T(4,128)S(1)} async-done(((f32[16,3,384]{2,1,0:T(4,128)}), f32[16,3,384]{2,1,0:T(4,128)S(1)}, u32[]{:S(2)}, u32[]{:S(2)}) %all-to-all-start.2) | async-done | bytes 73760 | tf_op jit(solution)/shard_map/all_to_all | solution.py:104
  154.8 3.2 %multiply_add_fusion = f32[384]{0:T(512)S(1)} fusion(f32[384]{0:T(512)S(1)} %get-tuple-element.26, f32[384]{0:T(512)S(1)} %get-tuple-element.43, f32[384]{0:T(512)S(1)} %get-tuple-element.47, f32[384]{0:T(512)S(1)} %get-tuple-element.49, f32[384]{0:T(512)S(1)} %multiply_reduce_fusion.16, f32[384]{0:T(512)S(1)} %fusion.19, f32[]{:T(128)} %bitcast.17, ...), kind=kLoop, calls=%fused_computation.136 | loop fusion | flops 3840 | bytes 10772 | tf_op jit(solution)/shard_map/add | solution.py:110
  158.0 2.9 %scatter_custom_fusion.1 = f32[384]{0:T(512)S(1)} fusion(s32[384]{0:T(512)S(1)} %fusion.25, f32[384]{0:T(512)S(1)} %multiply_add_fusion, f32[]{:T(128)} %constant.131.clone.1), kind=kCustom, calls=%fused_computation.144 | custom fusion | bytes 1540 | tf_op jit(solution)/shard_map/scatter | solution.py:118
  (132 shorter events, 30.6 us)
Async XLA Ops:
  0.0 6.0 %copy-start = (bf16[288,1024]{1,0:T(8,128)(2,1)S(1)}, bf16[288,1024]{1,0:T(8,128)(2,1)}, u32[]{:S(2)}) copy-start(bf16[288,1024]{1,0:T(8,128)(2,1)} %param.7) | copy-start | bytes 1769476
  9.7 9.6 %copy-start.2 = (s32[16,3]{1,0:T(8,128)S(1)}, s32[16,3]{1,0:T(8,128)}, u32[]{:S(2)}) copy-start(s32[16,3]{1,0:T(8,128)} %constant.154.clone) | copy-start | bytes 580
  9.7 10.4 %copy-start.3 = (s32[16]{0:T(128)S(1)}, s32[16]{0:T(128)}, u32[]{:S(2)}) copy-start(s32[16]{0:T(128)} %param.9) | copy-start | bytes 196
  9.7 25.1 %copy-start.1 = (f32[16,3]{1,0:T(8,128)S(1)}, f32[16,3]{1,0:T(8,128)}, u32[]{:S(2)}) copy-start(f32[16,3]{1,0:T(8,128)} %constant.155.clone) | copy-start | bytes 580
  9.7 19.0 %all-to-all-start = ((bf16[32,6,1024]{2,1,0:T(8,128)(2,1)}), bf16[32,6,1024]{2,1,0:T(8,128)(2,1)S(1)}, u32[]{:S(2)}, u32[]{:S(2)}) async-start(bf16[32,6,1024]{2,1,0:T(8,128)(2,1)} %get-tuple-element.52), calls=%async_computation | async-start | bytes 1048576 | tf_op jit(solution)/shard_map/all_to_all | solution.py:43
  28.7 19.9 %all-to-all-start.1 = ((bf16[32,6,1024]{2,1,0:T(8,128)(2,1)}), bf16[32,6,1024]{2,1,0:T(8,128)(2,1)S(1)}, u32[]{:S(2)}, u32[]{:S(2)}) async-start(bf16[32,6,1024]{2,1,0:T(8,128)(2,1)} %get-tuple-element.51), calls=%async_computation.1 | async-start | bytes 1048576 | tf_op jit(solution)/shard_map/all_to_all | solution.py:43
  37.2 19.6 %collective-permute-start.6 = (bf16[192,1024]{1,0:T(8,128)(2,1)S(1)}, bf16[192,1024]{1,0:T(8,128)(2,1)}, u32[]{:S(2)}, u32[]{:S(2)}) collective-permute-start(bf16[192,1024]{1,0:T(8,128)(2,1)S(1)} %reshape.382), channel_id=1, source_target_pairs={{0,1},{1,2},{2,3},{3,4},{4,5},{5,6},{6,7},{7,8},{8,9},{9,10},{10,1... | collective-permute-start | bytes 1179656 | tf_op jit(solution)/shard_map/ppermute | solution.py:51
  39.1 19.6 %collective-permute-start = (bf16[192,1024]{1,0:T(8,128)(2,1)S(1)}, bf16[192,1024]{1,0:T(8,128)(2,1)S(1)}, u32[]{:S(2)}, u32[]{:S(2)}) collective-permute-start(bf16[192,1024]{1,0:T(8,128)(2,1)S(1)} %reshape.382), channel_id=1, source_target_pairs={{0,15},{1,0},{2,1},{3,2},{4,3},{5,4},{6,5},{7,6},{8,7},{9,8},{10,9... | collective-permute-start | bytes 1179656 | tf_op jit(solution)/shard_map/ppermute | solution.py:51
  48.8 16.1 %collective-permute-start.8 = (bf16[192,1024]{1,0:T(8,128)(2,1)S(1)}, bf16[192,1024]{1,0:T(8,128)(2,1)S(1)}, u32[]{:S(2)}, u32[]{:S(2)}) collective-permute-start(bf16[192,1024]{1,0:T(8,128)(2,1)S(1)} %reshape.383), channel_id=1, source_target_pairs={{0,1},{1,2},{2,3},{3,4},{4,5},{5,6},{6,7},{7,8},{8,9},{9,10},{10,1... | collective-permute-start | bytes 1179656 | tf_op jit(solution)/shard_map/ppermute | solution.py:51
  50.7 16.2 %collective-permute-start.1 = (bf16[192,1024]{1,0:T(8,128)(2,1)S(1)}, bf16[192,1024]{1,0:T(8,128)(2,1)S(1)}, u32[]{:S(2)}, u32[]{:S(2)}) collective-permute-start(bf16[192,1024]{1,0:T(8,128)(2,1)S(1)} %reshape.383), channel_id=1, source_target_pairs={{0,15},{1,0},{2,1},{3,2},{4,3},{5,4},{6,5},{7,6},{8,7},{9,8},{10,9... | collective-permute-start | bytes 1179656 | tf_op jit(solution)/shard_map/ppermute | solution.py:51
  56.8 23.4 %collective-permute-start.7 = (bf16[192,1024]{1,0:T(8,128)(2,1)}, bf16[192,1024]{1,0:T(8,128)(2,1)S(1)}, u32[]{:S(2)}, u32[]{:S(2)}) collective-permute-start(bf16[192,1024]{1,0:T(8,128)(2,1)} %collective-permute-done.6), channel_id=1, source_target_pairs={{0,1},{1,2},{2,3},{3,4},{4,5},{5,6},{6,7},{7,8},{8,9},{9,10},{10,1... | collective-permute-start | bytes 1179656 | tf_op jit(solution)/shard_map/ppermute | solution.py:51
  58.7 15.8 %collective-permute-start.2 = (bf16[192,1024]{1,0:T(8,128)(2,1)S(1)}, bf16[192,1024]{1,0:T(8,128)(2,1)S(1)}, u32[]{:S(2)}, u32[]{:S(2)}) collective-permute-start(bf16[192,1024]{1,0:T(8,128)(2,1)S(1)} %collective-permute-done), channel_id=1, source_target_pairs={{0,15},{1,0},{2,1},{3,2},{4,3},{5,4},{6,5},{7,6},{8,7},{9,8},{10,9... | collective-permute-start | bytes 1179656 | tf_op jit(solution)/shard_map/ppermute | solution.py:51
  64.9 23.8 %collective-permute-start.9 = (bf16[192,1024]{1,0:T(8,128)(2,1)S(1)}, bf16[192,1024]{1,0:T(8,128)(2,1)S(1)}, u32[]{:S(2)}, u32[]{:S(2)}) collective-permute-start(bf16[192,1024]{1,0:T(8,128)(2,1)S(1)} %collective-permute-done.8), channel_id=1, source_target_pairs={{0,1},{1,2},{2,3},{3,4},{4,5},{5,6},{6,7},{7,8},{8,9},{9,10},{10,1... | collective-permute-start | bytes 1179656 | tf_op jit(solution)/shard_map/ppermute | solution.py:51
  66.9 16.1 %collective-permute-start.3 = (bf16[192,1024]{1,0:T(8,128)(2,1)S(1)}, bf16[192,1024]{1,0:T(8,128)(2,1)S(1)}, u32[]{:S(2)}, u32[]{:S(2)}) collective-permute-start(bf16[192,1024]{1,0:T(8,128)(2,1)S(1)} %collective-permute-done.1), channel_id=1, source_target_pairs={{0,15},{1,0},{2,1},{3,2},{4,3},{5,4},{6,5},{7,6},{8,7},{9,8},{10,9... | collective-permute-start | bytes 1179656 | tf_op jit(solution)/shard_map/ppermute | solution.py:51
  74.5 16.9 %collective-permute-start.4 = (bf16[192,1024]{1,0:T(8,128)(2,1)S(1)}, bf16[192,1024]{1,0:T(8,128)(2,1)S(1)}, u32[]{:S(2)}, u32[]{:S(2)}) collective-permute-start(bf16[192,1024]{1,0:T(8,128)(2,1)S(1)} %collective-permute-done.2), channel_id=1, source_target_pairs={{0,15},{1,0},{2,1},{3,2},{4,3},{5,4},{6,5},{7,6},{8,7},{9,8},{10,9... | collective-permute-start | bytes 1179656 | tf_op jit(solution)/shard_map/ppermute | solution.py:51
  80.2 19.9 %collective-permute-start.10 = (bf16[192,1024]{1,0:T(8,128)(2,1)S(1)}, bf16[192,1024]{1,0:T(8,128)(2,1)S(1)}, u32[]{:S(2)}, u32[]{:S(2)}) collective-permute-start(bf16[192,1024]{1,0:T(8,128)(2,1)S(1)} %collective-permute-done.7), channel_id=1, source_target_pairs={{0,1},{1,2},{2,3},{3,4},{4,5},{5,6},{6,7},{7,8},{8,9},{9,10},{10,1... | collective-permute-start | bytes 1179656 | tf_op jit(solution)/shard_map/ppermute | solution.py:51
  83.0 16.4 %collective-permute-start.5 = (bf16[192,1024]{1,0:T(8,128)(2,1)S(1)}, bf16[192,1024]{1,0:T(8,128)(2,1)S(1)}, u32[]{:S(2)}, u32[]{:S(2)}) collective-permute-start(bf16[192,1024]{1,0:T(8,128)(2,1)S(1)} %collective-permute-done.3), channel_id=1, source_target_pairs={{0,15},{1,0},{2,1},{3,2},{4,3},{5,4},{6,5},{7,6},{8,7},{9,8},{10,9... | collective-permute-start | bytes 1179656 | tf_op jit(solution)/shard_map/ppermute | solution.py:51
  88.8 13.9 %collective-permute-start.11 = (bf16[192,1024]{1,0:T(8,128)(2,1)S(1)}, bf16[192,1024]{1,0:T(8,128)(2,1)S(1)}, u32[]{:S(2)}, u32[]{:S(2)}) collective-permute-start(bf16[192,1024]{1,0:T(8,128)(2,1)S(1)} %collective-permute-done.9), channel_id=1, source_target_pairs={{0,1},{1,2},{2,3},{3,4},{4,5},{5,6},{6,7},{7,8},{8,9},{9,10},{10,1... | collective-permute-start | bytes 1179656 | tf_op jit(solution)/shard_map/ppermute | solution.py:51
  100.1 15.6 %collective-permute-start.14 = (bf16[192,1024]{1,0:T(8,128)(2,1)S(1)}, bf16[192,1024]{1,0:T(8,128)(2,1)S(1)}, u32[]{:S(2)}, u32[]{:S(2)}) collective-permute-start(bf16[192,1024]{1,0:T(8,128)(2,1)S(1)} %collective-permute-done.10), channel_id=1, source_target_pairs={{0,1},{1,2},{2,3},{3,4},{4,5},{5,6},{6,7},{7,8},{8,9},{9,10},{10,1... | collective-permute-start | bytes 1179656 | tf_op jit(solution)/shard_map/ppermute | solution.py:51
  102.7 20.4 %collective-permute-start.15 = (bf16[192,1024]{1,0:T(8,128)(2,1)S(1)}, bf16[192,1024]{1,0:T(8,128)(2,1)S(1)}, u32[]{:S(2)}, u32[]{:S(2)}) collective-permute-start(bf16[192,1024]{1,0:T(8,128)(2,1)S(1)} %collective-permute-done.11), channel_id=1, source_target_pairs={{0,1},{1,2},{2,3},{3,4},{4,5},{5,6},{6,7},{7,8},{8,9},{9,10},{10,1... | collective-permute-start | bytes 1179656 | tf_op jit(solution)/shard_map/ppermute | solution.py:51
  105.2 18.0 %collective-permute-start.12 = (bf16[192,1024]{1,0:T(8,128)(2,1)S(1)}, bf16[192,1024]{1,0:T(8,128)(2,1)S(1)}, u32[]{:S(2)}, u32[]{:S(2)}) collective-permute-start(bf16[192,1024]{1,0:T(8,128)(2,1)S(1)} %collective-permute-done.4), channel_id=1, source_target_pairs={{0,15},{1,0},{2,1},{3,2},{4,3},{5,4},{6,5},{7,6},{8,7},{9,8},{10,9... | collective-permute-start | bytes 1179656 | tf_op jit(solution)/shard_map/ppermute | solution.py:51
  111.1 16.4 %collective-permute-start.13 = (bf16[192,1024]{1,0:T(8,128)(2,1)S(1)}, bf16[192,1024]{1,0:T(8,128)(2,1)S(1)}, u32[]{:S(2)}, u32[]{:S(2)}) collective-permute-start(bf16[192,1024]{1,0:T(8,128)(2,1)S(1)} %collective-permute-done.5), channel_id=1, source_target_pairs={{0,15},{1,0},{2,1},{3,2},{4,3},{5,4},{6,5},{7,6},{8,7},{9,8},{10,9... | collective-permute-start | bytes 1179656 | tf_op jit(solution)/shard_map/ppermute | solution.py:51
  131.7 23.0 %all-to-all-start.2 = ((f32[16,3,384]{2,1,0:T(4,128)}), f32[16,3,384]{2,1,0:T(4,128)S(1)}, u32[]{:S(2)}, u32[]{:S(2)}) async-start(f32[16,3,384]{2,1,0:T(4,128)} %gather_fusion), calls=%async_computation.2 | async-start | bytes 196608 | tf_op jit(solution)/shard_map/all_to_all | solution.py:104

commit v5 on v4

--- a/solution.py
+++ b/solution.py
@@ -87,25 +87,22 @@
         add(p, q, to_p)
         add(q, p, to_q)
 
-    depth = max(len(items) for t, items in outgoing_sums.items() if t != 0)
-    zero = jnp.zeros((BLK,), jnp.float32)
-    table = [[zero] * depth for _ in range(grp_count)]
-    source_table = [[0] * depth for _ in range(grp_count)]
-    present_table = [[0.0] * depth for _ in range(grp_count)]
-    for target, items in outgoing_sums.items():
+    packed = []
+    target_table = []
+    source_table = []
+    for target, items in sorted(outgoing_sums.items()):
         if target == 0:
             continue
-        for k, (source, sums) in enumerate(items):
-            table[target % grp_count][k] = sums
-            source_table[target % grp_count][k] = source - target
-            present_table[target % grp_count][k] = 1.0
-    by_offset = jnp.stack([jnp.stack(row) for row in table])
-    by_device = by_offset[(blocks_iota - me) % grp_count]
-    arrived_sums = lax.all_to_all(by_device, "grp", split_axis=0, concat_axis=0, tiled=True)
+        for source, sums in items:
+            packed.append(sums)
+            target_table.append(target % grp_count)
+            source_table.append(source - target)
+    gathered = lax.all_gather(jnp.stack(packed), "grp", axis=0, tiled=False)
     offset_of_sender = (me - blocks_iota) % grp_count
-    sources = (me + jnp.array(source_table, jnp.int32)[offset_of_sender]) % grp_count
-    weights = member[sources] * jnp.array(present_table, jnp.float32)[offset_of_sender]
-    slot_sums = jnp.sum(arrived_sums * weights[:, :, None], axis=(0, 1))
+    meant = offset_of_sender[:, None] == jnp.array(target_table, jnp.int32)[None, :]
+    sources = (me + jnp.array(source_table, jnp.int32)) % grp_count
+    weights = jnp.where(meant, member[sources][None, :], 0.0)
+    slot_sums = jnp.sum(gathered * weights[:, :, None], axis=(0, 1))
     for source, sums in outgoing_sums[0]:
         slot_sums = slot_sums + sums * member[(me + source) % grp_count]
 
@@ -115,7 +112,8 @@
     within = jnp.arange(capacity, dtype=jnp.int32)
     places = jnp.where(own_valid > 0, offsets[:, None] + within[None, :], BLK)
     places = places.reshape(wide_count, 2, split).transpose(1, 0, 2).reshape(-1)
-    density = jnp.zeros((BLK,), jnp.float32).at[places].set(slot_sums, mode="drop")
+    rows_iota = jnp.arange(BLK, dtype=jnp.int32)
+    density = jnp.sum(jnp.where(places[:, None] == rows_iota[None, :], slot_sums[:, None], 0.0), axis=0)
     return density.reshape(1, BLK)
 
 

time: 163 us -> 165 us (1.012)
  blocking collectives: 0 us -> 30.1 us
  waiting for transfers between devices: 44.2 us -> 30.9 us
  starting transfers between devices: 86.6 us -> 77.8 us
  local copies, waits for them, and re-layouts: 10.6 us -> 4.81 us
    all_gather x0 -> x1, blocking collectives: none -> 30.1 us  [per_device(): gathered = lax.all_gather(jnp.stack(packed), 'grp', axis=0, tiled=False)]
    all_to_all x1 -> x0, waiting for transfers between devices: 12.2 us -> none  [per_device(): lax.all_to_all(by_device, 'grp', split_axis=0, concat_axis=0, tiled=True)]
    all_to_all x1 -> x0, starting transfers between devices: 9.92 us -> none  [per_device(): lax.all_to_all(by_device, 'grp', split_axis=0, concat_axis=0, tiled=True)]
    scatter x1 -> x0, local copies, waits for them, and re-layouts: 2.91 us -> none  [per_device(): jnp.zeros((BLK,), jnp.float32).at[places].set(slot_sums, mode='drop')]
    gather x5 -> x1, local copies, waits for them, and re-layouts: 3.21 us -> 0.66 us  [per_device(): weights = jnp.where(meant, member[sources][None, :], 0.0)]
    ppermute x16, waiting for transfers between devices: 23.6 us -> 21.6 us  [shift(): lax.ppermute(value, 'grp', [(i, (i + offset) % grp_count) for i in range(...]
  transfers between devices with their start and end apart: 19 -> 18, of which waited for: 9 -> 9; matrix products, arithmetic and copies ran while one was open for 6% -> 5% of each run, Pallas kernels for 0% -> 0%
where the time goes in v5:
time: 165 us; the launch traced here: 164 us
  starting transfers between devices  77.8 us (47%)
  waiting for transfers between devices  30.9 us (19%)
  blocking collectives  30.1 us (18%)
  other arithmetic  12.2 us (7%)
  matrix products  6.3 us (4%)
  local copies, waits for them, and re-layouts  4.81 us (3%)
    ppermute x16, starting transfers between devices, shift(): lax.ppermute(value, 'grp', [(i, (i + offset) % grp_count) for i in range(...  62.2 us
    all_gather x1, blocking collectives, per_device(): gathered = lax.all_gather(jnp.stack(packed), 'grp', axis=0, tiled=False)  30.1 us
    ppermute x16, waiting for transfers between devices, shift(): lax.ppermute(value, 'grp', [(i, (i + offset) % grp_count) for i in range(...  21.6 us
    all_to_all x2, starting transfers between devices, per_device(): lax.all_to_all(h, 'wide', split_axis=0, concat_axis=0, tiled=True)  15.6 us
    all_to_all x2, waiting for transfers between devices, per_device(): lax.all_to_all(h, 'wide', split_axis=0, concat_axis=0, tiled=True)  9.26 us
    dot_general x9, matrix products, pair_products(): lax.dot_general(left_rows, right_rows, (((1,), (1,)), ((), ())), preferre...  6.3 us
  transfers between devices with their start and end apart: 18, of which 9 were waited for; matrix products, arithmetic and copies ran while one was open for 5% of the time, Pallas kernels for 0%

profile of v5, /device:TPU:6, one launch (start us, length us, event | category | flops | bytes accessed | tf_op | source)
XLA Modules:
  0.0 163.6 jit_solution(8067110122791817097)
XLA Ops:
  6.0 2.3 %scatter_custom_fusion = bf16[384,1024]{1,0:T(8,128)(2,1)S(1)} fusion(bf16[384,1024]{1,0:T(8,128)(2,1)S(1)} %scatter.15, s32[288]{0:T(512)S(1)} %compare_select_fusion.1, bf16[288,1024]{1,0:T(8,128)(2,1)S(1)} %copy-done, f32[288]{0:T(512)S(1)} %add_rsqrt_fusion), kind=kCustom, calls=%fused_computation.35 | custom fusion | flops 884736 | bytes 1378304 | tf_op jit(solution)/shard_map/scatter | solution.py:39
  9.7 9.5 %all-to-all-start = ((bf16[32,6,1024]{2,1,0:T(8,128)(2,1)}), bf16[32,6,1024]{2,1,0:T(8,128)(2,1)S(1)}, u32[]{:S(2)}, u32[]{:S(2)}) async-start(bf16[32,6,1024]{2,1,0:T(8,128)(2,1)} %get-tuple-element.42), calls=%async_computation | async-start | bytes 1048576 | tf_op jit(solution)/shard_map/all_to_all | solution.py:43
  19.4 9.3 %all-to-all-done = bf16[32,6,1024]{2,1,0:T(8,128)(2,1)S(1)} async-done(((bf16[32,6,1024]{2,1,0:T(8,128)(2,1)}), bf16[32,6,1024]{2,1,0:T(8,128)(2,1)S(1)}, u32[]{:S(2)}, u32[]{:S(2)}) %all-to-all-start) | async-done | bytes 393248 | tf_op jit(solution)/shard_map/all_to_all | solution.py:43
  28.7 6.1 %all-to-all-start.1 = ((bf16[32,6,1024]{2,1,0:T(8,128)(2,1)}), bf16[32,6,1024]{2,1,0:T(8,128)(2,1)S(1)}, u32[]{:S(2)}, u32[]{:S(2)}) async-start(bf16[32,6,1024]{2,1,0:T(8,128)(2,1)} %get-tuple-element.41), calls=%async_computation.1 | async-start | bytes 1048576 | tf_op jit(solution)/shard_map/all_to_all | solution.py:43
  38.4 9.5 %collective-permute-start.8 = (bf16[192,1024]{1,0:T(8,128)(2,1)S(1)}, bf16[192,1024]{1,0:T(8,128)(2,1)S(1)}, u32[]{:S(2)}, u32[]{:S(2)}) collective-permute-start(bf16[192,1024]{1,0:T(8,128)(2,1)S(1)} %reshape.270), channel_id=1, source_target_pairs={{0,15},{1,0},{2,1},{3,2},{4,3},{5,4},{6,5},{7,6},{8,7},{9,8},{10,9... | collective-permute-start | bytes 1179656 | tf_op jit(solution)/shard_map/ppermute | solution.py:51
  48.0 1.9 %collective-permute-start.4 = (bf16[192,1024]{1,0:T(8,128)(2,1)S(1)}, bf16[192,1024]{1,0:T(8,128)(2,1)S(1)}, u32[]{:S(2)}, u32[]{:S(2)}) collective-permute-start(bf16[192,1024]{1,0:T(8,128)(2,1)S(1)} %reshape.271), channel_id=1, source_target_pairs={{0,1},{1,2},{2,3},{3,4},{4,5},{5,6},{6,7},{7,8},{8,9},{9,10},{10,1... | collective-permute-start | bytes 1179656 | tf_op jit(solution)/shard_map/ppermute | solution.py:51
  49.9 5.8 %collective-permute-start.12 = (bf16[192,1024]{1,0:T(8,128)(2,1)S(1)}, bf16[192,1024]{1,0:T(8,128)(2,1)S(1)}, u32[]{:S(2)}, u32[]{:S(2)}) collective-permute-start(bf16[192,1024]{1,0:T(8,128)(2,1)S(1)} %reshape.271), channel_id=1, source_target_pairs={{0,15},{1,0},{2,1},{3,2},{4,3},{5,4},{6,5},{7,6},{8,7},{9,8},{10,9... | collective-permute-start | bytes 1179656 | tf_op jit(solution)/shard_map/ppermute | solution.py:51
  59.4 4.1 %collective-permute-done.4 = bf16[192,1024]{1,0:T(8,128)(2,1)S(1)} collective-permute-done((bf16[192,1024]{1,0:T(8,128)(2,1)S(1)}, bf16[192,1024]{1,0:T(8,128)(2,1)S(1)}, u32[]{:S(2)}, u32[]{:S(2)}) %collective-permute-start.4) | collective-permute-done | bytes 393248 | tf_op jit(solution)/shard_map/ppermute | solution.py:51
  65.4 5.1 %collective-permute-start.9 = (bf16[192,1024]{1,0:T(8,128)(2,1)S(1)}, bf16[192,1024]{1,0:T(8,128)(2,1)S(1)}, u32[]{:S(2)}, u32[]{:S(2)}) collective-permute-start(bf16[192,1024]{1,0:T(8,128)(2,1)S(1)} %collective-permute-done.8), channel_id=1, source_target_pairs={{0,15},{1,0},{2,1},{3,2},{4,3},{5,4},{6,5},{7,6},{8,7},{9,8},{10,9... | collective-permute-start | bytes 1179656 | tf_op jit(solution)/shard_map/ppermute | solution.py:51
  70.5 3.0 %collective-permute-start.13 = (bf16[192,1024]{1,0:T(8,128)(2,1)S(1)}, bf16[192,1024]{1,0:T(8,128)(2,1)S(1)}, u32[]{:S(2)}, u32[]{:S(2)}) collective-permute-start(bf16[192,1024]{1,0:T(8,128)(2,1)S(1)} %collective-permute-done.12), channel_id=1, source_target_pairs={{0,15},{1,0},{2,1},{3,2},{4,3},{5,4},{6,5},{7,6},{8,7},{9,8},{10,9... | collective-permute-start | bytes 1179656 | tf_op jit(solution)/shard_map/ppermute | solution.py:51
  74.4 2.8 %collective-permute-start.2 = (bf16[192,1024]{1,0:T(8,128)(2,1)S(1)}, bf16[192,1024]{1,0:T(8,128)(2,1)S(1)}, u32[]{:S(2)}, u32[]{:S(2)}) collective-permute-start(bf16[192,1024]{1,0:T(8,128)(2,1)S(1)} %collective-permute-done.1), channel_id=1, source_target_pairs={{0,1},{1,2},{2,3},{3,4},{4,5},{5,6},{6,7},{7,8},{8,9},{9,10},{10,1... | collective-permute-start | bytes 1179656 | tf_op jit(solution)/shard_map/ppermute | solution.py:51
  77.2 2.8 %collective-permute-done.9 = bf16[192,1024]{1,0:T(8,128)(2,1)S(1)} collective-permute-done((bf16[192,1024]{1,0:T(8,128)(2,1)S(1)}, bf16[192,1024]{1,0:T(8,128)(2,1)S(1)}, u32[]{:S(2)}, u32[]{:S(2)}) %collective-permute-start.9) | collective-permute-done | bytes 393248 | tf_op jit(solution)/shard_map/ppermute | solution.py:51
  80.0 5.6 %collective-permute-start.10 = (bf16[192,1024]{1,0:T(8,128)(2,1)S(1)}, bf16[192,1024]{1,0:T(8,128)(2,1)S(1)}, u32[]{:S(2)}, u32[]{:S(2)}) collective-permute-start(bf16[192,1024]{1,0:T(8,128)(2,1)S(1)} %collective-permute-done.9), channel_id=1, source_target_pairs={{0,15},{1,0},{2,1},{3,2},{4,3},{5,4},{6,5},{7,6},{8,7},{9,8},{10,9... | collective-permute-start | bytes 1179656 | tf_op jit(solution)/shard_map/ppermute | solution.py:51
  88.4 5.6 %collective-permute-start.14 = (bf16[192,1024]{1,0:T(8,128)(2,1)S(1)}, bf16[192,1024]{1,0:T(8,128)(2,1)S(1)}, u32[]{:S(2)}, u32[]{:S(2)}) collective-permute-start(bf16[192,1024]{1,0:T(8,128)(2,1)S(1)} %collective-permute-done.13), channel_id=1, source_target_pairs={{0,15},{1,0},{2,1},{3,2},{4,3},{5,4},{6,5},{7,6},{8,7},{9,8},{10,9... | collective-permute-start | bytes 1179656 | tf_op jit(solution)/shard_map/ppermute | solution.py:51
  94.8 2.0 %collective-permute-done.10 = bf16[192,1024]{1,0:T(8,128)(2,1)S(1)} collective-permute-done((bf16[192,1024]{1,0:T(8,128)(2,1)S(1)}, bf16[192,1024]{1,0:T(8,128)(2,1)S(1)}, u32[]{:S(2)}, u32[]{:S(2)}) %collective-permute-start.10) | collective-permute-done | bytes 393248 | tf_op jit(solution)/shard_map/ppermute | solution.py:51
  96.8 5.6 %collective-permute-start.11 = (bf16[192,1024]{1,0:T(8,128)(2,1)S(1)}, bf16[192,1024]{1,0:T(8,128)(2,1)S(1)}, u32[]{:S(2)}, u32[]{:S(2)}) collective-permute-start(bf16[192,1024]{1,0:T(8,128)(2,1)S(1)} %collective-permute-done.10), channel_id=1, source_target_pairs={{0,15},{1,0},{2,1},{3,2},{4,3},{5,4},{6,5},{7,6},{8,7},{9,8},{10,9... | collective-permute-start | bytes 1179656 | tf_op jit(solution)/shard_map/ppermute | solution.py:51
  102.5 2.8 %collective-permute-done.14 = bf16[192,1024]{1,0:T(8,128)(2,1)S(1)} collective-permute-done((bf16[192,1024]{1,0:T(8,128)(2,1)S(1)}, bf16[192,1024]{1,0:T(8,128)(2,1)S(1)}, u32[]{:S(2)}, u32[]{:S(2)}) %collective-permute-start.14) | collective-permute-done | bytes 393248 | tf_op jit(solution)/shard_map/ppermute | solution.py:51
  109.2 5.6 %collective-permute-start.15 = (bf16[192,1024]{1,0:T(8,128)(2,1)S(1)}, bf16[192,1024]{1,0:T(8,128)(2,1)S(1)}, u32[]{:S(2)}, u32[]{:S(2)}) collective-permute-start(bf16[192,1024]{1,0:T(8,128)(2,1)S(1)} %collective-permute-done.14), channel_id=1, source_target_pairs={{0,15},{1,0},{2,1},{3,2},{4,3},{5,4},{6,5},{7,6},{8,7},{9,8},{10,9... | collective-permute-start | bytes 1179656 | tf_op jit(solution)/shard_map/ppermute | solution.py:51
  114.9 2.1 %collective-permute-start.7 = (bf16[192,1024]{1,0:T(8,128)(2,1)S(1)}, bf16[192,1024]{1,0:T(8,128)(2,1)S(1)}, u32[]{:S(2)}, u32[]{:S(2)}) collective-permute-start(bf16[192,1024]{1,0:T(8,128)(2,1)S(1)} %collective-permute-done.6), channel_id=1, source_target_pairs={{0,1},{1,2},{2,3},{3,4},{4,5},{5,6},{6,7},{7,8},{8,9},{9,10},{10,1... | collective-permute-start | bytes 1179656 | tf_op jit(solution)/shard_map/ppermute | solution.py:51
  117.1 2.1 %collective-permute-done.3 = bf16[192,1024]{1,0:T(8,128)(2,1)S(1)} collective-permute-done((bf16[192,1024]{1,0:T(8,128)(2,1)S(1)}, bf16[192,1024]{1,0:T(8,128)(2,1)S(1)}, u32[]{:S(2)}, u32[]{:S(2)}) %collective-permute-start.3) | collective-permute-done | bytes 393248 | tf_op jit(solution)/shard_map/ppermute | solution.py:51
  119.2 2.0 %collective-permute-done.15 = bf16[192,1024]{1,0:T(8,128)(2,1)S(1)} collective-permute-done((bf16[192,1024]{1,0:T(8,128)(2,1)S(1)}, bf16[192,1024]{1,0:T(8,128)(2,1)S(1)}, u32[]{:S(2)}, u32[]{:S(2)}) %collective-permute-start.15) | collective-permute-done | bytes 393248 | tf_op jit(solution)/shard_map/ppermute | solution.py:51
  122.0 5.2 %collective-permute-done.7 = bf16[192,1024]{1,0:T(8,128)(2,1)S(1)} collective-permute-done((bf16[192,1024]{1,0:T(8,128)(2,1)S(1)}, bf16[192,1024]{1,0:T(8,128)(2,1)S(1)}, u32[]{:S(2)}, u32[]{:S(2)}) %collective-permute-start.7) | collective-permute-done | bytes 393248 | tf_op jit(solution)/shard_map/ppermute | solution.py:51
  129.4 30.1 %all-gather.1 = f32[16,12,384]{2,1,0:T(8,128)S(1)} all-gather(f32[1,12,384]{2,1,0:T(8,128)S(1)} %bitcast.40), channel_id=2, replica_groups=mesh['wide'=32,'grp'=16] {'grp'}, dimensions={0}, use_global_device_ids=true | all-gather | bytes 313344 | tf_op jit(solution)/shard_map/all_gather | solution.py:100
  159.7 3.2 %multiply_add_fusion = f32[384]{0:T(512)S(1)} fusion(f32[384]{0:T(512)S(1)} %get-tuple-element.52, f32[384]{0:T(512)S(1)} %get-tuple-element.55, f32[384]{0:T(512)S(1)} %get-tuple-element.53, f32[384]{0:T(512)S(1)} %get-tuple-element.57, f32[384]{0:T(512)S(1)} %multiply_reduce_fusion.16, f32[384]{0:T(512)S(1)} %fusion.19, f32[]{:T(128)} %bitcast.8, ...), kind=kLoop, calls=%fused_computation.108 | loop fusion | flops 3840 | bytes 10772 | tf_op jit(solution)/shard_map/add | solution.py:107
  (109 shorter events, 28.2 us)
Async XLA Ops:
  0.0 6.0 %copy-start = (bf16[288,1024]{1,0:T(8,128)(2,1)S(1)}, bf16[288,1024]{1,0:T(8,128)(2,1)}, u32[]{:S(2)}) copy-start(bf16[288,1024]{1,0:T(8,128)(2,1)} %param.7) | copy-start | bytes 1769476
  9.7 9.6 %copy-start.3 = (s32[12]{0:T(128)S(1)}, s32[12]{0:T(128)}, u32[]{:S(2)}) copy-start(s32[12]{0:T(128)} %constant.140.clone) | copy-start | bytes 148
  9.7 9.6 %copy-start.2 = (s32[16]{0:T(128)S(1)}, s32[16]{0:T(128)}, u32[]{:S(2)}) copy-start(s32[16]{0:T(128)} %param.9) | copy-start | bytes 196
  9.7 19.0 %all-to-all-start = ((bf16[32,6,1024]{2,1,0:T(8,128)(2,1)}), bf16[32,6,1024]{2,1,0:T(8,128)(2,1)S(1)}, u32[]{:S(2)}, u32[]{:S(2)}) async-start(bf16[32,6,1024]{2,1,0:T(8,128)(2,1)} %get-tuple-element.42), calls=%async_computation | async-start | bytes 1048576 | tf_op jit(solution)/shard_map/all_to_all | solution.py:43
  19.3 16.9 %copy-start.1 = (s32[12]{0:T(128)S(1)}, s32[12]{0:T(128)}, u32[]{:S(2)}) copy-start(s32[12]{0:T(128)} %constant.139.clone) | copy-start | bytes 148
  28.7 19.2 %all-to-all-start.1 = ((bf16[32,6,1024]{2,1,0:T(8,128)(2,1)}), bf16[32,6,1024]{2,1,0:T(8,128)(2,1)S(1)}, u32[]{:S(2)}, u32[]{:S(2)}) async-start(bf16[32,6,1024]{2,1,0:T(8,128)(2,1)} %get-tuple-element.41), calls=%async_computation.1 | async-start | bytes 1048576 | tf_op jit(solution)/shard_map/all_to_all | solution.py:43
  36.4 21.0 %collective-permute-start = (bf16[192,1024]{1,0:T(8,128)(2,1)S(1)}, bf16[192,1024]{1,0:T(8,128)(2,1)S(1)}, u32[]{:S(2)}, u32[]{:S(2)}) collective-permute-start(bf16[192,1024]{1,0:T(8,128)(2,1)S(1)} %reshape.270), channel_id=1, source_target_pairs={{0,1},{1,2},{2,3},{3,4},{4,5},{5,6},{6,7},{7,8},{8,9},{9,10},{10,1... | collective-permute-start | bytes 1179656 | tf_op jit(solution)/shard_map/ppermute | solution.py:51
  38.4 27.0 %collective-permute-start.8 = (bf16[192,1024]{1,0:T(8,128)(2,1)S(1)}, bf16[192,1024]{1,0:T(8,128)(2,1)S(1)}, u32[]{:S(2)}, u32[]{:S(2)}) collective-permute-start(bf16[192,1024]{1,0:T(8,128)(2,1)S(1)} %reshape.270), channel_id=1, source_target_pairs={{0,15},{1,0},{2,1},{3,2},{4,3},{5,4},{6,5},{7,6},{8,7},{9,8},{10,9... | collective-permute-start | bytes 1179656 | tf_op jit(solution)/shard_map/ppermute | solution.py:51
  48.0 15.4 %collective-permute-start.4 = (bf16[192,1024]{1,0:T(8,128)(2,1)S(1)}, bf16[192,1024]{1,0:T(8,128)(2,1)S(1)}, u32[]{:S(2)}, u32[]{:S(2)}) collective-permute-start(bf16[192,1024]{1,0:T(8,128)(2,1)S(1)} %reshape.271), channel_id=1, source_target_pairs={{0,1},{1,2},{2,3},{3,4},{4,5},{5,6},{6,7},{7,8},{8,9},{9,10},{10,1... | collective-permute-start | bytes 1179656 | tf_op jit(solution)/shard_map/ppermute | solution.py:51
  49.9 20.6 %collective-permute-start.12 = (bf16[192,1024]{1,0:T(8,128)(2,1)S(1)}, bf16[192,1024]{1,0:T(8,128)(2,1)S(1)}, u32[]{:S(2)}, u32[]{:S(2)}) collective-permute-start(bf16[192,1024]{1,0:T(8,128)(2,1)S(1)} %reshape.271), channel_id=1, source_target_pairs={{0,15},{1,0},{2,1},{3,2},{4,3},{5,4},{6,5},{7,6},{8,7},{9,8},{10,9... | collective-permute-start | bytes 1179656 | tf_op jit(solution)/shard_map/ppermute | solution.py:51
  57.4 16.9 %collective-permute-start.1 = (bf16[192,1024]{1,0:T(8,128)(2,1)S(1)}, bf16[192,1024]{1,0:T(8,128)(2,1)S(1)}, u32[]{:S(2)}, u32[]{:S(2)}) collective-permute-start(bf16[192,1024]{1,0:T(8,128)(2,1)S(1)} %collective-permute-done), channel_id=1, source_target_pairs={{0,1},{1,2},{2,3},{3,4},{4,5},{5,6},{6,7},{7,8},{8,9},{9,10},{10,1... | collective-permute-start | bytes 1179656 | tf_op jit(solution)/shard_map/ppermute | solution.py:51
  63.4 22.2 %collective-permute-start.5 = (bf16[192,1024]{1,0:T(8,128)(2,1)S(1)}, bf16[192,1024]{1,0:T(8,128)(2,1)S(1)}, u32[]{:S(2)}, u32[]{:S(2)}) collective-permute-start(bf16[192,1024]{1,0:T(8,128)(2,1)S(1)} %collective-permute-done.4), channel_id=1, source_target_pairs={{0,1},{1,2},{2,3},{3,4},{4,5},{5,6},{6,7},{7,8},{8,9},{9,10},{10,1... | collective-permute-start | bytes 1179656 | tf_op jit(solution)/shard_map/ppermute | solution.py:51
  65.4 14.6 %collective-permute-start.9 = (bf16[192,1024]{1,0:T(8,128)(2,1)S(1)}, bf16[192,1024]{1,0:T(8,128)(2,1)S(1)}, u32[]{:S(2)}, u32[]{:S(2)}) collective-permute-start(bf16[192,1024]{1,0:T(8,128)(2,1)S(1)} %collective-permute-done.8), channel_id=1, source_target_pairs={{0,15},{1,0},{2,1},{3,2},{4,3},{5,4},{6,5},{7,6},{8,7},{9,8},{10,9... | collective-permute-start | bytes 1179656 | tf_op jit(solution)/shard_map/ppermute | solution.py:51
  70.5 17.9 %collective-permute-start.13 = (bf16[192,1024]{1,0:T(8,128)(2,1)S(1)}, bf16[192,1024]{1,0:T(8,128)(2,1)S(1)}, u32[]{:S(2)}, u32[]{:S(2)}) collective-permute-start(bf16[192,1024]{1,0:T(8,128)(2,1)S(1)} %collective-permute-done.12), channel_id=1, source_target_pairs={{0,15},{1,0},{2,1},{3,2},{4,3},{5,4},{6,5},{7,6},{8,7},{9,8},{10,9... | collective-permute-start | bytes 1179656 | tf_op jit(solution)/shard_map/ppermute | solution.py:51
  74.4 31.5 %collective-permute-start.2 = (bf16[192,1024]{1,0:T(8,128)(2,1)S(1)}, bf16[192,1024]{1,0:T(8,128)(2,1)S(1)}, u32[]{:S(2)}, u32[]{:S(2)}) collective-permute-start(bf16[192,1024]{1,0:T(8,128)(2,1)S(1)} %collective-permute-done.1), channel_id=1, source_target_pairs={{0,1},{1,2},{2,3},{3,4},{4,5},{5,6},{6,7},{7,8},{8,9},{9,10},{10,1... | collective-permute-start | bytes 1179656 | tf_op jit(solution)/shard_map/ppermute | solution.py:51
  80.0 16.9 %collective-permute-start.10 = (bf16[192,1024]{1,0:T(8,128)(2,1)S(1)}, bf16[192,1024]{1,0:T(8,128)(2,1)S(1)}, u32[]{:S(2)}, u32[]{:S(2)}) collective-permute-start(bf16[192,1024]{1,0:T(8,128)(2,1)S(1)} %collective-permute-done.9), channel_id=1, source_target_pairs={{0,15},{1,0},{2,1},{3,2},{4,3},{5,4},{6,5},{7,6},{8,7},{9,8},{10,9... | collective-permute-start | bytes 1179656 | tf_op jit(solution)/shard_map/ppermute | solution.py:51
  85.6 22.9 %collective-permute-start.6 = (bf16[192,1024]{1,0:T(8,128)(2,1)S(1)}, bf16[192,1024]{1,0:T(8,128)(2,1)S(1)}, u32[]{:S(2)}, u32[]{:S(2)}) collective-permute-start(bf16[192,1024]{1,0:T(8,128)(2,1)S(1)} %collective-permute-done.5), channel_id=1, source_target_pairs={{0,1},{1,2},{2,3},{3,4},{4,5},{5,6},{6,7},{7,8},{8,9},{9,10},{10,1... | collective-permute-start | bytes 1179656 | tf_op jit(solution)/shard_map/ppermute | solution.py:51
  88.4 16.9 %collective-permute-start.14 = (bf16[192,1024]{1,0:T(8,128)(2,1)S(1)}, bf16[192,1024]{1,0:T(8,128)(2,1)S(1)}, u32[]{:S(2)}, u32[]{:S(2)}) collective-permute-start(bf16[192,1024]{1,0:T(8,128)(2,1)S(1)} %collective-permute-done.13), channel_id=1, source_target_pairs={{0,15},{1,0},{2,1},{3,2},{4,3},{5,4},{6,5},{7,6},{8,7},{9,8},{10,9... | collective-permute-start | bytes 1179656 | tf_op jit(solution)/shard_map/ppermute | solution.py:51
  96.8 20.3 %collective-permute-start.11 = (bf16[192,1024]{1,0:T(8,128)(2,1)S(1)}, bf16[192,1024]{1,0:T(8,128)(2,1)S(1)}, u32[]{:S(2)}, u32[]{:S(2)}) collective-permute-start(bf16[192,1024]{1,0:T(8,128)(2,1)S(1)} %collective-permute-done.10), channel_id=1, source_target_pairs={{0,15},{1,0},{2,1},{3,2},{4,3},{5,4},{6,5},{7,6},{8,7},{9,8},{10,9... | collective-permute-start | bytes 1179656 | tf_op jit(solution)/shard_map/ppermute | solution.py:51
  105.9 13.3 %collective-permute-start.3 = (bf16[192,1024]{1,0:T(8,128)(2,1)S(1)}, bf16[192,1024]{1,0:T(8,128)(2,1)S(1)}, u32[]{:S(2)}, u32[]{:S(2)}) collective-permute-start(bf16[192,1024]{1,0:T(8,128)(2,1)S(1)} %collective-permute-done.2), channel_id=1, source_target_pairs={{0,1},{1,2},{2,3},{3,4},{4,5},{5,6},{6,7},{7,8},{8,9},{9,10},{10,1... | collective-permute-start | bytes 1179656 | tf_op jit(solution)/shard_map/ppermute | solution.py:51
  109.2 12.1 %collective-permute-start.15 = (bf16[192,1024]{1,0:T(8,128)(2,1)S(1)}, bf16[192,1024]{1,0:T(8,128)(2,1)S(1)}, u32[]{:S(2)}, u32[]{:S(2)}) collective-permute-start(bf16[192,1024]{1,0:T(8,128)(2,1)S(1)} %collective-permute-done.14), channel_id=1, source_target_pairs={{0,15},{1,0},{2,1},{3,2},{4,3},{5,4},{6,5},{7,6},{8,7},{9,8},{10,9... | collective-permute-start | bytes 1179656 | tf_op jit(solution)/shard_map/ppermute | solution.py:51
  114.9 12.3 %collective-permute-start.7 = (bf16[192,1024]{1,0:T(8,128)(2,1)S(1)}, bf16[192,1024]{1,0:T(8,128)(2,1)S(1)}, u32[]{:S(2)}, u32[]{:S(2)}) collective-permute-start(bf16[192,1024]{1,0:T(8,128)(2,1)S(1)} %collective-permute-done.6), channel_id=1, source_target_pairs={{0,1},{1,2},{2,3},{3,4},{4,5},{5,6},{6,7},{7,8},{8,9},{9,10},{10,1... | collective-permute-start | bytes 1179656 | tf_op jit(solution)/shard_map/ppermute | solution.py:51

commit v6 on v4

--- a/solution.py
+++ b/solution.py
@@ -2,6 +2,7 @@
 import jax.numpy as jnp
 from jax import lax
 from jax.sharding import PartitionSpec as P
+
 
 BLK = 384
 
@@ -63,36 +64,45 @@
             right = shift(right, -1)
             rows_at.setdefault(-step, []).append(left)
             rows_at.setdefault(step, []).append(right)
-    rows_at = {k: jnp.concatenate(v, axis=0) for k, v in rows_at.items()}
+    halves_at = rows_at
+    rows_at = {}
+    valid_at = {}
+    for k, v in halves_at.items():
+        rows_at[k] = jnp.concatenate(v, axis=0)
+        valid_at[k] = valid_of(rows_at[k])
     own = rows_at[0]
-    valid_at = {k: valid_of(v) for k, v in rows_at.items()}
 
-    outgoing_sums = {}
+    early = {}
+    late = {}
 
-    def add(target, source, sums):
-        outgoing_sums.setdefault(target, []).append((source, sums))
+    def add(sums_by_target, target, source, sums):
+        sums_by_target.setdefault(target, []).append((source, sums))
 
     e = pair_products(own, own)
-    add(0, 0, jnp.sum(e * valid_at[0][None, :], axis=1))
-    half = grp_count // 2
-    plan = [(0, 1), (0, 2), (0, 3), (0, 4), (-2, 3), (-3, 3), (-3, 4), (-4, 4)]
+    add(early, 0, 0, jnp.sum(e * valid_at[0][None, :], axis=1))
+    plan = [(0, 1), (0, 2), (0, 3), (-2, 2), (-2, 3), (-3, 3), (-4, 3)]
     for p, q in plan:
         e = pair_products(rows_at[p], rows_at[q])
         to_p = jnp.sum(e * valid_at[q][None, :], axis=1)
         to_q = jnp.sum(e * valid_at[p][:, None], axis=0)
-        if q - p == half:
-            keep = (me < half).astype(jnp.float32)
-            to_p = to_p * keep
-            to_q = to_q * keep
-        add(p, q, to_p)
-        add(q, p, to_q)
+        group = late if max(-p, q) == reach else early
+        add(group, p, q, to_p)
+        add(group, q, p, to_q)
+    e = pair_products(rows_at[-reach], rows_at[reach])
+    add(late, -reach, reach, jnp.sum(e * valid_at[reach][None, :], axis=1))
 
-    depth = max(len(items) for t, items in outgoing_sums.items() if t != 0)
+    def weighted(stacked, items, target):
+        sources = (me + jnp.array([s - target for s, _ in items], jnp.int32)) % grp_count
+        return jnp.sum(stacked * member[sources][:, None], axis=0)
+
+    slot_sums = weighted(jnp.stack([s for _, s in early[0]]), early[0], 0)
+
+    depth = max(len(items) for t, items in early.items() if t != 0)
     zero = jnp.zeros((BLK,), jnp.float32)
     table = [[zero] * depth for _ in range(grp_count)]
     source_table = [[0] * depth for _ in range(grp_count)]
     present_table = [[0.0] * depth for _ in range(grp_count)]
-    for target, items in outgoing_sums.items():
+    for target, items in early.items():
         if target == 0:
             continue
         for k, (source, sums) in enumerate(items):
@@ -105,9 +115,11 @@
     offset_of_sender = (me - blocks_iota) % grp_count
     sources = (me + jnp.array(source_table, jnp.int32)[offset_of_sender]) % grp_count
     weights = member[sources] * jnp.array(present_table, jnp.float32)[offset_of_sender]
-    slot_sums = jnp.sum(arrived_sums * weights[:, :, None], axis=(0, 1))
-    for source, sums in outgoing_sums[0]:
-        slot_sums = slot_sums + sums * member[(me + source) % grp_count]
+    slot_sums = slot_sums + jnp.sum(arrived_sums * weights[:, :, None], axis=(0, 1))
+
+    for target, items in sorted(late.items()):
+        stacked = shift(jnp.stack([s for _, s in items]), target)
+        slot_sums = slot_sums + weighted(stacked, items, target)
 
     own_valid = valid_at[0].reshape(2, wide_count, split).transpose(1, 0, 2).reshape(wide_count, capacity)
     arrived = jnp.sum(own_valid, axis=1).astype(jnp.int32)
@@ -115,12 +127,11 @@
     within = jnp.arange(capacity, dtype=jnp.int32)
     places = jnp.where(own_valid > 0, offsets[:, None] + within[None, :], BLK)
     places = places.reshape(wide_count, 2, split).transpose(1, 0, 2).reshape(-1)
-    density = jnp.zeros((BLK,), jnp.float32).at[places].set(slot_sums, mode="drop")
+    rows_iota = jnp.arange(BLK, dtype=jnp.int32)
+    density = jnp.sum(jnp.where(places[:, None] == rows_iota[None, :], slot_sums[:, None], 0.0), axis=0)
     return density.reshape(1, BLK)
 
 
 def solution(mesh):
     placed = (P(("wide", "grp"), None), P(("wide", "grp")), P(("wide", "grp")))
-    return jax.shard_map(
-        per_device, mesh=mesh, in_specs=placed, out_specs=P(("wide", "grp"), None), check_vma=False
-    )
+    return jax.shard_map(per_device, mesh=mesh, in_specs=placed, out_specs=P(("wide", "grp"), None), check_vma=False)

time: 163 us -> 166 us (1.018)
  starting transfers between devices: 86.6 us -> 96.4 us
  waiting for transfers between devices: 44.2 us -> 41.2 us
  other arithmetic: 12.3 us -> 10.1 us
    all_to_all x1, waiting for transfers between devices: 12.2 us -> 0.01 us  [per_device(): lax.all_to_all(by_device, 'grp', split_axis=0, concat_axis=0, tiled=True)]
    ppermute x16 -> x18, starting transfers between devices: 61.1 us -> 70.9 us  [shift(): lax.ppermute(value, 'grp', [(i, (i + offset) % grp_count) for i in range(...]
    ppermute x16 -> x18, waiting for transfers between devices: 23.6 us -> 32.8 us  [shift(): lax.ppermute(value, 'grp', [(i, (i + offset) % grp_count) for i in range(...]
    add x1, other arithmetic: 3.19 us -> 0.01 us  [per_device(): slot_sums = slot_sums + weighted(stacked, items, target)]
    scatter x1 -> x0, local copies, waits for them, and re-layouts: 2.91 us -> none  [per_device(): jnp.zeros((BLK,), jnp.float32).at[places].set(slot_sums, mode='drop')]
    gather x0 -> x3, local copies, waits for them, and re-layouts: none -> 1.94 us  [weighted(): return jnp.sum(stacked * member[sources][:, None], axis=0)]
  transfers between devices with their start and end apart: 19 -> 21, of which waited for: 9 -> 10; matrix products, arithmetic and copies ran while one was open for 6% -> 7% of each run, Pallas kernels for 0% -> 0%
where the time goes in v6:
time: 166 us; the launch traced here: 164 us
  starting transfers between devices  96.4 us (58%)
  waiting for transfers between devices  41.2 us (25%)
  other arithmetic  10.1 us (6%)
  local copies, waits for them, and re-layouts  8.95 us (5%)
  matrix products  6.03 us (4%)
    ppermute x18, starting transfers between devices, shift(): lax.ppermute(value, 'grp', [(i, (i + offset) % grp_count) for i in range(...  70.9 us
    ppermute x18, waiting for transfers between devices, shift(): lax.ppermute(value, 'grp', [(i, (i + offset) % grp_count) for i in range(...  32.8 us
    all_to_all x2, starting transfers between devices, per_device(): lax.all_to_all(h, 'wide', split_axis=0, concat_axis=0, tiled=True)  15.7 us
    all_to_all x1, starting transfers between devices, per_device(): lax.all_to_all(by_device, 'grp', split_axis=0, concat_axis=0, tiled=True)  9.81 us
    all_to_all x2, waiting for transfers between devices, per_device(): lax.all_to_all(h, 'wide', split_axis=0, concat_axis=0, tiled=True)  8.36 us
    dot_general x9, matrix products, pair_products(): lax.dot_general(left_rows, right_rows, (((1,), (1,)), ((), ())), preferre...  6.03 us
  transfers between devices with their start and end apart: 21, of which 10 were waited for; matrix products, arithmetic and copies ran while one was open for 7% of the time, Pallas kernels for 0%

profile of v6, /device:TPU:6, one launch (start us, length us, event | category | flops | bytes accessed | tf_op | source)
XLA Modules:
  0.0 164.2 jit_solution(16070764815439646616)
XLA Ops:
  6.0 2.3 %scatter_custom_fusion = bf16[384,1024]{1,0:T(8,128)(2,1)S(1)} fusion(bf16[384,1024]{1,0:T(8,128)(2,1)S(1)} %scatter.15, s32[288]{0:T(512)S(1)} %compare_select_fusion.1, bf16[288,1024]{1,0:T(8,128)(2,1)S(1)} %copy-done, f32[288]{0:T(512)S(1)} %add_rsqrt_fusion), kind=kCustom, calls=%fused_computation.42 | custom fusion | flops 884736 | bytes 1378304 | tf_op jit(solution)/shard_map/scatter | solution.py:40
  9.7 9.5 %all-to-all-start = ((bf16[32,6,1024]{2,1,0:T(8,128)(2,1)}), bf16[32,6,1024]{2,1,0:T(8,128)(2,1)S(1)}, u32[]{:S(2)}, u32[]{:S(2)}) async-start(bf16[32,6,1024]{2,1,0:T(8,128)(2,1)} %get-tuple-element.57), calls=%async_computation | async-start | bytes 1048576 | tf_op jit(solution)/shard_map/all_to_all | solution.py:44
  20.3 8.4 %all-to-all-done = bf16[32,6,1024]{2,1,0:T(8,128)(2,1)S(1)} async-done(((bf16[32,6,1024]{2,1,0:T(8,128)(2,1)}), bf16[32,6,1024]{2,1,0:T(8,128)(2,1)S(1)}, u32[]{:S(2)}, u32[]{:S(2)}) %all-to-all-start) | async-done | bytes 393248 | tf_op jit(solution)/shard_map/all_to_all | solution.py:44
  28.7 6.2 %all-to-all-start.1 = ((bf16[32,6,1024]{2,1,0:T(8,128)(2,1)}), bf16[32,6,1024]{2,1,0:T(8,128)(2,1)S(1)}, u32[]{:S(2)}, u32[]{:S(2)}) async-start(bf16[32,6,1024]{2,1,0:T(8,128)(2,1)} %get-tuple-element.56), calls=%async_computation.1 | async-start | bytes 1048576 | tf_op jit(solution)/shard_map/all_to_all | solution.py:44
  40.5 9.5 %collective-permute-start = (bf16[192,1024]{1,0:T(8,128)(2,1)S(1)}, bf16[192,1024]{1,0:T(8,128)(2,1)S(1)}, u32[]{:S(2)}, u32[]{:S(2)}) collective-permute-start(bf16[192,1024]{1,0:T(8,128)(2,1)S(1)} %reshape.352), channel_id=1, source_target_pairs={{0,15},{1,0},{2,1},{3,2},{4,3},{5,4},{6,5},{7,6},{8,7},{9,8},{10,9... | collective-permute-start | bytes 1179656 | tf_op jit(solution)/shard_map/ppermute | solution.py:52
  50.2 1.9 %collective-permute-start.8 = (bf16[192,1024]{1,0:T(8,128)(2,1)S(1)}, bf16[192,1024]{1,0:T(8,128)(2,1)}, u32[]{:S(2)}, u32[]{:S(2)}) collective-permute-start(bf16[192,1024]{1,0:T(8,128)(2,1)S(1)} %reshape.353), channel_id=1, source_target_pairs={{0,1},{1,2},{2,3},{3,4},{4,5},{5,6},{6,7},{7,8},{8,9},{9,10},{10,1... | collective-permute-start | bytes 1179656 | tf_op jit(solution)/shard_map/ppermute | solution.py:52
  52.1 5.1 %collective-permute-start.1 = (bf16[192,1024]{1,0:T(8,128)(2,1)S(1)}, bf16[192,1024]{1,0:T(8,128)(2,1)S(1)}, u32[]{:S(2)}, u32[]{:S(2)}) collective-permute-start(bf16[192,1024]{1,0:T(8,128)(2,1)S(1)} %reshape.353), channel_id=1, source_target_pairs={{0,15},{1,0},{2,1},{3,2},{4,3},{5,4},{6,5},{7,6},{8,7},{9,8},{10,9... | collective-permute-start | bytes 1179656 | tf_op jit(solution)/shard_map/ppermute | solution.py:52
  60.8 5.1 %collective-permute-start.2 = (bf16[192,1024]{1,0:T(8,128)(2,1)S(1)}, bf16[192,1024]{1,0:T(8,128)(2,1)S(1)}, u32[]{:S(2)}, u32[]{:S(2)}) collective-permute-start(bf16[192,1024]{1,0:T(8,128)(2,1)S(1)} %collective-permute-done), channel_id=1, source_target_pairs={{0,15},{1,0},{2,1},{3,2},{4,3},{5,4},{6,5},{7,6},{8,7},{9,8},{10,9... | collective-permute-start | bytes 1179656 | tf_op jit(solution)/shard_map/ppermute | solution.py:52
  66.0 2.0 %collective-permute-done.1 = bf16[192,1024]{1,0:T(8,128)(2,1)S(1)} collective-permute-done((bf16[192,1024]{1,0:T(8,128)(2,1)S(1)}, bf16[192,1024]{1,0:T(8,128)(2,1)S(1)}, u32[]{:S(2)}, u32[]{:S(2)}) %collective-permute-start.1) | collective-permute-done | bytes 393248 | tf_op jit(solution)/shard_map/ppermute | solution.py:52
  67.9 5.6 %collective-permute-start.3 = (bf16[192,1024]{1,0:T(8,128)(2,1)S(1)}, bf16[192,1024]{1,0:T(8,128)(2,1)S(1)}, u32[]{:S(2)}, u32[]{:S(2)}) collective-permute-start(bf16[192,1024]{1,0:T(8,128)(2,1)S(1)} %collective-permute-done.1), channel_id=1, source_target_pairs={{0,15},{1,0},{2,1},{3,2},{4,3},{5,4},{6,5},{7,6},{8,7},{9,8},{10,9... | collective-permute-start | bytes 1179656 | tf_op jit(solution)/shard_map/ppermute | solution.py:52
  76.4 7.6 %collective-permute-done.3 = bf16[192,1024]{1,0:T(8,128)(2,1)S(1)} collective-permute-done((bf16[192,1024]{1,0:T(8,128)(2,1)S(1)}, bf16[192,1024]{1,0:T(8,128)(2,1)S(1)}, u32[]{:S(2)}, u32[]{:S(2)}) %collective-permute-start.3) | collective-permute-done | bytes 393248 | tf_op jit(solution)/shard_map/ppermute | solution.py:52
  84.1 2.6 %collective-permute-done.9 = bf16[192,1024]{1,0:T(8,128)(2,1)S(1)} collective-permute-done((bf16[192,1024]{1,0:T(8,128)(2,1)}, bf16[192,1024]{1,0:T(8,128)(2,1)S(1)}, u32[]{:S(2)}, u32[]{:S(2)}) %collective-permute-start.9) | collective-permute-done | bytes 393248 | tf_op jit(solution)/shard_map/ppermute | solution.py:52
  89.3 5.1 %collective-permute-start.4 = (bf16[192,1024]{1,0:T(8,128)(2,1)S(1)}, bf16[192,1024]{1,0:T(8,128)(2,1)S(1)}, u32[]{:S(2)}, u32[]{:S(2)}) collective-permute-start(bf16[192,1024]{1,0:T(8,128)(2,1)S(1)} %collective-permute-done.2), channel_id=1, source_target_pairs={{0,15},{1,0},{2,1},{3,2},{4,3},{5,4},{6,5},{7,6},{8,7},{9,8},{10,9... | collective-permute-start | bytes 1179656 | tf_op jit(solution)/shard_map/ppermute | solution.py:52
  96.4 5.1 %collective-permute-start.5 = (bf16[192,1024]{1,0:T(8,128)(2,1)S(1)}, bf16[192,1024]{1,0:T(8,128)(2,1)S(1)}, u32[]{:S(2)}, u32[]{:S(2)}) collective-permute-start(bf16[192,1024]{1,0:T(8,128)(2,1)S(1)} %collective-permute-done.3), channel_id=1, source_target_pairs={{0,15},{1,0},{2,1},{3,2},{4,3},{5,4},{6,5},{7,6},{8,7},{9,8},{10,9... | collective-permute-start | bytes 1179656 | tf_op jit(solution)/shard_map/ppermute | solution.py:52
  102.3 6.2 %collective-permute-done.5 = bf16[192,1024]{1,0:T(8,128)(2,1)S(1)} collective-permute-done((bf16[192,1024]{1,0:T(8,128)(2,1)S(1)}, bf16[192,1024]{1,0:T(8,128)(2,1)S(1)}, u32[]{:S(2)}, u32[]{:S(2)}) %collective-permute-start.5) | collective-permute-done | bytes 393248 | tf_op jit(solution)/shard_map/ppermute | solution.py:52
  111.8 2.9 %collective-permute-start.13 = (bf16[192,1024]{1,0:T(8,128)(2,1)S(1)}, bf16[192,1024]{1,0:T(8,128)(2,1)S(1)}, u32[]{:S(2)}, u32[]{:S(2)}) collective-permute-start(bf16[192,1024]{1,0:T(8,128)(2,1)S(1)} %collective-permute-done.11), channel_id=1, source_target_pairs={{0,1},{1,2},{2,3},{3,4},{4,5},{5,6},{6,7},{7,8},{8,9},{9,10},{10,1... | collective-permute-start | bytes 1179656 | tf_op jit(solution)/shard_map/ppermute | solution.py:52
  115.3 4.6 %collective-permute-start.14 = (bf16[192,1024]{1,0:T(8,128)(2,1)S(1)}, bf16[192,1024]{1,0:T(8,128)(2,1)S(1)}, u32[]{:S(2)}, u32[]{:S(2)}) collective-permute-start(bf16[192,1024]{1,0:T(8,128)(2,1)S(1)} %collective-permute-done.4), channel_id=1, source_target_pairs={{0,15},{1,0},{2,1},{3,2},{4,3},{5,4},{6,5},{7,6},{8,7},{9,8},{10,9... | collective-permute-start | bytes 1179656 | tf_op jit(solution)/shard_map/ppermute | solution.py:52
  120.2 4.1 %collective-permute-start.15 = (bf16[192,1024]{1,0:T(8,128)(2,1)S(1)}, bf16[192,1024]{1,0:T(8,128)(2,1)S(1)}, u32[]{:S(2)}, u32[]{:S(2)}) collective-permute-start(bf16[192,1024]{1,0:T(8,128)(2,1)S(1)} %collective-permute-done.5), channel_id=1, source_target_pairs={{0,15},{1,0},{2,1},{3,2},{4,3},{5,4},{6,5},{7,6},{8,7},{9,8},{10,9... | collective-permute-start | bytes 1179656 | tf_op jit(solution)/shard_map/ppermute | solution.py:52
  124.8 5.3 %collective-permute-done.13 = bf16[192,1024]{1,0:T(8,128)(2,1)S(1)} collective-permute-done((bf16[192,1024]{1,0:T(8,128)(2,1)S(1)}, bf16[192,1024]{1,0:T(8,128)(2,1)S(1)}, u32[]{:S(2)}, u32[]{:S(2)}) %collective-permute-start.13) | collective-permute-done | bytes 393248 | tf_op jit(solution)/shard_map/ppermute | solution.py:52
  130.3 4.6 %collective-permute-done.15 = bf16[192,1024]{1,0:T(8,128)(2,1)S(1)} collective-permute-done((bf16[192,1024]{1,0:T(8,128)(2,1)S(1)}, bf16[192,1024]{1,0:T(8,128)(2,1)S(1)}, u32[]{:S(2)}, u32[]{:S(2)}) %collective-permute-start.15) | collective-permute-done | bytes 393248 | tf_op jit(solution)/shard_map/ppermute | solution.py:52
  138.4 9.8 %all-to-all-start.2 = ((f32[16,3,384]{2,1,0:T(4,128)}), f32[16,3,384]{2,1,0:T(4,128)S(1)}, u32[]{:S(2)}, u32[]{:S(2)}) async-start(f32[16,3,384]{2,1,0:T(4,128)} %gather_fusion.1), calls=%async_computation.2 | async-start | bytes 196608 | tf_op jit(solution)/shard_map/all_to_all | solution.py:114
  148.2 5.6 %collective-permute-start.17 = (f32[1,384]{1,0:T(1,128)S(1)}, f32[1,384]{1,0:T(1,128)S(1)}, u32[]{:S(2)}, u32[]{:S(2)}) collective-permute-start(f32[1,384]{1,0:T(1,128)S(1)} %stack.119), channel_id=1, source_target_pairs={{0,3},{1,4},{2,5},{3,6},{4,7},{5,8},{6,9},{7,10},{8,11},{9,12},{10... | collective-permute-start | bytes 4616 | tf_op jit(solution)/shard_map/ppermute | solution.py:52
  153.8 4.6 %collective-permute-start.16 = (f32[2,384]{1,0:T(2,128)S(1)}, f32[2,384]{1,0:T(2,128)S(1)}, u32[]{:S(2)}, u32[]{:S(2)}) collective-permute-start(f32[2,384]{1,0:T(2,128)S(1)} %pad_maximum_fusion), channel_id=1, source_target_pairs={{0,12},{1,13},{2,14},{3,15},{4,0},{5,1},{6,2},{7,3},{8,4},{9,5},{1... | collective-permute-start | bytes 9224 | tf_op jit(solution)/shard_map/ppermute | solution.py:52
  159.2 4.0 %collective-permute-done.16 = f32[2,384]{1,0:T(2,128)S(1)} collective-permute-done((f32[2,384]{1,0:T(2,128)S(1)}, f32[2,384]{1,0:T(2,128)S(1)}, u32[]{:S(2)}, u32[]{:S(2)}) %collective-permute-start.16) | collective-permute-done | bytes 3104 | tf_op jit(solution)/shard_map/ppermute | solution.py:52
  (148 shorter events, 35.0 us)
Async XLA Ops:
  9.7 9.6 %copy-start.4 = (s32[2]{0:T(128)S(1)}, s32[2]{0:T(128)}, u32[]{:S(2)}) copy-start(s32[2]{0:T(128)} %constant.162.clone) | copy-start | bytes 28
  9.7 9.6 %copy-start.2 = (s32[16,3]{1,0:T(8,128)S(1)}, s32[16,3]{1,0:T(8,128)}, u32[]{:S(2)}) copy-start(s32[16,3]{1,0:T(8,128)} %constant.160.clone) | copy-start | bytes 580
  9.7 10.5 %copy-start.3 = (s32[16]{0:T(128)S(1)}, s32[16]{0:T(128)}, u32[]{:S(2)}) copy-start(s32[16]{0:T(128)} %param.12) | copy-start | bytes 196
  9.7 19.0 %all-to-all-start = ((bf16[32,6,1024]{2,1,0:T(8,128)(2,1)}), bf16[32,6,1024]{2,1,0:T(8,128)(2,1)S(1)}, u32[]{:S(2)}, u32[]{:S(2)}) async-start(bf16[32,6,1024]{2,1,0:T(8,128)(2,1)} %get-tuple-element.57), calls=%async_computation | async-start | bytes 1048576 | tf_op jit(solution)/shard_map/all_to_all | solution.py:44
  28.7 21.3 %all-to-all-start.1 = ((bf16[32,6,1024]{2,1,0:T(8,128)(2,1)}), bf16[32,6,1024]{2,1,0:T(8,128)(2,1)S(1)}, u32[]{:S(2)}, u32[]{:S(2)}) async-start(bf16[32,6,1024]{2,1,0:T(8,128)(2,1)} %get-tuple-element.56), calls=%async_computation.1 | async-start | bytes 1048576 | tf_op jit(solution)/shard_map/all_to_all | solution.py:44
  38.6 20.3 %collective-permute-start.6 = (bf16[192,1024]{1,0:T(8,128)(2,1)S(1)}, bf16[192,1024]{1,0:T(8,128)(2,1)S(1)}, u32[]{:S(2)}, u32[]{:S(2)}) collective-permute-start(bf16[192,1024]{1,0:T(8,128)(2,1)S(1)} %reshape.352), channel_id=1, source_target_pairs={{0,1},{1,2},{2,3},{3,4},{4,5},{5,6},{6,7},{7,8},{8,9},{9,10},{10,1... | collective-permute-start | bytes 1179656 | tf_op jit(solution)/shard_map/ppermute | solution.py:52
  40.5 20.3 %collective-permute-start = (bf16[192,1024]{1,0:T(8,128)(2,1)S(1)}, bf16[192,1024]{1,0:T(8,128)(2,1)S(1)}, u32[]{:S(2)}, u32[]{:S(2)}) collective-permute-start(bf16[192,1024]{1,0:T(8,128)(2,1)S(1)} %reshape.352), channel_id=1, source_target_pairs={{0,15},{1,0},{2,1},{3,2},{4,3},{5,4},{6,5},{7,6},{8,7},{9,8},{10,9... | collective-permute-start | bytes 1179656 | tf_op jit(solution)/shard_map/ppermute | solution.py:52
  50.2 24.1 %collective-permute-start.8 = (bf16[192,1024]{1,0:T(8,128)(2,1)S(1)}, bf16[192,1024]{1,0:T(8,128)(2,1)}, u32[]{:S(2)}, u32[]{:S(2)}) collective-permute-start(bf16[192,1024]{1,0:T(8,128)(2,1)S(1)} %reshape.353), channel_id=1, source_target_pairs={{0,1},{1,2},{2,3},{3,4},{4,5},{5,6},{6,7},{7,8},{8,9},{9,10},{10,1... | collective-permute-start | bytes 1179656 | tf_op jit(solution)/shard_map/ppermute | solution.py:52
  52.1 15.8 %collective-permute-start.1 = (bf16[192,1024]{1,0:T(8,128)(2,1)S(1)}, bf16[192,1024]{1,0:T(8,128)(2,1)S(1)}, u32[]{:S(2)}, u32[]{:S(2)}) collective-permute-start(bf16[192,1024]{1,0:T(8,128)(2,1)S(1)} %reshape.353), channel_id=1, source_target_pairs={{0,15},{1,0},{2,1},{3,2},{4,3},{5,4},{6,5},{7,6},{8,7},{9,8},{10,9... | collective-permute-start | bytes 1179656 | tf_op jit(solution)/shard_map/ppermute | solution.py:52
  58.8 25.2 %collective-permute-start.7 = (bf16[192,1024]{1,0:T(8,128)(2,1)S(1)}, bf16[192,1024]{1,0:T(8,128)(2,1)S(1)}, u32[]{:S(2)}, u32[]{:S(2)}) collective-permute-start(bf16[192,1024]{1,0:T(8,128)(2,1)S(1)} %collective-permute-done.6), channel_id=1, source_target_pairs={{0,1},{1,2},{2,3},{3,4},{4,5},{5,6},{6,7},{7,8},{8,9},{9,10},{10,1... | collective-permute-start | bytes 1179656 | tf_op jit(solution)/shard_map/ppermute | solution.py:52
  60.8 15.6 %collective-permute-start.2 = (bf16[192,1024]{1,0:T(8,128)(2,1)S(1)}, bf16[192,1024]{1,0:T(8,128)(2,1)S(1)}, u32[]{:S(2)}, u32[]{:S(2)}) collective-permute-start(bf16[192,1024]{1,0:T(8,128)(2,1)S(1)} %collective-permute-done), channel_id=1, source_target_pairs={{0,15},{1,0},{2,1},{3,2},{4,3},{5,4},{6,5},{7,6},{8,7},{9,8},{10,9... | collective-permute-start | bytes 1179656 | tf_op jit(solution)/shard_map/ppermute | solution.py:52
  67.9 16.0 %collective-permute-start.3 = (bf16[192,1024]{1,0:T(8,128)(2,1)S(1)}, bf16[192,1024]{1,0:T(8,128)(2,1)S(1)}, u32[]{:S(2)}, u32[]{:S(2)}) collective-permute-start(bf16[192,1024]{1,0:T(8,128)(2,1)S(1)} %collective-permute-done.1), channel_id=1, source_target_pairs={{0,15},{1,0},{2,1},{3,2},{4,3},{5,4},{6,5},{7,6},{8,7},{9,8},{10,9... | collective-permute-start | bytes 1179656 | tf_op jit(solution)/shard_map/ppermute | solution.py:52
  74.3 12.5 %collective-permute-start.9 = (bf16[192,1024]{1,0:T(8,128)(2,1)}, bf16[192,1024]{1,0:T(8,128)(2,1)S(1)}, u32[]{:S(2)}, u32[]{:S(2)}) collective-permute-start(bf16[192,1024]{1,0:T(8,128)(2,1)} %collective-permute-done.8), channel_id=1, source_target_pairs={{0,1},{1,2},{2,3},{3,4},{4,5},{5,6},{6,7},{7,8},{8,9},{9,10},{10,1... | collective-permute-start | bytes 1179656 | tf_op jit(solution)/shard_map/ppermute | solution.py:52
  87.4 21.8 %collective-permute-start.10 = (bf16[192,1024]{1,0:T(8,128)(2,1)S(1)}, bf16[192,1024]{1,0:T(8,128)(2,1)S(1)}, u32[]{:S(2)}, u32[]{:S(2)}) collective-permute-start(bf16[192,1024]{1,0:T(8,128)(2,1)S(1)} %collective-permute-done.7), channel_id=1, source_target_pairs={{0,1},{1,2},{2,3},{3,4},{4,5},{5,6},{6,7},{7,8},{8,9},{9,10},{10,1... | collective-permute-start | bytes 1179656 | tf_op jit(solution)/shard_map/ppermute | solution.py:52
  89.3 12.9 %collective-permute-start.4 = (bf16[192,1024]{1,0:T(8,128)(2,1)S(1)}, bf16[192,1024]{1,0:T(8,128)(2,1)S(1)}, u32[]{:S(2)}, u32[]{:S(2)}) collective-permute-start(bf16[192,1024]{1,0:T(8,128)(2,1)S(1)} %collective-permute-done.2), channel_id=1, source_target_pairs={{0,15},{1,0},{2,1},{3,2},{4,3},{5,4},{6,5},{7,6},{8,7},{9,8},{10,9... | collective-permute-start | bytes 1179656 | tf_op jit(solution)/shard_map/ppermute | solution.py:52
  94.5 17.3 %collective-permute-start.11 = (bf16[192,1024]{1,0:T(8,128)(2,1)S(1)}, bf16[192,1024]{1,0:T(8,128)(2,1)S(1)}, u32[]{:S(2)}, u32[]{:S(2)}) collective-permute-start(bf16[192,1024]{1,0:T(8,128)(2,1)S(1)} %collective-permute-done.9), channel_id=1, source_target_pairs={{0,1},{1,2},{2,3},{3,4},{4,5},{5,6},{6,7},{7,8},{8,9},{9,10},{10,1... | collective-permute-start | bytes 1179656 | tf_op jit(solution)/shard_map/ppermute | solution.py:52
  96.4 12.1 %collective-permute-start.5 = (bf16[192,1024]{1,0:T(8,128)(2,1)S(1)}, bf16[192,1024]{1,0:T(8,128)(2,1)S(1)}, u32[]{:S(2)}, u32[]{:S(2)}) collective-permute-start(bf16[192,1024]{1,0:T(8,128)(2,1)S(1)} %collective-permute-done.3), channel_id=1, source_target_pairs={{0,15},{1,0},{2,1},{3,2},{4,3},{5,4},{6,5},{7,6},{8,7},{9,8},{10,9... | collective-permute-start | bytes 1179656 | tf_op jit(solution)/shard_map/ppermute | solution.py:52
  109.2 15.6 %collective-permute-start.12 = (bf16[192,1024]{1,0:T(8,128)(2,1)S(1)}, bf16[192,1024]{1,0:T(8,128)(2,1)S(1)}, u32[]{:S(2)}, u32[]{:S(2)}) collective-permute-start(bf16[192,1024]{1,0:T(8,128)(2,1)S(1)} %collective-permute-done.10), channel_id=1, source_target_pairs={{0,1},{1,2},{2,3},{3,4},{4,5},{5,6},{6,7},{7,8},{8,9},{9,10},{10,1... | collective-permute-start | bytes 1179656 | tf_op jit(solution)/shard_map/ppermute | solution.py:52
  111.8 18.3 %collective-permute-start.13 = (bf16[192,1024]{1,0:T(8,128)(2,1)S(1)}, bf16[192,1024]{1,0:T(8,128)(2,1)S(1)}, u32[]{:S(2)}, u32[]{:S(2)}) collective-permute-start(bf16[192,1024]{1,0:T(8,128)(2,1)S(1)} %collective-permute-done.11), channel_id=1, source_target_pairs={{0,1},{1,2},{2,3},{3,4},{4,5},{5,6},{6,7},{7,8},{8,9},{9,10},{10,1... | collective-permute-start | bytes 1179656 | tf_op jit(solution)/shard_map/ppermute | solution.py:52
  115.3 14.9 %collective-permute-start.14 = (bf16[192,1024]{1,0:T(8,128)(2,1)S(1)}, bf16[192,1024]{1,0:T(8,128)(2,1)S(1)}, u32[]{:S(2)}, u32[]{:S(2)}) collective-permute-start(bf16[192,1024]{1,0:T(8,128)(2,1)S(1)} %collective-permute-done.4), channel_id=1, source_target_pairs={{0,15},{1,0},{2,1},{3,2},{4,3},{5,4},{6,5},{7,6},{8,7},{9,8},{10,9... | collective-permute-start | bytes 1179656 | tf_op jit(solution)/shard_map/ppermute | solution.py:52
  120.2 14.7 %collective-permute-start.15 = (bf16[192,1024]{1,0:T(8,128)(2,1)S(1)}, bf16[192,1024]{1,0:T(8,128)(2,1)S(1)}, u32[]{:S(2)}, u32[]{:S(2)}) collective-permute-start(bf16[192,1024]{1,0:T(8,128)(2,1)S(1)} %collective-permute-done.5), channel_id=1, source_target_pairs={{0,15},{1,0},{2,1},{3,2},{4,3},{5,4},{6,5},{7,6},{8,7},{9,8},{10,9... | collective-permute-start | bytes 1179656 | tf_op jit(solution)/shard_map/ppermute | solution.py:52
  138.4 25.0 %all-to-all-start.2 = ((f32[16,3,384]{2,1,0:T(4,128)}), f32[16,3,384]{2,1,0:T(4,128)S(1)}, u32[]{:S(2)}, u32[]{:S(2)}) async-start(f32[16,3,384]{2,1,0:T(4,128)} %gather_fusion.1), calls=%async_computation.2 | async-start | bytes 196608 | tf_op jit(solution)/shard_map/all_to_all | solution.py:114
  148.2 10.3 %collective-permute-start.17 = (f32[1,384]{1,0:T(1,128)S(1)}, f32[1,384]{1,0:T(1,128)S(1)}, u32[]{:S(2)}, u32[]{:S(2)}) collective-permute-start(f32[1,384]{1,0:T(1,128)S(1)} %stack.119), channel_id=1, source_target_pairs={{0,3},{1,4},{2,5},{3,6},{4,7},{5,8},{6,9},{7,10},{8,11},{9,12},{10... | collective-permute-start | bytes 4616 | tf_op jit(solution)/shard_map/ppermute | solution.py:52
  153.8 9.4 %collective-permute-start.16 = (f32[2,384]{1,0:T(2,128)S(1)}, f32[2,384]{1,0:T(2,128)S(1)}, u32[]{:S(2)}, u32[]{:S(2)}) collective-permute-start(f32[2,384]{1,0:T(2,128)S(1)} %pad_maximum_fusion), channel_id=1, source_target_pairs={{0,12},{1,13},{2,14},{3,15},{4,0},{5,1},{6,2},{7,3},{8,4},{9,5},{1... | collective-permute-start | bytes 9224 | tf_op jit(solution)/shard_map/ppermute | solution.py:52
  (2 other events, 14.2 us)

commit v7 on v6

--- a/solution.py
+++ b/solution.py
@@ -40,8 +40,11 @@
     outgoing = empty.at[send_slots].set(unit_rows).reshape(wide_count, capacity, feature_width)
     split = capacity // 2
     halves = [outgoing[:, :split], outgoing[:, split:]]
+    lanes = 128
     own_halves = [
-        lax.all_to_all(h, "wide", split_axis=0, concat_axis=0, tiled=True).reshape(-1, feature_width)
+        lax.all_to_all(
+            h.reshape(wide_count, -1, lanes), "wide", split_axis=0, concat_axis=0, tiled=True
+        ).reshape(-1, feature_width)
         for h in halves
     ]
 
@@ -134,4 +137,6 @@
 
 def solution(mesh):
     placed = (P(("wide", "grp"), None), P(("wide", "grp")), P(("wide", "grp")))
-    return jax.shard_map(per_device, mesh=mesh, in_specs=placed, out_specs=P(("wide", "grp"), None), check_vma=False)
+    return jax.shard_map(
+        per_device, mesh=mesh, in_specs=placed, out_specs=P(("wide", "grp"), None), check_vma=False
+    )

time: 166 us -> 188 us (1.13)
  waiting for transfers between devices: 41.2 us -> 61 us
  starting transfers between devices: 96.4 us -> 88.1 us
  matrix products: 6.03 us -> 11.6 us
  local copies, waits for them, and re-layouts: 8.95 us -> 13.4 us
    all_to_all x1, waiting for transfers between devices: 0.01 us -> 12.1 us  [per_device(): lax.all_to_all(by_device, 'grp', split_axis=0, concat_axis=0, tiled=True)]
    ppermute x18, waiting for transfers between devices: 32.8 us -> 43 us  [shift(): lax.ppermute(value, 'grp', [(i, (i + offset) % grp_count) for i in range(...]
    dot_general x9, matrix products: 6.03 us -> 11.6 us  [pair_products(): lax.dot_general(left_rows, right_rows, (((1,), (1,)), ((), ())), preferre...]
    ppermute x18, starting transfers between devices: 70.9 us -> 65.9 us  [shift(): lax.ppermute(value, 'grp', [(i, (i + offset) % grp_count) for i in range(...]
    all_to_all x1, starting transfers between devices: 9.81 us -> 6.68 us  [per_device(): lax.all_to_all(by_device, 'grp', split_axis=0, concat_axis=0, tiled=True)]
    reshape x2 -> x6, local copies, waits for them, and re-layouts: 0.27 us -> 3.16 us  [the longest x2 2.41 us: per_device(): h.reshape(wide_count, -1, lanes)]
    all_to_all x2, waiting for transfers between devices: 8.36 us -> 5.86 us  [per_device(): lax.all_to_all(h.reshape(wide_count, -1, lanes), 'wide', split_axis=0, co...]
  transfers between devices with their start and end apart: 21 -> 21, of which waited for: 10 -> 12; matrix products, arithmetic and copies ran while one was open for 7% -> 14% of each run, Pallas kernels for 0% -> 0%
where the time goes in v7:
time: 188 us; the launch traced here: 187 us
  starting transfers between devices  88.1 us (47%)
  waiting for transfers between devices  61 us (32%)
  local copies, waits for them, and re-layouts  13.4 us (7%)
  matrix products  11.6 us (6%)
  other arithmetic  11.2 us (6%)
    ppermute x18, starting transfers between devices, shift(): lax.ppermute(value, 'grp', [(i, (i + offset) % grp_count) for i in range(...  65.9 us
    ppermute x18, waiting for transfers between devices, shift(): lax.ppermute(value, 'grp', [(i, (i + offset) % grp_count) for i in range(...  43 us
    all_to_all x2, starting transfers between devices, per_device(): lax.all_to_all(h.reshape(wide_count, -1, lanes), 'wide', split_axis=0, co...  15.5 us
    all_to_all x1, waiting for transfers between devices, per_device(): lax.all_to_all(by_device, 'grp', split_axis=0, concat_axis=0, tiled=True)  12.1 us
    dot_general x9, matrix products, pair_products(): lax.dot_general(left_rows, right_rows, (((1,), (1,)), ((), ())), preferre...  11.6 us
    all_to_all x1, starting transfers between devices, per_device(): lax.all_to_all(by_device, 'grp', split_axis=0, concat_axis=0, tiled=True)  6.68 us
    all_to_all x2, waiting for transfers between devices, per_device(): lax.all_to_all(h.reshape(wide_count, -1, lanes), 'wide', split_axis=0, co...  5.86 us
  transfers between devices with their start and end apart: 21, of which 12 were waited for; matrix products, arithmetic and copies ran while one was open for 14% of the time, Pallas kernels for 0%

profile of v7, /device:TPU:6, one launch (start us, length us, event | category | flops | bytes accessed | tf_op | source)
XLA Modules:
  0.0 186.7 jit_solution(18062445612081874726)
XLA Ops:
  6.0 2.3 %scatter_custom_fusion = bf16[384,1024]{1,0:T(8,128)(2,1)S(1)} fusion(bf16[384,1024]{1,0:T(8,128)(2,1)S(1)} %scatter.15, s32[288]{0:T(512)S(1)} %compare_select_fusion.1, bf16[288,1024]{1,0:T(8,128)(2,1)S(1)} %copy-done, f32[288]{0:T(512)S(1)} %add_rsqrt_fusion), kind=kCustom, calls=%fused_computation.56 | custom fusion | flops 884736 | bytes 1378304 | tf_op jit(solution)/shard_map/scatter | solution.py:40
  10.0 9.5 %all-to-all-start.1 = ((bf16[32,48,128]{2,1,0:T(8,128)(2,1)}), bf16[32,48,128]{2,1,0:T(8,128)(2,1)S(1)}, u32[]{:S(2)}, u32[]{:S(2)}) async-start(bf16[32,48,128]{2,1,0:T(8,128)(2,1)} %reshape.360), calls=%async_computation.1 | async-start | bytes 786432 | tf_op jit(solution)/shard_map/all_to_all | solution.py:45
  21.8 5.9 %all-to-all-done.1 = bf16[32,48,128]{2,1,0:T(8,128)(2,1)S(1)} async-done(((bf16[32,48,128]{2,1,0:T(8,128)(2,1)}), bf16[32,48,128]{2,1,0:T(8,128)(2,1)S(1)}, u32[]{:S(2)}, u32[]{:S(2)}) %all-to-all-start.1) | async-done | bytes 393248 | tf_op jit(solution)/shard_map/all_to_all | solution.py:45
  27.6 6.0 %all-to-all-start = ((bf16[32,48,128]{2,1,0:T(8,128)(2,1)}), bf16[32,48,128]{2,1,0:T(8,128)(2,1)S(1)}, u32[]{:S(2)}, u32[]{:S(2)}) async-start(bf16[32,48,128]{2,1,0:T(8,128)(2,1)} %reshape.358), calls=%async_computation | async-start | bytes 786432 | tf_op jit(solution)/shard_map/all_to_all | solution.py:45
  40.4 9.5 %collective-permute-start.1 = (bf16[192,1024]{0,1:T(8,128)(2,1)S(1)}, bf16[192,1024]{0,1:T(8,128)(2,1)S(1)}, u32[]{:S(2)}, u32[]{:S(2)}) collective-permute-start(bf16[192,1024]{0,1:T(8,128)(2,1)S(1)} %copy.78), channel_id=1, source_target_pairs={{0,15},{1,0},{2,1},{3,2},{4,3},{5,4},{6,5},{7,6},{8,7},{9,8},{10,9... | collective-permute-start | bytes 1179656 | tf_op jit(solution)/shard_map/ppermute | solution.py:55
  50.3 2.9 %collective-permute-start = (bf16[192,1024]{0,1:T(8,128)(2,1)S(1)}, bf16[192,1024]{0,1:T(8,128)(2,1)S(1)}, u32[]{:S(2)}, u32[]{:S(2)}) collective-permute-start(bf16[192,1024]{0,1:T(8,128)(2,1)S(1)} %copy.77), channel_id=1, source_target_pairs={{0,15},{1,0},{2,1},{3,2},{4,3},{5,4},{6,5},{7,6},{8,7},{9,8},{10,9... | collective-permute-start | bytes 1179656 | tf_op jit(solution)/shard_map/ppermute | solution.py:55
  53.3 2.9 %collective-permute-start.8 = (bf16[192,1024]{0,1:T(8,128)(2,1)S(1)}, bf16[192,1024]{0,1:T(8,128)(2,1)}, u32[]{:S(2)}, u32[]{:S(2)}) collective-permute-start(bf16[192,1024]{0,1:T(8,128)(2,1)S(1)} %copy.78), channel_id=1, source_target_pairs={{0,1},{1,2},{2,3},{3,4},{4,5},{5,6},{6,7},{7,8},{8,9},{9,10},{10,1... | collective-permute-start | bytes 1179656 | tf_op jit(solution)/shard_map/ppermute | solution.py:55
  58.7 3.5 %collective-permute-done.1 = bf16[192,1024]{0,1:T(8,128)(2,1)S(1)} collective-permute-done((bf16[192,1024]{0,1:T(8,128)(2,1)S(1)}, bf16[192,1024]{0,1:T(8,128)(2,1)S(1)}, u32[]{:S(2)}, u32[]{:S(2)}) %collective-permute-start.1) | collective-permute-done | bytes 393248 | tf_op jit(solution)/shard_map/ppermute | solution.py:55
  62.2 5.6 %collective-permute-start.3 = (bf16[192,1024]{0,1:T(8,128)(2,1)S(1)}, bf16[192,1024]{0,1:T(8,128)(2,1)}, u32[]{:S(2)}, u32[]{:S(2)}) collective-permute-start(bf16[192,1024]{0,1:T(8,128)(2,1)S(1)} %collective-permute-done.1), channel_id=1, source_target_pairs={{0,15},{1,0},{2,1},{3,2},{4,3},{5,4},{6,5},{7,6},{8,7},{9,8},{10,9... | collective-permute-start | bytes 1179656 | tf_op jit(solution)/shard_map/ppermute | solution.py:55
  67.8 5.6 %collective-permute-done = bf16[192,1024]{0,1:T(8,128)(2,1)S(1)} collective-permute-done((bf16[192,1024]{0,1:T(8,128)(2,1)S(1)}, bf16[192,1024]{0,1:T(8,128)(2,1)S(1)}, u32[]{:S(2)}, u32[]{:S(2)}) %collective-permute-start) | collective-permute-done | bytes 393248 | tf_op jit(solution)/shard_map/ppermute | solution.py:55
  73.4 5.6 %collective-permute-start.2 = (bf16[192,1024]{0,1:T(8,128)(2,1)S(1)}, bf16[192,1024]{0,1:T(8,128)(2,1)}, u32[]{:S(2)}, u32[]{:S(2)}) collective-permute-start(bf16[192,1024]{0,1:T(8,128)(2,1)S(1)} %collective-permute-done), channel_id=1, source_target_pairs={{0,15},{1,0},{2,1},{3,2},{4,3},{5,4},{6,5},{7,6},{8,7},{9,8},{10,9... | collective-permute-start | bytes 1179656 | tf_op jit(solution)/shard_map/ppermute | solution.py:55
  84.7 5.7 %collective-permute-start.5 = (bf16[192,1024]{0,1:T(8,128)(2,1)}, bf16[192,1024]{0,1:T(8,128)(2,1)S(1)}, u32[]{:S(2)}, u32[]{:S(2)}) collective-permute-start(bf16[192,1024]{0,1:T(8,128)(2,1)} %collective-permute-done.3), channel_id=1, source_target_pairs={{0,15},{1,0},{2,1},{3,2},{4,3},{5,4},{6,5},{7,6},{8,7},{9,8},{10,9... | collective-permute-start | bytes 1179656 | tf_op jit(solution)/shard_map/ppermute | solution.py:55
  90.4 5.5 %collective-permute-done.2 = bf16[192,1024]{0,1:T(8,128)(2,1)} collective-permute-done((bf16[192,1024]{0,1:T(8,128)(2,1)S(1)}, bf16[192,1024]{0,1:T(8,128)(2,1)}, u32[]{:S(2)}, u32[]{:S(2)}) %collective-permute-start.2) | collective-permute-done | bytes 393248 | tf_op jit(solution)/shard_map/ppermute | solution.py:55
  95.9 5.7 %collective-permute-start.4 = (bf16[192,1024]{0,1:T(8,128)(2,1)}, bf16[192,1024]{0,1:T(8,128)(2,1)S(1)}, u32[]{:S(2)}, u32[]{:S(2)}) collective-permute-start(bf16[192,1024]{0,1:T(8,128)(2,1)} %collective-permute-done.2), channel_id=1, source_target_pairs={{0,15},{1,0},{2,1},{3,2},{4,3},{5,4},{6,5},{7,6},{8,7},{9,8},{10,9... | collective-permute-start | bytes 1179656 | tf_op jit(solution)/shard_map/ppermute | solution.py:55
  110.1 2.1 %fusion.10 = f32[384,384]{0,1:T(8,128)S(1)} fusion(bf16[192,1024]{0,1:T(8,128)(2,1)S(1)} %collective-permute-done.9, bf16[192,1024]{0,1:T(8,128)(2,1)S(1)} %collective-permute-done.7, bf16[192,1024]{0,1:T(8,128)(2,1)} %collective-permute-done.3, bf16[192,1024]{0,1:T(8,128)(2,1)} %collective-permute-done.2), kind=kOutput, calls=%fused_computation.28 | convolution fusion | flops 305430528 | bytes 2162688 | tf_op jit(solution)/shard_map/dot_general | solution.py:16
  112.3 7.3 %collective-permute-done.11 = bf16[192,1024]{0,1:T(8,128)(2,1)S(1)} collective-permute-done((bf16[192,1024]{0,1:T(8,128)(2,1)S(1)}, bf16[192,1024]{0,1:T(8,128)(2,1)S(1)}, u32[]{:S(2)}, u32[]{:S(2)}) %collective-permute-start.11) | collective-permute-done | bytes 393248 | tf_op jit(solution)/shard_map/ppermute | solution.py:55
  121.4 9.3 %collective-permute-done.10 = bf16[192,1024]{0,1:T(8,128)(2,1)S(1)} collective-permute-done((bf16[192,1024]{0,1:T(8,128)(2,1)S(1)}, bf16[192,1024]{0,1:T(8,128)(2,1)S(1)}, u32[]{:S(2)}, u32[]{:S(2)}) %collective-permute-start.10) | collective-permute-done | bytes 393248 | tf_op jit(solution)/shard_map/ppermute | solution.py:55
  132.7 2.1 %fusion.6 = f32[384,384]{0,1:T(8,128)S(1)} fusion(bf16[192,1024]{0,1:T(8,128)(2,1)} %collective-permute-done.3, bf16[192,1024]{0,1:T(8,128)(2,1)} %collective-permute-done.2, bf16[192,1024]{0,1:T(8,128)(2,1)S(1)} %copy.78, bf16[192,1024]{0,1:T(8,128)(2,1)S(1)} %copy.77), kind=kOutput, calls=%fused_computation.24 | convolution fusion | flops 305430528 | bytes 2162688 | tf_op jit(solution)/shard_map/dot_general | solution.py:16
  135.7 5.1 %collective-permute-start.15 = (bf16[192,1024]{0,1:T(8,128)(2,1)S(1)}, bf16[192,1024]{0,1:T(8,128)(2,1)S(1)}, u32[]{:S(2)}, u32[]{:S(2)}) collective-permute-start(bf16[192,1024]{0,1:T(8,128)(2,1)S(1)} %collective-permute-done.5), channel_id=1, source_target_pairs={{0,15},{1,0},{2,1},{3,2},{4,3},{5,4},{6,5},{7,6},{8,7},{9,8},{10,9... | collective-permute-start | bytes 1179656 | tf_op jit(solution)/shard_map/ppermute | solution.py:55
  146.0 4.5 %collective-permute-done.12 = bf16[192,1024]{0,1:T(8,128)(2,1)S(1)} collective-permute-done((bf16[192,1024]{0,1:T(8,128)(2,1)S(1)}, bf16[192,1024]{0,1:T(8,128)(2,1)S(1)}, u32[]{:S(2)}, u32[]{:S(2)}) %collective-permute-start.12) | collective-permute-done | bytes 393248 | tf_op jit(solution)/shard_map/ppermute | solution.py:55
  154.2 3.5 %collective-permute-done.14 = bf16[192,1024]{0,1:T(8,128)(2,1)S(1)} collective-permute-done((bf16[192,1024]{0,1:T(8,128)(2,1)S(1)}, bf16[192,1024]{0,1:T(8,128)(2,1)S(1)}, u32[]{:S(2)}, u32[]{:S(2)}) %collective-permute-start.14) | collective-permute-done | bytes 393248 | tf_op jit(solution)/shard_map/ppermute | solution.py:55
  158.9 5.5 %collective-permute-start.16 = (f32[2,384]{1,0:T(2,128)S(1)}, f32[2,384]{1,0:T(2,128)S(1)}, u32[]{:S(2)}, u32[]{:S(2)}) collective-permute-start(f32[2,384]{1,0:T(2,128)S(1)} %pad_maximum_fusion.11), channel_id=1, source_target_pairs={{0,12},{1,13},{2,14},{3,15},{4,0},{5,1},{6,2},{7,3},{8,4},{9,5},{1... | collective-permute-start | bytes 9224 | tf_op jit(solution)/shard_map/ppermute | solution.py:55
  166.1 6.7 %all-to-all-start.2 = ((f32[16,3,384]{2,1,0:T(4,128)}), f32[16,3,384]{2,1,0:T(4,128)S(1)}, u32[]{:S(2)}, u32[]{:S(2)}) async-start(f32[16,3,384]{2,1,0:T(4,128)} %gather_fusion.1), calls=%async_computation.2 | async-start | bytes 196608 | tf_op jit(solution)/shard_map/all_to_all | solution.py:117
  173.7 12.1 %all-to-all-done.2 = f32[16,3,384]{2,1,0:T(4,128)S(1)} async-done(((f32[16,3,384]{2,1,0:T(4,128)}), f32[16,3,384]{2,1,0:T(4,128)S(1)}, u32[]{:S(2)}, u32[]{:S(2)}) %all-to-all-start.2) | async-done | bytes 73760 | tf_op jit(solution)/shard_map/all_to_all | solution.py:117
  (146 shorter events, 50.8 us)
Async XLA Ops:
  10.0 17.6 %all-to-all-start.1 = ((bf16[32,48,128]{2,1,0:T(8,128)(2,1)}), bf16[32,48,128]{2,1,0:T(8,128)(2,1)S(1)}, u32[]{:S(2)}, u32[]{:S(2)}) async-start(bf16[32,48,128]{2,1,0:T(8,128)(2,1)} %reshape.360), calls=%async_computation.1 | async-start | bytes 786432 | tf_op jit(solution)/shard_map/all_to_all | solution.py:45
  27.6 22.3 %all-to-all-start = ((bf16[32,48,128]{2,1,0:T(8,128)(2,1)}), bf16[32,48,128]{2,1,0:T(8,128)(2,1)S(1)}, u32[]{:S(2)}, u32[]{:S(2)}) async-start(bf16[32,48,128]{2,1,0:T(8,128)(2,1)} %reshape.358), calls=%async_computation | async-start | bytes 786432 | tf_op jit(solution)/shard_map/all_to_all | solution.py:45
  40.4 21.8 %collective-permute-start.1 = (bf16[192,1024]{0,1:T(8,128)(2,1)S(1)}, bf16[192,1024]{0,1:T(8,128)(2,1)S(1)}, u32[]{:S(2)}, u32[]{:S(2)}) collective-permute-start(bf16[192,1024]{0,1:T(8,128)(2,1)S(1)} %copy.78), channel_id=1, source_target_pairs={{0,15},{1,0},{2,1},{3,2},{4,3},{5,4},{6,5},{7,6},{8,7},{9,8},{10,9... | collective-permute-start | bytes 1179656 | tf_op jit(solution)/shard_map/ppermute | solution.py:55
  50.3 23.1 %collective-permute-start = (bf16[192,1024]{0,1:T(8,128)(2,1)S(1)}, bf16[192,1024]{0,1:T(8,128)(2,1)S(1)}, u32[]{:S(2)}, u32[]{:S(2)}) collective-permute-start(bf16[192,1024]{0,1:T(8,128)(2,1)S(1)} %copy.77), channel_id=1, source_target_pairs={{0,15},{1,0},{2,1},{3,2},{4,3},{5,4},{6,5},{7,6},{8,7},{9,8},{10,9... | collective-permute-start | bytes 1179656 | tf_op jit(solution)/shard_map/ppermute | solution.py:55
  53.3 25.7 %collective-permute-start.8 = (bf16[192,1024]{0,1:T(8,128)(2,1)S(1)}, bf16[192,1024]{0,1:T(8,128)(2,1)}, u32[]{:S(2)}, u32[]{:S(2)}) collective-permute-start(bf16[192,1024]{0,1:T(8,128)(2,1)S(1)} %copy.78), channel_id=1, source_target_pairs={{0,1},{1,2},{2,3},{3,4},{4,5},{5,6},{6,7},{7,8},{8,9},{9,10},{10,1... | collective-permute-start | bytes 1179656 | tf_op jit(solution)/shard_map/ppermute | solution.py:55
  56.2 24.9 %collective-permute-start.6 = (bf16[192,1024]{0,1:T(8,128)(2,1)S(1)}, bf16[192,1024]{0,1:T(8,128)(2,1)}, u32[]{:S(2)}, u32[]{:S(2)}) collective-permute-start(bf16[192,1024]{0,1:T(8,128)(2,1)S(1)} %copy.77), channel_id=1, source_target_pairs={{0,1},{1,2},{2,3},{3,4},{4,5},{5,6},{6,7},{7,8},{8,9},{9,10},{10,1... | collective-permute-start | bytes 1179656 | tf_op jit(solution)/shard_map/ppermute | solution.py:55
  62.2 22.5 %collective-permute-start.3 = (bf16[192,1024]{0,1:T(8,128)(2,1)S(1)}, bf16[192,1024]{0,1:T(8,128)(2,1)}, u32[]{:S(2)}, u32[]{:S(2)}) collective-permute-start(bf16[192,1024]{0,1:T(8,128)(2,1)S(1)} %collective-permute-done.1), channel_id=1, source_target_pairs={{0,15},{1,0},{2,1},{3,2},{4,3},{5,4},{6,5},{7,6},{8,7},{9,8},{10,9... | collective-permute-start | bytes 1179656 | tf_op jit(solution)/shard_map/ppermute | solution.py:55
  73.4 22.5 %collective-permute-start.2 = (bf16[192,1024]{0,1:T(8,128)(2,1)S(1)}, bf16[192,1024]{0,1:T(8,128)(2,1)}, u32[]{:S(2)}, u32[]{:S(2)}) collective-permute-start(bf16[192,1024]{0,1:T(8,128)(2,1)S(1)} %collective-permute-done), channel_id=1, source_target_pairs={{0,15},{1,0},{2,1},{3,2},{4,3},{5,4},{6,5},{7,6},{8,7},{9,8},{10,9... | collective-permute-start | bytes 1179656 | tf_op jit(solution)/shard_map/ppermute | solution.py:55
  79.0 22.6 %collective-permute-start.9 = (bf16[192,1024]{0,1:T(8,128)(2,1)}, bf16[192,1024]{0,1:T(8,128)(2,1)S(1)}, u32[]{:S(2)}, u32[]{:S(2)}) collective-permute-start(bf16[192,1024]{0,1:T(8,128)(2,1)} %collective-permute-done.8), channel_id=1, source_target_pairs={{0,1},{1,2},{2,3},{3,4},{4,5},{5,6},{6,7},{7,8},{8,9},{9,10},{10,1... | collective-permute-start | bytes 1179656 | tf_op jit(solution)/shard_map/ppermute | solution.py:55
  81.1 24.5 %collective-permute-start.7 = (bf16[192,1024]{0,1:T(8,128)(2,1)}, bf16[192,1024]{0,1:T(8,128)(2,1)S(1)}, u32[]{:S(2)}, u32[]{:S(2)}) collective-permute-start(bf16[192,1024]{0,1:T(8,128)(2,1)} %collective-permute-done.6), channel_id=1, source_target_pairs={{0,1},{1,2},{2,3},{3,4},{4,5},{5,6},{6,7},{7,8},{8,9},{9,10},{10,1... | collective-permute-start | bytes 1179656 | tf_op jit(solution)/shard_map/ppermute | solution.py:55
  84.7 51.0 %collective-permute-start.5 = (bf16[192,1024]{0,1:T(8,128)(2,1)}, bf16[192,1024]{0,1:T(8,128)(2,1)S(1)}, u32[]{:S(2)}, u32[]{:S(2)}) collective-permute-start(bf16[192,1024]{0,1:T(8,128)(2,1)} %collective-permute-done.3), channel_id=1, source_target_pairs={{0,15},{1,0},{2,1},{3,2},{4,3},{5,4},{6,5},{7,6},{8,7},{9,8},{10,9... | collective-permute-start | bytes 1179656 | tf_op jit(solution)/shard_map/ppermute | solution.py:55
  95.9 44.9 %collective-permute-start.4 = (bf16[192,1024]{0,1:T(8,128)(2,1)}, bf16[192,1024]{0,1:T(8,128)(2,1)S(1)}, u32[]{:S(2)}, u32[]{:S(2)}) collective-permute-start(bf16[192,1024]{0,1:T(8,128)(2,1)} %collective-permute-done.2), channel_id=1, source_target_pairs={{0,15},{1,0},{2,1},{3,2},{4,3},{5,4},{6,5},{7,6},{8,7},{9,8},{10,9... | collective-permute-start | bytes 1179656 | tf_op jit(solution)/shard_map/ppermute | solution.py:55
  101.6 17.9 %collective-permute-start.11 = (bf16[192,1024]{0,1:T(8,128)(2,1)S(1)}, bf16[192,1024]{0,1:T(8,128)(2,1)S(1)}, u32[]{:S(2)}, u32[]{:S(2)}) collective-permute-start(bf16[192,1024]{0,1:T(8,128)(2,1)S(1)} %collective-permute-done.9), channel_id=1, source_target_pairs={{0,1},{1,2},{2,3},{3,4},{4,5},{5,6},{6,7},{7,8},{8,9},{9,10},{10,1... | collective-permute-start | bytes 1179656 | tf_op jit(solution)/shard_map/ppermute | solution.py:55
  105.7 25.1 %collective-permute-start.10 = (bf16[192,1024]{0,1:T(8,128)(2,1)S(1)}, bf16[192,1024]{0,1:T(8,128)(2,1)S(1)}, u32[]{:S(2)}, u32[]{:S(2)}) collective-permute-start(bf16[192,1024]{0,1:T(8,128)(2,1)S(1)} %collective-permute-done.7), channel_id=1, source_target_pairs={{0,1},{1,2},{2,3},{3,4},{4,5},{5,6},{6,7},{7,8},{8,9},{9,10},{10,1... | collective-permute-start | bytes 1179656 | tf_op jit(solution)/shard_map/ppermute | solution.py:55
  119.5 26.5 %collective-permute-start.13 = (bf16[192,1024]{0,1:T(8,128)(2,1)S(1)}, bf16[192,1024]{0,1:T(8,128)(2,1)S(1)}, u32[]{:S(2)}, u32[]{:S(2)}) collective-permute-start(bf16[192,1024]{0,1:T(8,128)(2,1)S(1)} %collective-permute-done.11), channel_id=1, source_target_pairs={{0,1},{1,2},{2,3},{3,4},{4,5},{5,6},{6,7},{7,8},{8,9},{9,10},{10,1... | collective-permute-start | bytes 1179656 | tf_op jit(solution)/shard_map/ppermute | solution.py:55
  130.8 19.7 %collective-permute-start.12 = (bf16[192,1024]{0,1:T(8,128)(2,1)S(1)}, bf16[192,1024]{0,1:T(8,128)(2,1)S(1)}, u32[]{:S(2)}, u32[]{:S(2)}) collective-permute-start(bf16[192,1024]{0,1:T(8,128)(2,1)S(1)} %collective-permute-done.10), channel_id=1, source_target_pairs={{0,1},{1,2},{2,3},{3,4},{4,5},{5,6},{6,7},{7,8},{8,9},{9,10},{10,1... | collective-permute-start | bytes 1179656 | tf_op jit(solution)/shard_map/ppermute | solution.py:55
  135.7 18.5 %collective-permute-start.15 = (bf16[192,1024]{0,1:T(8,128)(2,1)S(1)}, bf16[192,1024]{0,1:T(8,128)(2,1)S(1)}, u32[]{:S(2)}, u32[]{:S(2)}) collective-permute-start(bf16[192,1024]{0,1:T(8,128)(2,1)S(1)} %collective-permute-done.5), channel_id=1, source_target_pairs={{0,15},{1,0},{2,1},{3,2},{4,3},{5,4},{6,5},{7,6},{8,7},{9,8},{10,9... | collective-permute-start | bytes 1179656 | tf_op jit(solution)/shard_map/ppermute | solution.py:55
  140.8 16.9 %collective-permute-start.14 = (bf16[192,1024]{0,1:T(8,128)(2,1)S(1)}, bf16[192,1024]{0,1:T(8,128)(2,1)S(1)}, u32[]{:S(2)}, u32[]{:S(2)}) collective-permute-start(bf16[192,1024]{0,1:T(8,128)(2,1)S(1)} %collective-permute-done.4), channel_id=1, source_target_pairs={{0,15},{1,0},{2,1},{3,2},{4,3},{5,4},{6,5},{7,6},{8,7},{9,8},{10,9... | collective-permute-start | bytes 1179656 | tf_op jit(solution)/shard_map/ppermute | solution.py:55
  152.3 20.6 %collective-permute-start.17 = (f32[1,384]{1,0:T(1,128)S(1)}, f32[1,384]{1,0:T(1,128)S(1)}, u32[]{:S(2)}, u32[]{:S(2)}) collective-permute-start(f32[1,384]{1,0:T(1,128)S(1)} %stack.119), channel_id=1, source_target_pairs={{0,3},{1,4},{2,5},{3,6},{4,7},{5,8},{6,9},{7,10},{8,11},{9,12},{10... | collective-permute-start | bytes 4616 | tf_op jit(solution)/shard_map/ppermute | solution.py:55
  157.9 14.9 %copy-start.4 = (f32[1,384]{1,0:T(1,128)S(1)}, f32[1,384]{1,0:T(1,128)}, u32[]{:S(2)}) copy-start(f32[1,384]{1,0:T(1,128)} %stack.90) | copy-start | bytes 4612
  157.9 14.9 %copy-start.6 = (f32[4]{0:T(128)S(1)}, f32[4]{0:T(128)}, u32[]{:S(2)}) copy-start(f32[4]{0:T(128)} %gather_fusion) | copy-start | bytes 52
  157.9 15.7 %copy-start.7 = (f32[2]{0:T(128)S(1)}, f32[2]{0:T(128)}, u32[]{:S(2)}) copy-start(f32[2]{0:T(128)} %gather_fusion.5) | copy-start | bytes 28
  158.9 14.7 %collective-permute-start.16 = (f32[2,384]{1,0:T(2,128)S(1)}, f32[2,384]{1,0:T(2,128)S(1)}, u32[]{:S(2)}, u32[]{:S(2)}) collective-permute-start(f32[2,384]{1,0:T(2,128)S(1)} %pad_maximum_fusion.11), channel_id=1, source_target_pairs={{0,12},{1,13},{2,14},{3,15},{4,0},{5,1},{6,2},{7,3},{8,4},{9,5},{1... | collective-permute-start | bytes 9224 | tf_op jit(solution)/shard_map/ppermute | solution.py:55
  166.1 19.7 %all-to-all-start.2 = ((f32[16,3,384]{2,1,0:T(4,128)}), f32[16,3,384]{2,1,0:T(4,128)S(1)}, u32[]{:S(2)}, u32[]{:S(2)}) async-start(f32[16,3,384]{2,1,0:T(4,128)} %gather_fusion.1), calls=%async_computation.2 | async-start | bytes 196608 | tf_op jit(solution)/shard_map/all_to_all | solution.py:117
  (7 other events, 53.4 us)

commit v8 on v6

--- a/solution.py
+++ b/solution.py
@@ -38,8 +38,9 @@
     send_slots = bucket * capacity + row_ranks
     empty = jnp.zeros((wide_count * capacity, feature_width), jnp.bfloat16).at[:, 0].set(SENTINEL)
     outgoing = empty.at[send_slots].set(unit_rows).reshape(wide_count, capacity, feature_width)
-    split = capacity // 2
-    halves = [outgoing[:, :split], outgoing[:, split:]]
+    parts = 1
+    split = capacity // parts
+    halves = [outgoing[:, k * split:(k + 1) * split] for k in range(parts)]
     own_halves = [
         lax.all_to_all(h, "wide", split_axis=0, concat_axis=0, tiled=True).reshape(-1, feature_width)
         for h in halves
@@ -121,12 +122,12 @@
         stacked = shift(jnp.stack([s for _, s in items]), target)
         slot_sums = slot_sums + weighted(stacked, items, target)
 
-    own_valid = valid_at[0].reshape(2, wide_count, split).transpose(1, 0, 2).reshape(wide_count, capacity)
+    own_valid = valid_at[0].reshape(parts, wide_count, split).transpose(1, 0, 2).reshape(wide_count, capacity)
     arrived = jnp.sum(own_valid, axis=1).astype(jnp.int32)
     offsets = jnp.cumsum(arrived) - arrived
     within = jnp.arange(capacity, dtype=jnp.int32)
     places = jnp.where(own_valid > 0, offsets[:, None] + within[None, :], BLK)
-    places = places.reshape(wide_count, 2, split).transpose(1, 0, 2).reshape(-1)
+    places = places.reshape(wide_count, parts, split).transpose(1, 0, 2).reshape(-1)
     rows_iota = jnp.arange(BLK, dtype=jnp.int32)
     density = jnp.sum(jnp.where(places[:, None] == rows_iota[None, :], slot_sums[:, None], 0.0), axis=0)
     return density.reshape(1, BLK)

time: 166 us -> 160 us (0.964)
  starting transfers between devices: 96.4 us -> 60.9 us
  waiting for transfers between devices: 41.2 us -> 66.3 us
  matrix products: 6.03 us -> 9.44 us
  other arithmetic: 10.1 us -> 12 us
    ppermute x18 -> x10, starting transfers between devices: 70.9 us -> 43 us  [shift(): lax.ppermute(value, 'grp', [(i, (i + offset) % grp_count) for i in range(...]
    ppermute x18 -> x10, waiting for transfers between devices: 32.8 us -> 56.2 us  [shift(): lax.ppermute(value, 'grp', [(i, (i + offset) % grp_count) for i in range(...]
    all_to_all x2 -> x1, starting transfers between devices: 15.7 us -> 9.57 us  [per_device(): lax.all_to_all(h, 'wide', split_axis=0, concat_axis=0, tiled=True)]
    dot_general x9, matrix products: 6.03 us -> 9.44 us  [pair_products(): lax.dot_general(left_rows, right_rows, (((1,), (1,)), ((), ())), preferre...]
    convert_element_type x5, other arithmetic: 0.56 us -> 2.35 us  [valid_of(): return (rows[:, 0].astype(jnp.float32) < 1.5).astype(jnp.float32)]
    all_to_all x2 -> x1, waiting for transfers between devices: 8.36 us -> 10.2 us  [per_device(): lax.all_to_all(h, 'wide', split_axis=0, concat_axis=0, tiled=True)]
  transfers between devices with their start and end apart: 21 -> 12, of which waited for: 10 -> 6; matrix products, arithmetic and copies ran while one was open for 7% -> 12% of each run, Pallas kernels for 0% -> 0%
where the time goes in v8:
time: 160 us; the launch traced here: 158 us
  waiting for transfers between devices  66.3 us (41%)
  starting transfers between devices  60.9 us (38%)
  other arithmetic  12 us (8%)
  matrix products  9.44 us (6%)
  local copies, waits for them, and re-layouts  8.11 us (5%)
    ppermute x10, waiting for transfers between devices, shift(): lax.ppermute(value, 'grp', [(i, (i + offset) % grp_count) for i in range(...  56.2 us
    ppermute x10, starting transfers between devices, shift(): lax.ppermute(value, 'grp', [(i, (i + offset) % grp_count) for i in range(...  43 us
    all_to_all x1, waiting for transfers between devices, per_device(): lax.all_to_all(h, 'wide', split_axis=0, concat_axis=0, tiled=True)  10.2 us
    all_to_all x1, starting transfers between devices, per_device(): lax.all_to_all(h, 'wide', split_axis=0, concat_axis=0, tiled=True)  9.57 us
    dot_general x9, matrix products, pair_products(): lax.dot_general(left_rows, right_rows, (((1,), (1,)), ((), ())), preferre...  9.44 us
    all_to_all x1, starting transfers between devices, per_device(): lax.all_to_all(by_device, 'grp', split_axis=0, concat_axis=0, tiled=True)  8.37 us
  transfers between devices with their start and end apart: 12, of which 6 were waited for; matrix products, arithmetic and copies ran while one was open for 12% of the time, Pallas kernels for 0%

profile of v8, /device:TPU:6, one launch (start us, length us, event | category | flops | bytes accessed | tf_op | source)
XLA Modules:
  0.0 158.0 jit_solution(7966136946672824525)
XLA Ops:
  1.3 1.3 fusion.22
  6.0 2.3 %scatter_custom_fusion = bf16[384,1024]{1,0:T(8,128)(2,1)S(1)} fusion(bf16[384,1024]{1,0:T(8,128)(2,1)S(1)} %scatter.15, s32[288]{0:T(512)S(1)} %compare_select_fusion.1, bf16[288,1024]{1,0:T(8,128)(2,1)S(1)} %copy-done, f32[288]{0:T(512)S(1)} %add_rsqrt_fusion), kind=kCustom, calls=%fused_computation.42 | custom fusion | flops 884736 | bytes 1378304 | tf_op jit(solution)/shard_map/scatter | solution.py:40
  9.5 9.6 %all-to-all-start = ((bf16[32,12,1024]{2,1,0:T(8,128)(2,1)}), bf16[32,12,1024]{2,1,0:T(8,128)(2,1)S(1)}, u32[]{:S(2)}, u32[]{:S(2)}) async-start(bf16[32,12,1024]{2,1,0:T(8,128)(2,1)} %reshape.348), calls=%async_computation | async-start | bytes 2097152 | tf_op jit(solution)/shard_map/all_to_all | solution.py:45
  23.6 10.2 %all-to-all-done = bf16[32,12,1024]{2,1,0:T(8,128)(2,1)S(1)} async-done(((bf16[32,12,1024]{2,1,0:T(8,128)(2,1)}), bf16[32,12,1024]{2,1,0:T(8,128)(2,1)S(1)}, u32[]{:S(2)}, u32[]{:S(2)}) %all-to-all-start) | async-done | bytes 786464 | tf_op jit(solution)/shard_map/all_to_all | solution.py:45
  33.9 1.9 %collective-permute-start.3 = (bf16[384,1024]{1,0:T(8,128)(2,1)S(1)}, bf16[384,1024]{1,0:T(8,128)(2,1)}, u32[]{:S(2)}, u32[]{:S(2)}) collective-permute-start(bf16[384,1024]{1,0:T(8,128)(2,1)S(1)} %reshape.349), channel_id=1, source_target_pairs={{0,1},{1,2},{2,3},{3,4},{4,5},{5,6},{6,7},{7,8},{8,9},{9,10},{10,1... | collective-permute-start | bytes 2359304 | tf_op jit(solution)/shard_map/ppermute | solution.py:53
  35.9 9.4 %collective-permute-start = (bf16[384,1024]{1,0:T(8,128)(2,1)S(1)}, bf16[384,1024]{1,0:T(8,128)(2,1)S(1)}, u32[]{:S(2)}, u32[]{:S(2)}) collective-permute-start(bf16[384,1024]{1,0:T(8,128)(2,1)S(1)} %reshape.349), channel_id=1, source_target_pairs={{0,15},{1,0},{2,1},{3,2},{4,3},{5,4},{6,5},{7,6},{8,7},{9,8},{10,9... | collective-permute-start | bytes 2359304 | tf_op jit(solution)/shard_map/ppermute | solution.py:53
  46.0 15.2 %collective-permute-done.3 = bf16[384,1024]{1,0:T(8,128)(2,1)} collective-permute-done((bf16[384,1024]{1,0:T(8,128)(2,1)S(1)}, bf16[384,1024]{1,0:T(8,128)(2,1)}, u32[]{:S(2)}, u32[]{:S(2)}) %collective-permute-start.3) | collective-permute-done | bytes 786464 | tf_op jit(solution)/shard_map/ppermute | solution.py:53
  61.2 1.9 %collective-permute-start.4 = (bf16[384,1024]{1,0:T(8,128)(2,1)}, bf16[384,1024]{1,0:T(8,128)(2,1)S(1)}, u32[]{:S(2)}, u32[]{:S(2)}) collective-permute-start(bf16[384,1024]{1,0:T(8,128)(2,1)} %collective-permute-done.3), channel_id=1, source_target_pairs={{0,1},{1,2},{2,3},{3,4},{4,5},{5,6},{6,7},{7,8},{8,9},{9,10},{10,1... | collective-permute-start | bytes 2359304 | tf_op jit(solution)/shard_map/ppermute | solution.py:53
  63.1 5.3 %collective-permute-start.1 = (bf16[384,1024]{1,0:T(8,128)(2,1)S(1)}, bf16[384,1024]{1,0:T(8,128)(2,1)}, u32[]{:S(2)}, u32[]{:S(2)}) collective-permute-start(bf16[384,1024]{1,0:T(8,128)(2,1)S(1)} %collective-permute-done), channel_id=1, source_target_pairs={{0,15},{1,0},{2,1},{3,2},{4,3},{5,4},{6,5},{7,6},{8,7},{9,8},{10,9... | collective-permute-start | bytes 2359304 | tf_op jit(solution)/shard_map/ppermute | solution.py:53
  70.1 14.3 %collective-permute-done.4 = bf16[384,1024]{1,0:T(8,128)(2,1)S(1)} collective-permute-done((bf16[384,1024]{1,0:T(8,128)(2,1)}, bf16[384,1024]{1,0:T(8,128)(2,1)S(1)}, u32[]{:S(2)}, u32[]{:S(2)}) %collective-permute-start.4) | collective-permute-done | bytes 786464 | tf_op jit(solution)/shard_map/ppermute | solution.py:53
  84.4 1.9 %collective-permute-start.5 = (bf16[384,1024]{1,0:T(8,128)(2,1)S(1)}, bf16[384,1024]{1,0:T(8,128)(2,1)S(1)}, u32[]{:S(2)}, u32[]{:S(2)}) collective-permute-start(bf16[384,1024]{1,0:T(8,128)(2,1)S(1)} %collective-permute-done.4), channel_id=1, source_target_pairs={{0,1},{1,2},{2,3},{3,4},{4,5},{5,6},{6,7},{7,8},{8,9},{9,10},{10,1... | collective-permute-start | bytes 2359304 | tf_op jit(solution)/shard_map/ppermute | solution.py:53
  86.4 5.1 %collective-permute-start.2 = (bf16[384,1024]{1,0:T(8,128)(2,1)}, bf16[384,1024]{1,0:T(8,128)(2,1)S(1)}, u32[]{:S(2)}, u32[]{:S(2)}) collective-permute-start(bf16[384,1024]{1,0:T(8,128)(2,1)} %collective-permute-done.1), channel_id=1, source_target_pairs={{0,15},{1,0},{2,1},{3,2},{4,3},{5,4},{6,5},{7,6},{8,7},{9,8},{10,9... | collective-permute-start | bytes 2359304 | tf_op jit(solution)/shard_map/ppermute | solution.py:53
  92.6 1.8 %fusion.10 = f32[384,384]{0,1:T(8,128)S(1)} fusion(bf16[384,1024]{1,0:T(8,128)(2,1)S(1)} %collective-permute-done.4, bf16[384,1024]{1,0:T(8,128)(2,1)} %collective-permute-done.1), kind=kOutput, calls=%fused_computation.28 | convolution fusion | flops 302284800 | bytes 2162688 | tf_op jit(solution)/shard_map/dot_general | solution.py:16
  94.4 1.7 %fusion.6 = f32[384,384]{0,1:T(8,128)S(1)} fusion(bf16[384,1024]{1,0:T(8,128)(2,1)S(1)} %reshape.349, bf16[384,1024]{1,0:T(8,128)(2,1)} %collective-permute-done.1), kind=kOutput, calls=%fused_computation.24 | convolution fusion | flops 302284800 | bytes 2162688 | tf_op jit(solution)/shard_map/dot_general | solution.py:16
  96.2 10.5 %collective-permute-done.5 = bf16[384,1024]{1,0:T(8,128)(2,1)S(1)} collective-permute-done((bf16[384,1024]{1,0:T(8,128)(2,1)S(1)}, bf16[384,1024]{1,0:T(8,128)(2,1)S(1)}, u32[]{:S(2)}, u32[]{:S(2)}) %collective-permute-start.5) | collective-permute-done | bytes 786464 | tf_op jit(solution)/shard_map/ppermute | solution.py:53
  106.6 1.9 %collective-permute-start.6 = (bf16[384,1024]{1,0:T(8,128)(2,1)S(1)}, bf16[384,1024]{1,0:T(8,128)(2,1)S(1)}, u32[]{:S(2)}, u32[]{:S(2)}) collective-permute-start(bf16[384,1024]{1,0:T(8,128)(2,1)S(1)} %collective-permute-done.5), channel_id=1, source_target_pairs={{0,1},{1,2},{2,3},{3,4},{4,5},{5,6},{6,7},{7,8},{8,9},{9,10},{10,1... | collective-permute-start | bytes 2359304 | tf_op jit(solution)/shard_map/ppermute | solution.py:53
  108.8 5.3 %collective-permute-start.7 = (bf16[384,1024]{1,0:T(8,128)(2,1)S(1)}, bf16[384,1024]{1,0:T(8,128)(2,1)}, u32[]{:S(2)}, u32[]{:S(2)}) collective-permute-start(bf16[384,1024]{1,0:T(8,128)(2,1)S(1)} %collective-permute-done.2), channel_id=1, source_target_pairs={{0,15},{1,0},{2,1},{3,2},{4,3},{5,4},{6,5},{7,6},{8,7},{9,8},{10,9... | collective-permute-start | bytes 2359304 | tf_op jit(solution)/shard_map/ppermute | solution.py:53
  115.9 12.1 %collective-permute-done.6 = bf16[384,1024]{1,0:T(8,128)(2,1)S(1)} collective-permute-done((bf16[384,1024]{1,0:T(8,128)(2,1)S(1)}, bf16[384,1024]{1,0:T(8,128)(2,1)S(1)}, u32[]{:S(2)}, u32[]{:S(2)}) %collective-permute-start.6) | collective-permute-done | bytes 786464 | tf_op jit(solution)/shard_map/ppermute | solution.py:53
  129.6 1.2 gather_fusion.1
  130.9 8.4 %all-to-all-start.1 = ((f32[16,3,384]{2,1,0:T(4,128)}), f32[16,3,384]{2,1,0:T(4,128)S(1)}, u32[]{:S(2)}, u32[]{:S(2)}) async-start(f32[16,3,384]{2,1,0:T(4,128)} %gather_fusion.1), calls=%async_computation.1 | async-start | bytes 196608 | tf_op jit(solution)/shard_map/all_to_all | solution.py:115
  139.2 5.6 %collective-permute-start.9 = (f32[1,384]{1,0:T(1,128)S(1)}, f32[1,384]{1,0:T(1,128)S(1)}, u32[]{:S(2)}, u32[]{:S(2)}) collective-permute-start(f32[1,384]{1,0:T(1,128)S(1)} %stack.119), channel_id=1, source_target_pairs={{0,3},{1,4},{2,5},{3,6},{4,7},{5,8},{6,9},{7,10},{8,11},{9,12},{10... | collective-permute-start | bytes 4616 | tf_op jit(solution)/shard_map/ppermute | solution.py:53
  145.9 1.8 %fusion.20 = f32[384]{0:T(512)S(1)} fusion(bf16[384,1024]{1,0:T(8,128)(2,1)S(1)} %collective-permute-done.6, bf16[384,1024]{1,0:T(8,128)(2,1)} %collective-permute-done.7, f32[384]{0:T(512)S(1)} %convert_reduce_fusion.2), kind=kOutput, calls=%fused_computation.38 | convolution fusion | flops 302579328 | bytes 1575936 | tf_op jit(solution)/shard_map/dot_general | solution.py:16
  147.7 4.6 %collective-permute-start.8 = (f32[2,384]{1,0:T(2,128)S(1)}, f32[2,384]{1,0:T(2,128)S(1)}, u32[]{:S(2)}, u32[]{:S(2)}) collective-permute-start(f32[2,384]{1,0:T(2,128)S(1)} %pad_maximum_fusion), channel_id=1, source_target_pairs={{0,12},{1,13},{2,14},{3,15},{4,0},{5,1},{6,2},{7,3},{8,4},{9,5},{1... | collective-permute-start | bytes 9224 | tf_op jit(solution)/shard_map/ppermute | solution.py:53
  153.0 4.1 %collective-permute-done.8 = f32[2,384]{1,0:T(2,128)S(1)} collective-permute-done((f32[2,384]{1,0:T(2,128)S(1)}, f32[2,384]{1,0:T(2,128)S(1)}, u32[]{:S(2)}, u32[]{:S(2)}) %collective-permute-start.8) | collective-permute-done | bytes 3104 | tf_op jit(solution)/shard_map/ppermute | solution.py:53
  (115 shorter events, 19.5 us)
Async XLA Ops:
  0.0 6.0 %copy-start = (bf16[288,1024]{1,0:T(8,128)(2,1)S(1)}, bf16[288,1024]{1,0:T(8,128)(2,1)}, u32[]{:S(2)}) copy-start(bf16[288,1024]{1,0:T(8,128)(2,1)} %param.10) | copy-start | bytes 1769476
  9.5 9.6 %copy-start.6 = (s32[2]{0:T(128)S(1)}, s32[2]{0:T(128)}, u32[]{:S(2)}) copy-start(s32[2]{0:T(128)} %constant.160.clone) | copy-start | bytes 28
  9.5 9.7 %copy-start.5 = (s32[16]{0:T(128)S(1)}, s32[16]{0:T(128)}, u32[]{:S(2)}) copy-start(s32[16]{0:T(128)} %param.12) | copy-start | bytes 196
  9.5 24.3 %all-to-all-start = ((bf16[32,12,1024]{2,1,0:T(8,128)(2,1)}), bf16[32,12,1024]{2,1,0:T(8,128)(2,1)S(1)}, u32[]{:S(2)}, u32[]{:S(2)}) async-start(bf16[32,12,1024]{2,1,0:T(8,128)(2,1)} %reshape.348), calls=%async_computation | async-start | bytes 2097152 | tf_op jit(solution)/shard_map/all_to_all | solution.py:45
  19.1 2.1 %copy-start.2 = (f32[16,3]{1,0:T(8,128)S(1)}, f32[16,3]{1,0:T(8,128)}, u32[]{:S(2)}) copy-start(f32[16,3]{1,0:T(8,128)} %constant.159.clone) | copy-start | bytes 580
  19.1 2.7 %copy-start.1 = (s32[16,3]{1,0:T(8,128)S(1)}, s32[16,3]{1,0:T(8,128)}, u32[]{:S(2)}) copy-start(s32[16,3]{1,0:T(8,128)} %constant.158.clone) | copy-start | bytes 580
  33.9 27.2 %collective-permute-start.3 = (bf16[384,1024]{1,0:T(8,128)(2,1)S(1)}, bf16[384,1024]{1,0:T(8,128)(2,1)}, u32[]{:S(2)}, u32[]{:S(2)}) collective-permute-start(bf16[384,1024]{1,0:T(8,128)(2,1)S(1)} %reshape.349), channel_id=1, source_target_pairs={{0,1},{1,2},{2,3},{3,4},{4,5},{5,6},{6,7},{7,8},{8,9},{9,10},{10,1... | collective-permute-start | bytes 2359304 | tf_op jit(solution)/shard_map/ppermute | solution.py:53
  35.9 27.2 %collective-permute-start = (bf16[384,1024]{1,0:T(8,128)(2,1)S(1)}, bf16[384,1024]{1,0:T(8,128)(2,1)S(1)}, u32[]{:S(2)}, u32[]{:S(2)}) collective-permute-start(bf16[384,1024]{1,0:T(8,128)(2,1)S(1)} %reshape.349), channel_id=1, source_target_pairs={{0,15},{1,0},{2,1},{3,2},{4,3},{5,4},{6,5},{7,6},{8,7},{9,8},{10,9... | collective-permute-start | bytes 2359304 | tf_op jit(solution)/shard_map/ppermute | solution.py:53
  61.2 23.3 %collective-permute-start.4 = (bf16[384,1024]{1,0:T(8,128)(2,1)}, bf16[384,1024]{1,0:T(8,128)(2,1)S(1)}, u32[]{:S(2)}, u32[]{:S(2)}) collective-permute-start(bf16[384,1024]{1,0:T(8,128)(2,1)} %collective-permute-done.3), channel_id=1, source_target_pairs={{0,1},{1,2},{2,3},{3,4},{4,5},{5,6},{6,7},{7,8},{8,9},{9,10},{10,1... | collective-permute-start | bytes 2359304 | tf_op jit(solution)/shard_map/ppermute | solution.py:53
  63.1 23.3 %collective-permute-start.1 = (bf16[384,1024]{1,0:T(8,128)(2,1)S(1)}, bf16[384,1024]{1,0:T(8,128)(2,1)}, u32[]{:S(2)}, u32[]{:S(2)}) collective-permute-start(bf16[384,1024]{1,0:T(8,128)(2,1)S(1)} %collective-permute-done), channel_id=1, source_target_pairs={{0,15},{1,0},{2,1},{3,2},{4,3},{5,4},{6,5},{7,6},{8,7},{9,8},{10,9... | collective-permute-start | bytes 2359304 | tf_op jit(solution)/shard_map/ppermute | solution.py:53
  84.4 10.0 %copy-start.3 = (bf16[384,1024]{1,0:T(8,128)(2,1)}, bf16[384,1024]{1,0:T(8,128)(2,1)S(1)}, u32[]{:S(2)}) copy-start(bf16[384,1024]{1,0:T(8,128)(2,1)S(1)} %collective-permute-done.4) | copy-start | bytes 2359300
  84.4 22.2 %collective-permute-start.5 = (bf16[384,1024]{1,0:T(8,128)(2,1)S(1)}, bf16[384,1024]{1,0:T(8,128)(2,1)S(1)}, u32[]{:S(2)}, u32[]{:S(2)}) collective-permute-start(bf16[384,1024]{1,0:T(8,128)(2,1)S(1)} %collective-permute-done.4), channel_id=1, source_target_pairs={{0,1},{1,2},{2,3},{3,4},{4,5},{5,6},{6,7},{7,8},{8,9},{9,10},{10,1... | collective-permute-start | bytes 2359304 | tf_op jit(solution)/shard_map/ppermute | solution.py:53
  86.4 22.3 %collective-permute-start.2 = (bf16[384,1024]{1,0:T(8,128)(2,1)}, bf16[384,1024]{1,0:T(8,128)(2,1)S(1)}, u32[]{:S(2)}, u32[]{:S(2)}) collective-permute-start(bf16[384,1024]{1,0:T(8,128)(2,1)} %collective-permute-done.1), channel_id=1, source_target_pairs={{0,15},{1,0},{2,1},{3,2},{4,3},{5,4},{6,5},{7,6},{8,7},{9,8},{10,9... | collective-permute-start | bytes 2359304 | tf_op jit(solution)/shard_map/ppermute | solution.py:53
  106.6 21.3 %collective-permute-start.6 = (bf16[384,1024]{1,0:T(8,128)(2,1)S(1)}, bf16[384,1024]{1,0:T(8,128)(2,1)S(1)}, u32[]{:S(2)}, u32[]{:S(2)}) collective-permute-start(bf16[384,1024]{1,0:T(8,128)(2,1)S(1)} %collective-permute-done.5), channel_id=1, source_target_pairs={{0,1},{1,2},{2,3},{3,4},{4,5},{5,6},{6,7},{7,8},{8,9},{9,10},{10,1... | collective-permute-start | bytes 2359304 | tf_op jit(solution)/shard_map/ppermute | solution.py:53
  108.8 5.9 %copy-start.4 = (bf16[384,1024]{1,0:T(8,128)(2,1)S(1)}, bf16[384,1024]{1,0:T(8,128)(2,1)}, u32[]{:S(2)}) copy-start(bf16[384,1024]{1,0:T(8,128)(2,1)} %copy-done.3) | copy-start | bytes 2359300
  108.8 36.1 %collective-permute-start.7 = (bf16[384,1024]{1,0:T(8,128)(2,1)S(1)}, bf16[384,1024]{1,0:T(8,128)(2,1)}, u32[]{:S(2)}, u32[]{:S(2)}) collective-permute-start(bf16[384,1024]{1,0:T(8,128)(2,1)S(1)} %collective-permute-done.2), channel_id=1, source_target_pairs={{0,15},{1,0},{2,1},{3,2},{4,3},{5,4},{6,5},{7,6},{8,7},{9,8},{10,9... | collective-permute-start | bytes 2359304 | tf_op jit(solution)/shard_map/ppermute | solution.py:53
  130.9 26.3 %all-to-all-start.1 = ((f32[16,3,384]{2,1,0:T(4,128)}), f32[16,3,384]{2,1,0:T(4,128)S(1)}, u32[]{:S(2)}, u32[]{:S(2)}) async-start(f32[16,3,384]{2,1,0:T(4,128)} %gather_fusion.1), calls=%async_computation.1 | async-start | bytes 196608 | tf_op jit(solution)/shard_map/all_to_all | solution.py:115
  139.2 13.1 %collective-permute-start.9 = (f32[1,384]{1,0:T(1,128)S(1)}, f32[1,384]{1,0:T(1,128)S(1)}, u32[]{:S(2)}, u32[]{:S(2)}) collective-permute-start(f32[1,384]{1,0:T(1,128)S(1)} %stack.119), channel_id=1, source_target_pairs={{0,3},{1,4},{2,5},{3,6},{4,7},{5,8},{6,9},{7,10},{8,11},{9,12},{10... | collective-permute-start | bytes 4616 | tf_op jit(solution)/shard_map/ppermute | solution.py:53
  147.7 9.4 %collective-permute-start.8 = (f32[2,384]{1,0:T(2,128)S(1)}, f32[2,384]{1,0:T(2,128)S(1)}, u32[]{:S(2)}, u32[]{:S(2)}) collective-permute-start(f32[2,384]{1,0:T(2,128)S(1)} %pad_maximum_fusion), channel_id=1, source_target_pairs={{0,12},{1,13},{2,14},{3,15},{4,0},{5,1},{6,2},{7,3},{8,4},{9,5},{1... | collective-permute-start | bytes 9224 | tf_op jit(solution)/shard_map/ppermute | solution.py:53
